TPU v7x, 32 devices: a whole 2x2x4 slice. The times are simulated.
32 devices in a mesh: groups: 2 (over y), leaf: 4 (over z), state: 2 (over x), sub: 2 (over core).
Axes of the slice: x: 2, y: 2, z: 4, core: 2. Of those that a mesh axis runs over, the one named last changes fastest.
Arguments:
- sphere_coef: bfloat16 [12, 25, 2, 2, 4, 2048], P(None, None, None, None, None, ('groups', 'leaf', 'state', 'sub')), parts along dimension 5, may hold values from -6 to 6
- live_blocks: int32 [32], P(('groups', 'leaf', 'state', 'sub')), parts along dimension 0, may hold values from 1 to 4, as said below
- cluster: int32 [2048], P(('groups', 'leaf', 'state', 'sub')), parts along dimension 0, may hold values from 0 to 15
- leaf_parent: int32 [512], P(('groups', 'leaf', 'state', 'sub')), parts along dimension 0, may hold values from 0 to 1
- leaf_octant: int32 [512], P(('groups', 'leaf', 'state', 'sub')), parts along dimension 0, may hold values from 0 to 7
- box_octant: int32 [64], P(('groups', 'leaf', 'state', 'sub')), parts along dimension 0, may hold values from 0 to 7
- rotation: float32 [8, 2, 12, 25, 25], replicated, may hold values from -0.875 to 0.875
- axial_one: float32 [2, 25, 2, 12, 2, 12], replicated, may hold values from -0.3125 to 0.3125
- axial_two: float32 [2, 25, 2, 12, 2, 12], replicated, may hold values from -0.3125 to 0.3125
- owner_rotation: float32 [8, 2, 12, 25, 25], P(('groups', 'leaf')), parts along dimension 0, may hold values from -0.875 to 0.875
- owner_axial: float32 [8, 2, 25, 2, 128, 2, 12], P(('groups', 'leaf'), None, None, None, ('state', 'sub')), parts along dimension 0, may hold values from -0.875 to 0.875
- owner_angle: float32 [8], P('groups'), parts along dimension 0, may hold values from -3.140625 to 3.140625
- turn_table: bfloat16 [8, 128, 25, 256], P(('groups', 'leaf'), ('state', 'sub')), parts along dimension 0, may hold values from -0.625 to 0.625
- angular_table: bfloat16 [256, 128, 32], P('leaf', ('state', 'sub')), may hold values from -0.375 to 0.375
Outputs:
- far_field: float32 [32, 4, 2, 2, 2048], P(('groups', 'leaf', 'state', 'sub')), parts along dimension 0
There are 2 independent parts, one for each index of `groups`. A program takes and returns all parts, laid end to end along the dimension named above; an argument that names none is the same for every part. Nothing has to cross between parts.
Inputs may be any that keep to these rules, and one draw needn't show every extreme that they name: `live_blocks`: live blocks of 16 sphere slots on each device; some device has all 4 live in every draw.
All inputs are finite; a program needn't handle non-finite values.
Results may differ from a plain program's by a relative error of at most 0.018.
Values may be sent and summed in bfloat16 or wider, within the bound.
No kernel may reach another device: no remote copies, remote signals or barrier semaphores. Data moves between devices by JAX's collectives and lax.ppermute only.
A program may use at most 64 MiB of HBM per device.

v0:
```python
import math

import jax
import jax.numpy as jnp
from jax import lax
from jax.sharding import PartitionSpec as P

STATES = 4
SBLK = 4
PHI = 2048
HI = lax.Precision.HIGH
LEAF_PREC = lax.Precision.DEFAULT


def complex_join(first, second, half):
    real = first[..., :half] - second[..., half:]
    imag = first[..., half:] + second[..., :half]
    return jnp.concatenate([real, imag], axis=-1)


def turn_select(vectors, rotation, octants, backward, prec):
    degrees, orders, width = vectors.shape
    if backward:
        mats = jnp.transpose(rotation, (1, 2, 0, 4, 3))
        sign = -1.0
    else:
        mats = jnp.transpose(rotation, (1, 2, 0, 3, 4))
        sign = 1.0
    mats = mats.reshape(2, degrees, 8 * orders, orders)
    first = jnp.einsum("lQp,lpC->lQC", mats[0], vectors, precision=prec)
    second = sign * jnp.einsum("lQp,lpC->lQC", mats[1], vectors, precision=prec)
    joined = complex_join(first, second, width // 2).reshape(degrees, 8, orders, width)
    count = octants.shape[0]
    chosen = (octants[None, :] == jnp.arange(8, dtype=jnp.int32)[:, None]).astype(jnp.float32)
    column_mask = jnp.tile(chosen, (1, width // count))
    return jnp.sum(joined * column_mask[None, :, None, :], axis=1)


def axial_apply(vectors, axial, prec):
    degrees, orders, width = vectors.shape
    rest = width // 4
    moved = vectors.reshape(degrees, orders, 2, 2, rest)
    moved = jnp.transpose(moved, (1, 3, 0, 2, 4)).reshape(orders, 2 * degrees, 2 * rest)
    mats = axial.reshape(2, orders, 2 * degrees, 2 * degrees)
    first = jnp.einsum("qab,qbC->qaC", mats[0], moved, precision=prec)
    second = jnp.einsum("qab,qbC->qaC", mats[1], moved, precision=prec)
    joined = complex_join(first, second, rest).reshape(orders, 2, degrees, 2, rest)
    return jnp.transpose(joined, (2, 0, 3, 1, 4)).reshape(degrees, orders, width)


def move_expansion(vectors, octants, rotation, axial, prec):
    turned = turn_select(vectors, rotation, octants, False, prec)
    return turn_select(axial_apply(turned, axial, prec), rotation, octants, True, prec)


def local_boxes(
    sphere_block,
    live_count,
    cluster,
    leaf_parent,
    leaf_octant,
    box_octant,
    rotation,
    axial_one,
    axial_two,
):
    degrees, orders = (sphere_block.shape[0], sphere_block.shape[1])
    channel = sphere_block.shape[2] * sphere_block.shape[3] * sphere_block.shape[4]
    slots = sphere_block.shape[-1]
    per_block = slots // SBLK
    alive = jnp.arange(slots, dtype=jnp.int32) // per_block < live_count
    leaf_total = leaf_parent.shape[0]
    member = (
        (cluster[:, None] == jnp.arange(leaf_total, dtype=jnp.int32)[None, :]) & alive[:, None]
    ).astype(jnp.bfloat16)
    ident = jnp.eye(channel, dtype=jnp.bfloat16)
    spread = (ident[:, None, :, None] * member[None, :, None, :]).reshape(
        channel * slots, channel * leaf_total
    )
    leaves = jnp.dot(
        sphere_block.reshape(degrees * orders, channel * slots),
        spread,
        preferred_element_type=jnp.float32,
    ).reshape(degrees, orders, channel * leaf_total)
    moved = move_expansion(leaves, leaf_octant, rotation, axial_one, LEAF_PREC)
    box_total = box_octant.shape[0]
    parents = (leaf_parent[:, None] == jnp.arange(box_total, dtype=jnp.int32)[None, :]).astype(
        jnp.float32
    )
    wide_ident = jnp.eye(channel, dtype=jnp.float32)
    wide_parents = (wide_ident[:, None, :, None] * parents[None, :, None, :]).reshape(
        channel * leaf_total, channel * box_total
    )
    boxes = jnp.einsum("lpC,CD->lpD", moved, wide_parents, precision=HI)
    outer = move_expansion(boxes, box_octant, rotation, axial_two, HI)
    return outer.reshape(degrees, orders, channel, box_total).sum(-1)


def owner_frame(owner_sum, owner_turn, owner_shift):
    degrees, orders, width = owner_sum.shape
    states = width // 4
    first = jnp.einsum("lqp,lpC->lqC", owner_turn[0], owner_sum, precision=HI)
    second = jnp.einsum("lqp,lpC->lqC", owner_turn[1], owner_sum, precision=HI)
    turned = complex_join(first, second, width // 2)
    moved = turned.reshape(degrees, orders, 2, 2, states)
    moved = jnp.transpose(moved, (1, 3, 0, 2, 4)).reshape(orders, 2 * degrees, 2 * states)
    root_degrees = owner_shift.shape[3]
    mats = owner_shift.reshape(2, orders, 2 * root_degrees, 2 * degrees)
    first = jnp.einsum("qab,qbC->qaC", mats[0], moved, precision=HI)
    second = jnp.einsum("qab,qbC->qaC", mats[1], moved, precision=HI)
    joined = complex_join(first, second, states).reshape(orders, 2, root_degrees, 2, states)
    framed = jnp.transpose(joined, (2, 1, 3, 4, 0)).reshape(root_degrees, 4 * states, orders)
    return framed.astype(jnp.bfloat16)


def rotate_back(framed, functions, azimuth, half_orders):
    root_degrees, width = (framed.shape[0], framed.shape[1])
    states = width // 4
    orders_here = functions.shape[2]
    values = jnp.einsum("nCm,nmj->nCj", framed, functions, preferred_element_type=jnp.float32)
    values = values.reshape(root_degrees, 2, 2, states, orders_here)
    order_values = (jnp.arange(orders_here, dtype=jnp.int32) - half_orders).astype(jnp.float32)
    cosine = jnp.cos(order_values * azimuth)
    sine = jnp.sin(order_values * azimuth)
    real_part = cosine * values[:, :, 0] + sine * values[:, :, 1]
    imag_part = cosine * values[:, :, 1] - sine * values[:, :, 0]
    joined = jnp.stack([real_part, imag_part], axis=2)
    return jnp.transpose(joined, (4, 1, 2, 3, 0)).reshape(orders_here, 4 * states * root_degrees)


def legendre_field(root_coef, table):
    orders_here, root_degrees = (table.shape[0], table.shape[1])
    lat_total = table.shape[2] // 2
    rows = root_coef.shape[1] // root_degrees
    states = rows // 4
    half = rows // 2
    blocks = jnp.einsum(
        "jrn,jnK->jrK",
        root_coef.reshape(orders_here, rows, root_degrees),
        table,
        preferred_element_type=jnp.float32,
    )
    theta_part = blocks[:, :half, :lat_total] + blocks[:, half:, lat_total:]
    cross = blocks[:, :half, lat_total:] + blocks[:, half:, :lat_total]
    phi_part = jnp.concatenate([-cross[:, states:], cross[:, :states]], axis=1)
    return jnp.concatenate([theta_part, phi_part], axis=1)


def synthesize(spectrum, longitudes):
    orders = spectrum.shape[-1]
    fine = 128
    coarse = longitudes // fine
    order_ids = jnp.arange(orders, dtype=jnp.int32) - orders // 2
    coarse_angle = jnp.mod(order_ids[:, None] * (fine * jnp.arange(coarse, dtype=jnp.int32))[None, :], longitudes)
    coarse_angle = coarse_angle.astype(jnp.float32) * (2.0 * math.pi / longitudes)
    fine_angle = jnp.mod(order_ids[:, None] * jnp.arange(fine, dtype=jnp.int32)[None, :], longitudes)
    fine_angle = fine_angle.astype(jnp.float32) * (2.0 * math.pi / longitudes)
    pc, ps = jnp.cos(coarse_angle), jnp.sin(coarse_angle)
    qc, qs = jnp.cos(fine_angle), jnp.sin(fine_angle)
    spec = spectrum.astype(jnp.float32)
    sr, si = spec[:, 0], spec[:, 1]
    vr = sr[..., None, :] * pc.T - si[..., None, :] * ps.T
    vi = sr[..., None, :] * ps.T + si[..., None, :] * pc.T
    lhs = jnp.stack([vr, vi], axis=-2)
    rhs = jnp.stack([jnp.stack([qc, qs], axis=1), jnp.stack([-qs, qc], axis=1)], axis=0)
    out = jnp.einsum("csxkam,amfb->xscfkb", lhs, rhs, precision=HI)
    out = out.reshape(out.shape[:4] + (longitudes,))
    return out * (1.0 / math.sqrt(orders))


def pair_sum(x, axis):
    if lax.axis_size(axis) != 2:
        return lax.psum(x, axis)
    return x + lax.ppermute(x, axis, [(0, 1), (1, 0)])


def pair_scatter(x, axis):
    me = lax.axis_index(axis)
    keep = jnp.where(me == 0, x[0], x[1])
    give = jnp.where(me == 0, x[1], x[0])
    got = lax.ppermute(give.astype(jnp.bfloat16), axis, [(0, 1), (1, 0)])
    return keep + got.astype(keep.dtype)


def shift_all_to_all(x, axis):
    n = lax.axis_size(axis)
    me = lax.axis_index(axis)
    rows = jnp.arange(n)
    result = jnp.zeros_like(x)
    for step in range(n):
        target = (me + step) % n
        piece = jnp.take(x, target, axis=0)
        if step:
            piece = lax.ppermute(piece, axis, [(i, (i + step) % n) for i in range(n)])
        source = (me - step) % n
        result = jnp.where((rows == source).reshape((n,) + (1,) * (x.ndim - 1)), piece[None], result)
    return result


def shift_reduce_scatter(x, axis):
    n = lax.axis_size(axis)
    me = lax.axis_index(axis)
    total = jnp.take(x, me, axis=0)
    for step in range(1, n):
        piece = jnp.take(x, (me + step) % n, axis=0).astype(jnp.bfloat16)
        piece = lax.ppermute(piece, axis, [(i, (i + step) % n) for i in range(n)])
        total = total + piece.astype(total.dtype)
    return total


def on_device(
    sphere_coef,
    live_blocks,
    cluster,
    leaf_parent,
    leaf_octant,
    box_octant,
    rotation,
    axial_one,
    axial_two,
    owner_rotation,
    owner_axial,
    owner_angle,
    turn_table,
    angular_table,
):
    partial_owner = local_boxes(
        sphere_coef,
        live_blocks[0],
        cluster,
        leaf_parent,
        leaf_octant,
        box_octant,
        rotation,
        axial_one,
        axial_two,
    )
    owner_sum = pair_sum(pair_sum(partial_owner, "sub"), "state")
    framed = owner_frame(owner_sum, owner_rotation[0], owner_axial[0])
    leaf_size = lax.axis_size("leaf")
    orders = turn_table.shape[3]
    half_orders = orders // 2
    own_orders = orders // leaf_size
    own_azimuth = owner_angle[lax.axis_index("leaf")]
    piece = turn_table[0]
    contribution = rotate_back(framed, piece, own_azimuth, half_orders)
    if leaf_size <= 4:
        root = shift_reduce_scatter(contribution.reshape((leaf_size, own_orders) + contribution.shape[1:]), "leaf")
    else:
        root = lax.psum_scatter(contribution, "leaf", scatter_dimension=0, tiled=True)
    root_coef = root.astype(jnp.bfloat16)
    field = legendre_field(root_coef, angular_table)
    channel = field.shape[1]
    group_size = lax.axis_size("state") * lax.axis_size("sub")
    lat_rows = field.shape[2] // (leaf_size * group_size)
    shaped = field.reshape(own_orders, channel, leaf_size, group_size, lat_rows)
    shaped = jnp.transpose(shaped, (3, 2, 1, 4, 0)).reshape(
        group_size, leaf_size, channel * lat_rows * own_orders
    )
    if lax.axis_size("state") == 2 and lax.axis_size("sub") == 2 and leaf_size <= 4:
        halves = shaped.reshape((2, 2) + shaped.shape[1:])
        summed = pair_scatter(pair_scatter(jnp.swapaxes(halves, 0, 1), "sub"), "state")
        moved = shift_all_to_all(summed.astype(jnp.bfloat16), "leaf")
    else:
        summed = lax.psum_scatter(shaped.astype(jnp.bfloat16), ("state", "sub"), scatter_dimension=0, tiled=True)
        moved = lax.all_to_all(summed, "leaf", split_axis=1, concat_axis=2, tiled=True)
    spectrum = moved.reshape(leaf_size, channel, lat_rows, own_orders)
    spectrum = jnp.transpose(spectrum, (1, 2, 0, 3)).reshape(2, 2, -1, lat_rows, orders)
    return synthesize(spectrum, PHI)


def solution(mesh):
    return jax.shard_map(
        on_device,
        mesh=mesh,
        in_specs=(
            P(None, None, None, None, None, ("groups", "leaf", "state", "sub")),
            P(("groups", "leaf", "state", "sub")),
            P(("groups", "leaf", "state", "sub")),
            P(("groups", "leaf", "state", "sub")),
            P(("groups", "leaf", "state", "sub")),
            P(("groups", "leaf", "state", "sub")),
            P(),
            P(),
            P(),
            P(("groups", "leaf"), None, None, None, None),
            P(("groups", "leaf"), None, None, None, ("state", "sub"), None, None),
            P("groups"),
            P(("groups", "leaf"), ("state", "sub"), None, None),
            P("leaf", ("state", "sub"), None),
        ),
        out_specs=P(("groups", "leaf", "state", "sub"), None, None, None, None),
        check_vma=False,
    )
```

profile of v0, /device:TPU:0, one launch (start us, length us, event | category | flops | bytes accessed | tf_op | source)
XLA Modules:
  0.0 103.5 jit_solution(8502665907060461152)
XLA Ops:
  0.0 0.6 fusion.34
  0.6 4.5 %fusion.48 = (f32[1,12,8,25,25]{4,0,3,1,2:T(1,128)S(1)}, f32[1,12,8,25,25]{4,0,3,1,2:T(1,128)S(1)}) fusion(f32[2,12,8,25,25]{4,0,3,1,2:T(2,128)} %bitcast.233), kind=kLoop, calls=%fused_computation.156 | loop fusion | bytes 960000 | tf_op jit(solution)/shard_map/slice | solution.py:30
  5.2 2.3 %copy.177 = f32[1,12,8,25,25]{3,2,4,1,0:T(8,128)} copy(f32[1,12,8,25,25]{4,0,3,1,2:T(1,128)S(1)} %get-tuple-element.40) | data formatting | bytes 480000 | tf_op jit(solution)/shard_map/slice | solution.py:31
  7.4 1.7 %squeeze.65 = f32[12,200,25]{1,2,0:T(8,128)S(1)} reshape(f32[1,12,8,25,25]{3,2,4,1,0:T(8,128)} %copy.177) | data formatting | bytes 480000 | tf_op jit(solution)/shard_map/squeeze | solution.py:31
  9.9 1.5 %mul.402 = bf16[1024,256]{0,1:T(8,128)(2,1)} reshape(bf16[16,64,16,16]{1,0,3,2:T(8,128)(2,1)S(1)} %broadcast_multiply_fusion) | data formatting | bytes 1048576 | tf_op jit(solution)/shard_map/mul | solution.py:77
  11.5 2.7 %reshape.608 = bf16[300,1024]{1,0:T(8,128)(2,1)S(1)} reshape(bf16[12,25,2,2,4,64]{5,4,3,2,1,0:T(4,128)(2,1)} %param.18) | data formatting | bytes 1228800 | tf_op jit(solution)/shard_map/reshape | solution.py:81
  14.2 1.0 convolution_bitcast_fusion.6
  15.2 1.0 reshape.609
  16.2 1.1 %copy.176 = f32[1,12,8,25,25]{3,2,4,1,0:T(8,128)S(1)} copy(f32[1,12,8,25,25]{4,0,3,1,2:T(1,128)S(1)} %get-tuple-element.39) | data formatting | bytes 480000 | tf_op jit(solution)/shard_map/slice | solution.py:30
  19.0 1.6 %pad_maximum_fusion = f32[12,200,256]{2,1,0:T(8,128)} fusion(f32[12,200,128]{2,1,0:T(8,128)S(1)} %get-tuple-element.36, f32[12,200,128]{2,1,0:T(8,128)S(1)} %get-tuple-element.35), kind=kLoop, calls=%fused_computation.2 | loop fusion | flops 614400 | bytes 4915200 | tf_op jit(solution)/shard_map/concatenate | solution.py:18
  20.6 2.5 %reshape.610 = f32[12,8,25,256]{3,2,1,0:T(8,128)S(1)} reshape(f32[12,200,256]{2,1,0:T(8,128)} %pad_maximum_fusion) | data formatting | bytes 4915200 | tf_op jit(solution)/shard_map/reshape | solution.py:32
  23.1 0.7 fusion.42
  23.8 0.6 tile.8
  24.4 1.5 %tile.9 = f32[8,256]{1,0:T(8,128)} reshape(f32[8,16,16]{2,1,0:T(8,128)} %tile.8) | data formatting | bytes 16384 | tf_op jit(solution)/shard_map/tile | solution.py:35
  25.9 1.8 %multiply_reduce_fusion.1 = bf16[12,25,256]{2,1,0:T(8,128)(2,1)} fusion(f32[12,8,25,256]{3,2,1,0:T(8,128)S(1)} %reshape.610, f32[8,256]{1,0:T(8,128)} %tile.9), kind=kLoop, calls=%fused_computation.1 | loop fusion | flops 1152000 | bytes 2619392 | tf_op jit(solution)/shard_map/reduce_sum | solution.py:36
  27.8 1.2 %reshape.611 = bf16[12,25,2,2,64]{4,3,2,1,0:T(2,128)(2,1)S(1)} reshape(bf16[12,25,256]{2,1,0:T(8,128)(2,1)} %multiply_reduce_fusion.1) | data formatting | bytes 307200 | tf_op jit(solution)/shard_map/reshape | solution.py:42
  29.5 0.6 copy.224
  30.3 0.8 copy.223
  32.2 1.0 copy.183
  33.3 1.2 %reshape.614 = bf16[12,25,256]{2,1,0:T(8,128)(2,1)S(1)} reshape(bf16[12,25,2,2,64]{4,3,2,1,0:T(2,128)(2,1)} %copy.183) | data formatting | bytes 307200 | tf_op jit(solution)/shard_map/reshape | solution.py:48
  34.5 2.9 %fusion.47 = (f32[1,12,8,25,25]{3,0,4,1,2:T(1,128)S(1)}, f32[1,12,8,25,25]{3,0,4,1,2:T(1,128)}) fusion(f32[2,12,8,25,25]{3,0,4,1,2:T(2,128)S(1)} %bitcast.234), kind=kLoop, calls=%fused_computation.155 | loop fusion | bytes 960000 | tf_op jit(solution)/shard_map/slice | solution.py:30
  37.9 0.8 copy-done.2
  40.6 1.6 %pad_maximum_fusion.1 = f32[12,200,256]{2,1,0:T(8,128)} fusion(f32[12,200,128]{2,1,0:T(8,128)S(1)} %get-tuple-element.34, f32[12,200,128]{2,1,0:T(8,128)S(1)} %get-tuple-element.33), kind=kLoop, calls=%fused_computation.3 | loop fusion | flops 614400 | bytes 4915200 | tf_op jit(solution)/shard_map/concatenate | solution.py:18
  42.2 2.5 %reshape.615 = f32[12,8,25,256]{3,2,1,0:T(8,128)S(1)} reshape(f32[12,200,256]{2,1,0:T(8,128)} %pad_maximum_fusion.1) | data formatting | bytes 4915200 | tf_op jit(solution)/shard_map/reshape | solution.py:32
  44.7 1.9 %multiply_reduce_fusion = f32[12,25,256]{2,1,0:T(8,128)} fusion(f32[12,8,25,256]{3,2,1,0:T(8,128)S(1)} %reshape.615, f32[8,256]{1,0:T(8,128)} %tile.9), kind=kLoop, calls=%fused_computation | loop fusion | flops 1152000 | bytes 2772992 | tf_op jit(solution)/shard_map/reduce_sum | solution.py:36
  46.8 1.6 %fusion.53 = f32[12,25,32]{1,2,0:T(8,128)S(1)} fusion(f32[12,25,256]{2,1,0:T(8,128)} %multiply_reduce_fusion, f32[256,32,1]{0,1,2:T(8,128)S(1)} %reshape.778), kind=kOutput, calls=%fused_computation.161 | convolution fusion | flops 14745600 | bytes 378368 | tf_op jit(solution)/shard_map/lpC,CD->lpD/dot_general | solution.py:94
  48.4 1.3 %convolution_bitcast_fusion.5 = f32[12,200,32]{1,2,0:T(8,128)S(1)} fusion(f32[12,25,32]{1,2,0:T(8,128)S(1)} %fusion.53, f32[12,200,25]{1,2,0:T(8,128)} %copy-done.5), kind=kOutput, calls=%fused_computation.16 | convolution fusion | flops 11520000 | bytes 585600 | tf_op jit(solution)/shard_map/lQp,lpC->lQC/dot_general | solution.py:30
  51.9 0.7 copy.225
  52.9 0.9 copy.226
  58.2 2.1 %fusion.52 = (f32[1,1,12,25,25]{4,1,3,2,0:T(1,128)}, f32[1,1,12,25,25]{4,1,3,2,0:T(1,128)}) fusion(f32[1,2,12,25,25]{4,1,3,2,0:T(2,128)} %param.27), kind=kLoop, calls=%fused_computation.160 | loop fusion | bytes 120000 | tf_op jit(solution)/shard_map/slice | solution.py:102
  60.4 0.6 fusion.18
  61.6 0.7 fusion.43
  62.3 2.6 %collective-permute-start.1 = (f32[12,25,16]{1,2,0:T(8,128)S(1)}, f32[12,25,16]{1,2,0:T(8,128)S(1)}, u32[]{:S(2)}, u32[]{:S(2)}) collective-permute-start(f32[12,25,16]{1,2,0:T(8,128)S(1)} %add.191), channel_id=1, source_target_pairs={{0,2},{2,0},{1,3},{3,1},{4,6},{6,4},{5,7},{7,5},{8,10},{10,8},{9,1... | collective-permute-start | bytes 57608 | tf_op jit(solution)/shard_map/ppermute | solution.py:174
  66.2 2.1 %collective-permute-done.1 = f32[12,25,16]{1,2,0:T(8,128)S(1)} collective-permute-done((f32[12,25,16]{1,2,0:T(8,128)S(1)}, f32[12,25,16]{1,2,0:T(8,128)S(1)}, u32[]{:S(2)}, u32[]{:S(2)}) %collective-permute-start.1) | collective-permute-done | bytes 19232 | tf_op jit(solution)/shard_map/ppermute | solution.py:174
  71.3 1.0 constant_dynamic-slice_fusion.1
  72.3 1.9 %collective-permute-start.2 = (bf16[64,512]{0,1:T(8,128)(2,1)S(1)}, bf16[64,512]{0,1:T(8,128)(2,1)S(1)}, u32[]{:S(2)}, u32[]{:S(2)}) collective-permute-start(bf16[64,512]{0,1:T(8,128)(2,1)S(1)} %bitcast_convert_fusion.1), channel_id=1, source_target_pairs={{0,4},{4,8},{8,12},{12,0},{1,5},{5,9},{9,13},{13,1},{2,6},{6,10},{... | collective-permute-start | bytes 196616 | tf_op jit(solution)/shard_map/ppermute | solution.py:206
  74.2 2.7 %collective-permute-start.3 = (bf16[64,512]{0,1:T(8,128)(2,1)S(1)}, bf16[64,512]{0,1:T(8,128)(2,1)S(1)}, u32[]{:S(2)}, u32[]{:S(2)}) collective-permute-start(bf16[64,512]{0,1:T(8,128)(2,1)S(1)} %bitcast_convert_fusion), channel_id=1, source_target_pairs={{0,8},{4,12},{8,0},{12,4},{1,9},{5,13},{9,1},{13,5},{2,10},{6,14},... | collective-permute-start | bytes 196616 | tf_op jit(solution)/shard_map/ppermute | solution.py:206
  76.9 1.4 %collective-permute-start.4 = (bf16[64,512]{0,1:T(8,128)(2,1)S(1)}, bf16[64,512]{0,1:T(8,128)(2,1)S(1)}, u32[]{:S(2)}, u32[]{:S(2)}) collective-permute-start(bf16[64,512]{0,1:T(8,128)(2,1)S(1)} %convert_element_type.180), channel_id=1, source_target_pairs={{0,12},{4,0},{8,4},{12,8},{1,13},{5,1},{9,5},{13,9},{2,14},{6,2},{... | collective-permute-start | bytes 196616 | tf_op jit(solution)/shard_map/ppermute | solution.py:206
  78.4 0.8 copy.212
  79.2 1.4 %collective-permute-done.2 = bf16[64,512]{0,1:T(8,128)(2,1)S(1)} collective-permute-done((bf16[64,512]{0,1:T(8,128)(2,1)S(1)}, bf16[64,512]{0,1:T(8,128)(2,1)S(1)}, u32[]{:S(2)}, u32[]{:S(2)}) %collective-permute-start.2) | collective-permute-done | bytes 65568 | tf_op jit(solution)/shard_map/ppermute | solution.py:206
  80.7 4.6 %collective-permute-done.3 = bf16[64,512]{0,1:T(8,128)(2,1)S(1)} collective-permute-done((bf16[64,512]{0,1:T(8,128)(2,1)S(1)}, bf16[64,512]{0,1:T(8,128)(2,1)S(1)}, u32[]{:S(2)}, u32[]{:S(2)}) %collective-permute-start.3) | collective-permute-done | bytes 65568 | tf_op jit(solution)/shard_map/ppermute | solution.py:206
  87.0 1.1 %collective-permute-done.5 = bf16[2,4,1024]{2,1,0:T(4,128)(2,1)S(1)} collective-permute-done((bf16[2,4,1024]{2,1,0:T(4,128)(2,1)S(1)}, bf16[2,4,1024]{2,1,0:T(4,128)(2,1)S(1)}, u32[]{:S(2)}, u32[]{:S(2)}) %collective-permute-start.5) | collective-permute-done | bytes 16416 | tf_op jit(solution)/shard_map/ppermute | solution.py:181
  88.1 1.6 %collective-permute-start.6 = (bf16[4,1024]{1,0:T(4,128)(2,1)S(1)}, bf16[4,1024]{1,0:T(4,128)(2,1)S(1)}, u32[]{:S(2)}, u32[]{:S(2)}) collective-permute-start(bf16[4,1024]{1,0:T(4,128)(2,1)S(1)} %fusion.31), channel_id=1, source_target_pairs={{0,2},{2,0},{1,3},{3,1},{4,6},{6,4},{5,7},{7,5},{8,10},{10,8},{9,1... | collective-permute-start | bytes 24584 | tf_op jit(solution)/shard_map/ppermute | solution.py:181
  89.7 2.1 %collective-permute-done.6 = bf16[4,1024]{1,0:T(4,128)(2,1)S(1)} collective-permute-done((bf16[4,1024]{1,0:T(4,128)(2,1)S(1)}, bf16[4,1024]{1,0:T(4,128)(2,1)S(1)}, u32[]{:S(2)}, u32[]{:S(2)}) %collective-permute-start.6) | collective-permute-done | bytes 8224 | tf_op jit(solution)/shard_map/ppermute | solution.py:181
  91.9 4.4 %collective-permute-start.7 = (bf16[1024]{0:T(1024)(128)(2,1)S(1)}, bf16[1024]{0:T(1024)(128)(2,1)S(1)}, u32[]{:S(2)}, u32[]{:S(2)}) collective-permute-start(bf16[1024]{0:T(1024)(128)(2,1)S(1)} %get-tuple-element.29), channel_id=1, source_target_pairs={{0,12},{4,0},{8,4},{12,8},{1,13},{5,1},{9,5},{13,9},{2,14},{6,2},{... | collective-permute-start | bytes 6152 | tf_op jit(solution)/shard_map/ppermute | solution.py:194
  97.7 3.1 %collective-permute-done.8 = bf16[1024]{0:T(1024)(128)(2,1)S(1)} collective-permute-done((bf16[1024]{0:T(1024)(128)(2,1)S(1)}, bf16[1024]{0:T(1024)(128)(2,1)S(1)}, u32[]{:S(2)}, u32[]{:S(2)}) %collective-permute-start.8) | collective-permute-done | bytes 2080 | tf_op jit(solution)/shard_map/ppermute | solution.py:194
  100.8 1.2 %collective-permute-done.9 = bf16[1024]{0:T(1024)(128)(2,1)S(1)} collective-permute-done((bf16[1024]{0:T(1024)(128)(2,1)S(1)}, bf16[1024]{0:T(1024)(128)(2,1)S(1)}, u32[]{:S(2)}, u32[]{:S(2)}) %collective-permute-start.9) | collective-permute-done | bytes 2080 | tf_op jit(solution)/shard_map/ppermute | solution.py:194
  102.7 0.8 copy.219
  (161 shorter events, 21.7 us)
Async XLA Ops:
  0.0 70.0 %copy-start = (bf16[1,32,25,256]{3,1,2,0:T(8,128)(2,1)S(1)}, bf16[1,32,25,256]{3,1,2,0:T(8,128)(2,1)}, u32[]{:S(2)}) copy-start(bf16[1,32,25,256]{3,1,2,0:T(8,128)(2,1)} %param.30) | copy-start | bytes 1228804
  5.2 4.6 %copy-start.18 = (s32[64]{0:T(128)S(1)}, s32[64]{0:T(128)}, u32[]{:S(2)}) copy-start(s32[64]{0:T(128)} %param.20) | copy-start | bytes 772
  9.1 8.6 %copy-start.3 = (f32[12,200,25]{1,2,0:T(8,128)}, f32[12,200,25]{1,2,0:T(8,128)S(1)}, u32[]{:S(2)}) copy-start(f32[12,200,25]{1,2,0:T(8,128)S(1)} %squeeze.65) | copy-start | bytes 720004
  11.5 2.7 %copy-start.10 = (bf16[1024,256]{0,1:T(8,128)(2,1)S(1)}, bf16[1024,256]{0,1:T(8,128)(2,1)}, u32[]{:S(2)}) copy-start(bf16[1024,256]{0,1:T(8,128)(2,1)} %mul.402) | copy-start | bytes 1572868
  17.7 1.1 %copy-start.5 = (f32[12,200,25]{1,2,0:T(8,128)}, f32[12,200,25]{1,2,0:T(8,128)S(1)}, u32[]{:S(2)}) copy-start(f32[12,200,25]{1,2,0:T(8,128)S(1)} %squeeze.64) | copy-start | bytes 720004
  27.8 1.6 %copy-start.16 = (f32[2,25,2,12,2,12]{1,4,5,3,2,0:T(2,128)S(1)}, f32[2,25,2,12,2,12]{1,4,5,3,2,0:T(2,128)}, u32[]{:S(2)}) copy-start(f32[2,25,2,12,2,12]{1,4,5,3,2,0:T(2,128)} %param.25) | copy-start | bytes 345604
  31.7 2.8 %copy-start.1 = (f32[8,2,12,25,25]{4,1,3,2,0:T(2,128)S(1)}, f32[8,2,12,25,25]{4,1,3,2,0:T(2,128)}, u32[]{:S(2)}) copy-start(f32[8,2,12,25,25]{4,1,3,2,0:T(2,128)} %param.24) | copy-start | bytes 1440004
  37.4 1.3 %copy-start.2 = (f32[1,12,8,25,25]{3,0,4,1,2:T(1,128)S(1)}, f32[1,12,8,25,25]{3,0,4,1,2:T(1,128)}, u32[]{:S(2)}) copy-start(f32[1,12,8,25,25]{3,0,4,1,2:T(1,128)} %get-tuple-element.38) | copy-start | bytes 720004
  37.9 1.3 %copy-start.6 = (f32[12,200,25]{1,2,0:T(8,128)}, f32[12,200,25]{1,2,0:T(8,128)S(1)}, u32[]{:S(2)}) copy-start(f32[12,200,25]{1,2,0:T(8,128)S(1)} %squeeze.68) | copy-start | bytes 720004
  39.2 1.1 %copy-start.8 = (f32[12,200,25]{1,2,0:T(8,128)}, f32[12,200,25]{1,2,0:T(8,128)S(1)}, u32[]{:S(2)}) copy-start(f32[12,200,25]{1,2,0:T(8,128)S(1)} %squeeze.69) | copy-start | bytes 720004
  44.7 1.9 %copy-start.19 = (s32[16]{0:T(128)S(1)}, s32[16]{0:T(128)}, u32[]{:S(2)}) copy-start(s32[16]{0:T(128)} %param.21) | copy-start | bytes 196
  44.7 1.9 %copy-start.17 = (f32[16,16]{0,1:T(8,128)S(1)}, f32[16,16]{0,1:T(8,128)}, u32[]{:S(2)}) copy-start(f32[16,16]{0,1:T(8,128)} %fusion.34) | copy-start | bytes 3076
  46.6 3.2 %copy-start.4 = (f32[12,200,25]{1,2,0:T(8,128)S(1)}, f32[12,200,25]{1,2,0:T(8,128)}, u32[]{:S(2)}) copy-start(f32[12,200,25]{1,2,0:T(8,128)} %copy-done.3) | copy-start | bytes 720004
  50.1 0.7 copy-start.20
  50.8 1.1 %copy-start.14 = (f32[2,25,2,12,2,12]{1,4,5,3,2,0:T(2,128)S(1)}, f32[2,25,2,12,2,12]{1,4,5,3,2,0:T(2,128)}, u32[]{:S(2)}) copy-start(f32[2,25,2,12,2,12]{1,4,5,3,2,0:T(2,128)} %param.26) | copy-start | bytes 345604
  54.1 1.0 copy-start.7
  54.9 1.0 copy-start.9
  56.9 3.4 %copy-start.11 = (f32[1,2,25,2,32,2,12]{4,5,6,3,2,1,0:T(2,128)S(1)}, f32[1,2,25,2,32,2,12]{4,5,6,3,2,1,0:T(2,128)}, u32[]{:S(2)}) copy-start(f32[1,2,25,2,32,2,12]{4,5,6,3,2,1,0:T(2,128)} %param.28) | copy-start | bytes 921604
  57.7 4.6 %collective-permute-start = (f32[12,25,16]{1,2,0:T(8,128)S(1)}, f32[12,25,16]{1,2,0:T(8,128)S(1)}, u32[]{:S(2)}, u32[]{:S(2)}) collective-permute-start(f32[12,25,16]{1,2,0:T(8,128)S(1)} %reduce_sum.49), channel_id=1, source_target_pairs={{0,1},{1,0},{2,3},{3,2},{4,5},{5,4},{6,7},{7,6},{8,9},{9,8},{10,11... | collective-permute-start | bytes 57608 | tf_op jit(solution)/shard_map/ppermute | solution.py:174
  60.3 0.7 copy-start.21
  62.3 6.0 %collective-permute-start.1 = (f32[12,25,16]{1,2,0:T(8,128)S(1)}, f32[12,25,16]{1,2,0:T(8,128)S(1)}, u32[]{:S(2)}, u32[]{:S(2)}) collective-permute-start(f32[12,25,16]{1,2,0:T(8,128)S(1)} %add.191), channel_id=1, source_target_pairs={{0,2},{2,0},{1,3},{3,1},{4,6},{6,4},{5,7},{7,5},{8,10},{10,8},{9,1... | collective-permute-start | bytes 57608 | tf_op jit(solution)/shard_map/ppermute | solution.py:174
  65.2 3.1 %copy-start.13 = (f32[1,1,12,25,25]{4,1,3,2,0:T(1,128)S(1)}, f32[1,1,12,25,25]{4,1,3,2,0:T(1,128)}, u32[]{:S(2)}) copy-start(f32[1,1,12,25,25]{4,1,3,2,0:T(1,128)} %get-tuple-element.63) | copy-start | bytes 90004
  65.2 3.4 %copy-start.12 = (f32[1,1,12,25,25]{4,1,3,2,0:T(1,128)S(1)}, f32[1,1,12,25,25]{4,1,3,2,0:T(1,128)}, u32[]{:S(2)}) copy-start(f32[1,1,12,25,25]{4,1,3,2,0:T(1,128)} %get-tuple-element.64) | copy-start | bytes 90004
  71.2 7.2 %copy-start.15 = (bf16[64,32,32]{0,2,1:T(8,128)(2,1)S(1)}, bf16[64,32,32]{0,2,1:T(8,128)(2,1)}, u32[]{:S(2)}) copy-start(bf16[64,32,32]{0,2,1:T(8,128)(2,1)} %param.31) | copy-start | bytes 393220
  72.3 8.4 %collective-permute-start.2 = (bf16[64,512]{0,1:T(8,128)(2,1)S(1)}, bf16[64,512]{0,1:T(8,128)(2,1)S(1)}, u32[]{:S(2)}, u32[]{:S(2)}) collective-permute-start(bf16[64,512]{0,1:T(8,128)(2,1)S(1)} %bitcast_convert_fusion.1), channel_id=1, source_target_pairs={{0,4},{4,8},{8,12},{12,0},{1,5},{5,9},{9,13},{13,1},{2,6},{6,10},{... | collective-permute-start | bytes 196616 | tf_op jit(solution)/shard_map/ppermute | solution.py:206
  74.2 11.1 %collective-permute-start.3 = (bf16[64,512]{0,1:T(8,128)(2,1)S(1)}, bf16[64,512]{0,1:T(8,128)(2,1)S(1)}, u32[]{:S(2)}, u32[]{:S(2)}) collective-permute-start(bf16[64,512]{0,1:T(8,128)(2,1)S(1)} %bitcast_convert_fusion), channel_id=1, source_target_pairs={{0,8},{4,12},{8,0},{12,4},{1,9},{5,13},{9,1},{13,5},{2,10},{6,14},... | collective-permute-start | bytes 196616 | tf_op jit(solution)/shard_map/ppermute | solution.py:206
  76.9 8.4 %collective-permute-start.4 = (bf16[64,512]{0,1:T(8,128)(2,1)S(1)}, bf16[64,512]{0,1:T(8,128)(2,1)S(1)}, u32[]{:S(2)}, u32[]{:S(2)}) collective-permute-start(bf16[64,512]{0,1:T(8,128)(2,1)S(1)} %convert_element_type.180), channel_id=1, source_target_pairs={{0,12},{4,0},{8,4},{12,8},{1,13},{5,1},{9,5},{13,9},{2,14},{6,2},{... | collective-permute-start | bytes 196616 | tf_op jit(solution)/shard_map/ppermute | solution.py:206
  86.8 1.2 %collective-permute-start.5 = (bf16[2,4,1024]{2,1,0:T(4,128)(2,1)S(1)}, bf16[2,4,1024]{2,1,0:T(4,128)(2,1)S(1)}, u32[]{:S(2)}, u32[]{:S(2)}) collective-permute-start(bf16[2,4,1024]{2,1,0:T(4,128)(2,1)S(1)} %fusion.29), channel_id=1, source_target_pairs={{0,1},{1,0},{2,3},{3,2},{4,5},{5,4},{6,7},{7,6},{8,9},{9,8},{10,11... | collective-permute-start | bytes 49160 | tf_op jit(solution)/shard_map/ppermute | solution.py:181
  88.1 3.7 %collective-permute-start.6 = (bf16[4,1024]{1,0:T(4,128)(2,1)S(1)}, bf16[4,1024]{1,0:T(4,128)(2,1)S(1)}, u32[]{:S(2)}, u32[]{:S(2)}) collective-permute-start(bf16[4,1024]{1,0:T(4,128)(2,1)S(1)} %fusion.31), channel_id=1, source_target_pairs={{0,2},{2,0},{1,3},{3,1},{4,6},{6,4},{5,7},{7,5},{8,10},{10,8},{9,1... | collective-permute-start | bytes 24584 | tf_op jit(solution)/shard_map/ppermute | solution.py:181
  91.9 5.7 %collective-permute-start.7 = (bf16[1024]{0:T(1024)(128)(2,1)S(1)}, bf16[1024]{0:T(1024)(128)(2,1)S(1)}, u32[]{:S(2)}, u32[]{:S(2)}) collective-permute-start(bf16[1024]{0:T(1024)(128)(2,1)S(1)} %get-tuple-element.29), channel_id=1, source_target_pairs={{0,12},{4,0},{8,4},{12,8},{1,13},{5,1},{9,5},{13,9},{2,14},{6,2},{... | collective-permute-start | bytes 6152 | tf_op jit(solution)/shard_map/ppermute | solution.py:194
  96.3 4.5 %collective-permute-start.8 = (bf16[1024]{0:T(1024)(128)(2,1)S(1)}, bf16[1024]{0:T(1024)(128)(2,1)S(1)}, u32[]{:S(2)}, u32[]{:S(2)}) collective-permute-start(bf16[1024]{0:T(1024)(128)(2,1)S(1)} %get-tuple-element.32), channel_id=1, source_target_pairs={{0,8},{4,12},{8,0},{12,4},{1,9},{5,13},{9,1},{13,5},{2,10},{6,14},... | collective-permute-start | bytes 6152 | tf_op jit(solution)/shard_map/ppermute | solution.py:194
  96.7 5.4 %collective-permute-start.9 = (bf16[1024]{0:T(1024)(128)(2,1)S(1)}, bf16[1024]{0:T(1024)(128)(2,1)S(1)}, u32[]{:S(2)}, u32[]{:S(2)}) collective-permute-start(bf16[1024]{0:T(1024)(128)(2,1)S(1)} %get-tuple-element.31), channel_id=1, source_target_pairs={{0,4},{4,8},{8,12},{12,0},{1,5},{5,9},{9,13},{13,1},{2,6},{6,10},{... | collective-permute-start | bytes 6152 | tf_op jit(solution)/shard_map/ppermute | solution.py:194
where the time goes:
time: 104 us; the launch traced here: 103 us
  local copies, waits for them, and re-layouts  45.5 us (44%)
  waiting for transfers between devices  16.3 us (16%)
  starting transfers between devices  15.7 us (15%)
  other arithmetic  14.3 us (14%)
  matrix products  10.1 us (10%)
  between operations  1.71 us (2%)
    slice x4, local copies, waits for them, and re-layouts, turn_select(): first = jnp.einsum('lQp,lpC->lQC', mats[0], vectors, precision=prec)  8.68 us
    ppermute x3, waiting for transfers between devices, shift_reduce_scatter(): piece = lax.ppermute(piece, axis, [(i, (i + step) % n) for i in range(n)])  6.06 us
    reshape x4, local copies, waits for them, and re-layouts, turn_select(): complex_join(first, second, width // 2).reshape(degrees, 8, orders, width)  5.98 us
    ppermute x3, starting transfers between devices, shift_reduce_scatter(): piece = lax.ppermute(piece, axis, [(i, (i + step) % n) for i in range(n)])  5.94 us
    ppermute x3, starting transfers between devices, shift_all_to_all(): piece = lax.ppermute(piece, axis, [(i, (i + step) % n) for i in range(n)])  5.02 us
    ppermute x3, waiting for transfers between devices, shift_all_to_all(): piece = lax.ppermute(piece, axis, [(i, (i + step) % n) for i in range(n)])  4.91 us
    reduce_sum x4, other arithmetic, turn_select(): return jnp.sum(joined * column_mask[None, :, None, :], axis=1)  4.75 us
    concatenate x8, other arithmetic, complex_join(): return jnp.concatenate([real, imag], axis=-1)  3.47 us
  transfers between devices with their start and end apart: 10, of which 8 were waited for; matrix products, arithmetic and copies ran while one was open for 6% of the time, Pallas kernels for 0%

commit v1 on v0

--- a/solution.py
+++ b/solution.py
@@ -92,7 +92,7 @@
         channel * leaf_total, channel * box_total
     )
     boxes = jnp.einsum("lpC,CD->lpD", moved, wide_parents, precision=HI)
-    outer = move_expansion(boxes, box_octant, rotation, axial_two, HI)
+    outer = move_expansion(boxes, box_octant, rotation, axial_two, LEAF_PREC)
     return outer.reshape(degrees, orders, channel, box_total).sum(-1)
 
 

time: 104 us -> 100 us (0.962)
  local copies, waits for them, and re-layouts: 45.5 us -> 41.2 us
    unnamed x45 -> x41, local copies, waits for them, and re-layouts: 2.41 us -> 2.29 us
where the time goes in v1:
time: 100 us; the launch traced here: 99.5 us
  local copies, waits for them, and re-layouts  41.2 us (41%)
  waiting for transfers between devices  16.2 us (16%)
  starting transfers between devices  15.7 us (16%)
  other arithmetic  14.3 us (14%)
  matrix products  10.3 us (10%)
  between operations  1.74 us (2%)
    slice x4, local copies, waits for them, and re-layouts, turn_select(): first = jnp.einsum('lQp,lpC->lQC', mats[0], vectors, precision=prec)  8.61 us
    ppermute x3, waiting for transfers between devices, shift_reduce_scatter(): piece = lax.ppermute(piece, axis, [(i, (i + step) % n) for i in range(n)])  6.05 us
    reshape x4, local copies, waits for them, and re-layouts, turn_select(): complex_join(first, second, width // 2).reshape(degrees, 8, orders, width)  5.98 us
    ppermute x3, starting transfers between devices, shift_reduce_scatter(): piece = lax.ppermute(piece, axis, [(i, (i + step) % n) for i in range(n)])  5.92 us
    ppermute x3, starting transfers between devices, shift_all_to_all(): piece = lax.ppermute(piece, axis, [(i, (i + step) % n) for i in range(n)])  5.03 us
    ppermute x3, waiting for transfers between devices, shift_all_to_all(): piece = lax.ppermute(piece, axis, [(i, (i + step) % n) for i in range(n)])  4.9 us
    reduce_sum x4, other arithmetic, turn_select(): return jnp.sum(joined * column_mask[None, :, None, :], axis=1)  4.77 us
    concatenate x8, other arithmetic, complex_join(): return jnp.concatenate([real, imag], axis=-1)  3.46 us
  transfers between devices with their start and end apart: 10, of which 8 were waited for; matrix products, arithmetic and copies ran while one was open for 6% of the time, Pallas kernels for 0%

profile of v1, /device:TPU:0, one launch (start us, length us, event | category | flops | bytes accessed | tf_op | source)
XLA Modules:
  0.0 99.5 jit_solution(989697608507828641)
XLA Ops:
  0.0 0.6 fusion.34
  0.6 4.5 %fusion.48 = (bf16[1,12,8,25,25]{4,0,3,1,2:T(2,128)(2,1)S(1)}, bf16[1,12,8,25,25]{4,0,3,1,2:T(2,128)(2,1)S(1)}) fusion(f32[2,12,8,25,25]{4,0,3,1,2:T(2,128)} %bitcast.233), kind=kLoop, calls=%fused_computation.156 | loop fusion | bytes 480000 | tf_op jit(solution)/shard_map/slice | solution.py:30
  5.2 1.2 %copy.177 = bf16[1,12,8,25,25]{3,2,4,1,0:T(8,128)(2,1)S(1)} copy(bf16[1,12,8,25,25]{4,0,3,1,2:T(2,128)(2,1)S(1)} %get-tuple-element.40) | data formatting | bytes 240000 | tf_op jit(solution)/shard_map/slice | solution.py:31
  6.4 1.2 %squeeze.65 = bf16[12,200,25]{1,2,0:T(8,128)(2,1)} reshape(bf16[1,12,8,25,25]{3,2,4,1,0:T(8,128)(2,1)S(1)} %copy.177) | data formatting | bytes 240000 | tf_op jit(solution)/shard_map/squeeze | solution.py:31
  8.4 0.7 mul.402
  9.1 2.6 %reshape.608 = bf16[300,1024]{1,0:T(8,128)(2,1)S(1)} reshape(bf16[12,25,2,2,4,64]{5,4,3,2,1,0:T(4,128)(2,1)} %param.18) | data formatting | bytes 1228800 | tf_op jit(solution)/shard_map/reshape | solution.py:81
  12.2 1.2 %copy.176 = bf16[1,12,8,25,25]{3,2,4,1,0:T(8,128)(2,1)S(1)} copy(bf16[1,12,8,25,25]{4,0,3,1,2:T(2,128)(2,1)S(1)} %get-tuple-element.39) | data formatting | bytes 240000 | tf_op jit(solution)/shard_map/slice | solution.py:30
  15.3 1.6 %pad_maximum_fusion = f32[12,200,256]{2,1,0:T(8,128)} fusion(f32[12,200,128]{2,1,0:T(8,128)S(1)} %get-tuple-element.36, f32[12,200,128]{2,1,0:T(8,128)S(1)} %get-tuple-element.35), kind=kLoop, calls=%fused_computation.2 | loop fusion | flops 614400 | bytes 4915200 | tf_op jit(solution)/shard_map/concatenate | solution.py:18
  16.9 2.5 %reshape.610 = f32[12,8,25,256]{3,2,1,0:T(8,128)S(1)} reshape(f32[12,200,256]{2,1,0:T(8,128)} %pad_maximum_fusion) | data formatting | bytes 4915200 | tf_op jit(solution)/shard_map/reshape | solution.py:32
  19.4 0.7 fusion.42
  20.0 0.6 tile.8
  20.7 1.5 %tile.9 = f32[8,256]{1,0:T(8,128)} reshape(f32[8,16,16]{2,1,0:T(8,128)} %tile.8) | data formatting | bytes 16384 | tf_op jit(solution)/shard_map/tile | solution.py:35
  22.2 1.8 %multiply_reduce_fusion.1 = bf16[12,25,256]{2,1,0:T(8,128)(2,1)} fusion(f32[12,8,25,256]{3,2,1,0:T(8,128)S(1)} %reshape.610, f32[8,256]{1,0:T(8,128)} %tile.9), kind=kLoop, calls=%fused_computation.1 | loop fusion | flops 1152000 | bytes 2619392 | tf_op jit(solution)/shard_map/reduce_sum | solution.py:36
  24.0 1.2 %reshape.611 = bf16[12,25,2,2,64]{4,3,2,1,0:T(2,128)(2,1)S(1)} reshape(bf16[12,25,256]{2,1,0:T(8,128)(2,1)} %multiply_reduce_fusion.1) | data formatting | bytes 307200 | tf_op jit(solution)/shard_map/reshape | solution.py:42
  25.8 0.6 copy.224
  26.6 0.8 copy.223
  28.5 1.0 %copy.183 = bf16[12,25,2,2,64]{4,3,2,1,0:T(2,128)(2,1)} copy(bf16[12,25,2,2,64]{4,2,0,3,1:T(2,128)(2,1)S(1)} %bitcast.236) | data formatting | bytes 307200 | tf_op jit(solution)/shard_map/transpose | solution.py:48
  29.5 1.2 %reshape.614 = bf16[12,25,256]{2,1,0:T(8,128)(2,1)S(1)} reshape(bf16[12,25,2,2,64]{4,3,2,1,0:T(2,128)(2,1)} %copy.183) | data formatting | bytes 307200 | tf_op jit(solution)/shard_map/reshape | solution.py:48
  30.7 2.7 %fusion.47 = (bf16[1,12,8,25,25]{3,0,4,1,2:T(2,128)(2,1)S(1)}, bf16[1,12,8,25,25]{3,0,4,1,2:T(2,128)(2,1)}) fusion(f32[2,12,8,25,25]{3,0,4,1,2:T(2,128)S(1)} %bitcast.234), kind=kLoop, calls=%fused_computation.155 | loop fusion | bytes 480000 | tf_op jit(solution)/shard_map/slice | solution.py:30
  34.0 0.7 copy-done.2
  36.7 1.6 %pad_maximum_fusion.1 = f32[12,200,256]{2,1,0:T(8,128)} fusion(f32[12,200,128]{2,1,0:T(8,128)S(1)} %get-tuple-element.34, f32[12,200,128]{2,1,0:T(8,128)S(1)} %get-tuple-element.33), kind=kLoop, calls=%fused_computation.3 | loop fusion | flops 614400 | bytes 4915200 | tf_op jit(solution)/shard_map/concatenate | solution.py:18
  38.3 2.5 %reshape.615 = f32[12,8,25,256]{3,2,1,0:T(8,128)S(1)} reshape(f32[12,200,256]{2,1,0:T(8,128)} %pad_maximum_fusion.1) | data formatting | bytes 4915200 | tf_op jit(solution)/shard_map/reshape | solution.py:32
  40.8 1.9 %multiply_reduce_fusion = f32[12,25,256]{2,1,0:T(8,128)} fusion(f32[12,8,25,256]{3,2,1,0:T(8,128)S(1)} %reshape.615, f32[8,256]{1,0:T(8,128)} %tile.9), kind=kLoop, calls=%fused_computation | loop fusion | flops 1152000 | bytes 2772992 | tf_op jit(solution)/shard_map/reduce_sum | solution.py:36
  42.9 1.6 %fusion.53 = bf16[12,25,32]{1,2,0:T(8,128)(2,1)S(1)} fusion(f32[12,25,256]{2,1,0:T(8,128)} %multiply_reduce_fusion, f32[256,32,1]{0,1,2:T(8,128)S(1)} %reshape.778), kind=kOutput, calls=%fused_computation.161 | convolution fusion | flops 14745600 | bytes 359168 | tf_op jit(solution)/shard_map/lpC,CD->lpD/dot_general | solution.py:94
  44.5 1.1 %convolution_bitcast_fusion.5 = f32[12,200,32]{1,2,0:T(8,128)S(1)} fusion(bf16[12,25,32]{1,2,0:T(8,128)(2,1)S(1)} %fusion.53, bf16[12,200,25]{1,2,0:T(8,128)(2,1)} %copy-done.5), kind=kOutput, calls=%fused_computation.16 | convolution fusion | flops 3840000 | bytes 446400 | tf_op jit(solution)/shard_map/lQp,lpC->lQC/dot_general | solution.py:30
  47.6 0.6 copy.225
  48.4 0.8 copy.226
  52.5 1.4 %fusion.52 = (f32[1,1,12,25,25]{4,1,3,2,0:T(1,128)S(1)}, f32[1,1,12,25,25]{4,1,3,2,0:T(1,128)S(1)}) fusion(f32[1,2,12,25,25]{4,1,3,2,0:T(2,128)} %param.27), kind=kLoop, calls=%fused_computation.160 | loop fusion | bytes 120000 | tf_op jit(solution)/shard_map/slice | solution.py:102
  55.2 0.7 fusion.43
  55.9 2.6 %collective-permute-start.1 = (f32[12,25,16]{1,2,0:T(8,128)S(1)}, f32[12,25,16]{1,2,0:T(8,128)S(1)}, u32[]{:S(2)}, u32[]{:S(2)}) collective-permute-start(f32[12,25,16]{1,2,0:T(8,128)S(1)} %add.191), channel_id=1, source_target_pairs={{0,2},{2,0},{1,3},{3,1},{4,6},{6,4},{5,7},{7,5},{8,10},{10,8},{9,1... | collective-permute-start | bytes 57608 | tf_op jit(solution)/shard_map/ppermute | solution.py:174
  59.8 2.1 %collective-permute-done.1 = f32[12,25,16]{1,2,0:T(8,128)S(1)} collective-permute-done((f32[12,25,16]{1,2,0:T(8,128)S(1)}, f32[12,25,16]{1,2,0:T(8,128)S(1)}, u32[]{:S(2)}, u32[]{:S(2)}) %collective-permute-start.1) | collective-permute-done | bytes 19232 | tf_op jit(solution)/shard_map/ppermute | solution.py:174
  61.9 0.6 copy-done.11
  62.6 1.2 %convolution_bitcast_fusion.15 = f32[12,25,16]{1,2,0:T(8,128)S(1)} fusion(f32[1,1,12,25,25]{4,1,3,2,0:T(1,128)S(1)} %get-tuple-element.63, f32[12,25,16]{1,2,0:T(8,128)S(1)} %add.191, f32[12,25,16]{1,2,0:T(8,128)} %copy-done.11), kind=kOutput, calls=%fused_computation.30 | convolution fusion | flops 724800 | bytes 87600 | tf_op jit(solution)/shard_map/lqp,lpC->lqC/dot_general | solution.py:102
  63.7 1.2 %convolution_bitcast_fusion.14 = f32[12,25,16]{1,2,0:T(8,128)S(1)} fusion(f32[1,1,12,25,25]{4,1,3,2,0:T(1,128)S(1)} %get-tuple-element.64, f32[12,25,16]{1,2,0:T(8,128)S(1)} %add.191, f32[12,25,16]{1,2,0:T(8,128)} %copy-done.11), kind=kOutput, calls=%fused_computation.29 | convolution fusion | flops 724800 | bytes 87600 | tf_op jit(solution)/shard_map/lqp,lpC->lqC/dot_general | solution.py:103
  67.3 1.0 constant_dynamic-slice_fusion.1
  68.3 1.9 %collective-permute-start.2 = (bf16[64,512]{0,1:T(8,128)(2,1)S(1)}, bf16[64,512]{0,1:T(8,128)(2,1)S(1)}, u32[]{:S(2)}, u32[]{:S(2)}) collective-permute-start(bf16[64,512]{0,1:T(8,128)(2,1)S(1)} %bitcast_convert_fusion.1), channel_id=1, source_target_pairs={{0,4},{4,8},{8,12},{12,0},{1,5},{5,9},{9,13},{13,1},{2,6},{6,10},{... | collective-permute-start | bytes 196616 | tf_op jit(solution)/shard_map/ppermute | solution.py:206
  70.2 2.7 %collective-permute-start.3 = (bf16[64,512]{0,1:T(8,128)(2,1)S(1)}, bf16[64,512]{0,1:T(8,128)(2,1)S(1)}, u32[]{:S(2)}, u32[]{:S(2)}) collective-permute-start(bf16[64,512]{0,1:T(8,128)(2,1)S(1)} %bitcast_convert_fusion), channel_id=1, source_target_pairs={{0,8},{4,12},{8,0},{12,4},{1,9},{5,13},{9,1},{13,5},{2,10},{6,14},... | collective-permute-start | bytes 196616 | tf_op jit(solution)/shard_map/ppermute | solution.py:206
  72.9 1.4 %collective-permute-start.4 = (bf16[64,512]{0,1:T(8,128)(2,1)S(1)}, bf16[64,512]{0,1:T(8,128)(2,1)S(1)}, u32[]{:S(2)}, u32[]{:S(2)}) collective-permute-start(bf16[64,512]{0,1:T(8,128)(2,1)S(1)} %convert_element_type.180), channel_id=1, source_target_pairs={{0,12},{4,0},{8,4},{12,8},{1,13},{5,1},{9,5},{13,9},{2,14},{6,2},{... | collective-permute-start | bytes 196616 | tf_op jit(solution)/shard_map/ppermute | solution.py:206
  74.5 0.8 copy.212
  75.3 1.4 %collective-permute-done.2 = bf16[64,512]{0,1:T(8,128)(2,1)S(1)} collective-permute-done((bf16[64,512]{0,1:T(8,128)(2,1)S(1)}, bf16[64,512]{0,1:T(8,128)(2,1)S(1)}, u32[]{:S(2)}, u32[]{:S(2)}) %collective-permute-start.2) | collective-permute-done | bytes 65568 | tf_op jit(solution)/shard_map/ppermute | solution.py:206
  76.7 4.6 %collective-permute-done.3 = bf16[64,512]{0,1:T(8,128)(2,1)S(1)} collective-permute-done((bf16[64,512]{0,1:T(8,128)(2,1)S(1)}, bf16[64,512]{0,1:T(8,128)(2,1)S(1)}, u32[]{:S(2)}, u32[]{:S(2)}) %collective-permute-start.3) | collective-permute-done | bytes 65568 | tf_op jit(solution)/shard_map/ppermute | solution.py:206
  83.0 1.1 %collective-permute-done.5 = bf16[2,4,1024]{2,1,0:T(4,128)(2,1)S(1)} collective-permute-done((bf16[2,4,1024]{2,1,0:T(4,128)(2,1)S(1)}, bf16[2,4,1024]{2,1,0:T(4,128)(2,1)S(1)}, u32[]{:S(2)}, u32[]{:S(2)}) %collective-permute-start.5) | collective-permute-done | bytes 16416 | tf_op jit(solution)/shard_map/ppermute | solution.py:181
  84.1 1.6 %collective-permute-start.6 = (bf16[4,1024]{1,0:T(4,128)(2,1)S(1)}, bf16[4,1024]{1,0:T(4,128)(2,1)S(1)}, u32[]{:S(2)}, u32[]{:S(2)}) collective-permute-start(bf16[4,1024]{1,0:T(4,128)(2,1)S(1)} %fusion.31), channel_id=1, source_target_pairs={{0,2},{2,0},{1,3},{3,1},{4,6},{6,4},{5,7},{7,5},{8,10},{10,8},{9,1... | collective-permute-start | bytes 24584 | tf_op jit(solution)/shard_map/ppermute | solution.py:181
  85.7 2.1 %collective-permute-done.6 = bf16[4,1024]{1,0:T(4,128)(2,1)S(1)} collective-permute-done((bf16[4,1024]{1,0:T(4,128)(2,1)S(1)}, bf16[4,1024]{1,0:T(4,128)(2,1)S(1)}, u32[]{:S(2)}, u32[]{:S(2)}) %collective-permute-start.6) | collective-permute-done | bytes 8224 | tf_op jit(solution)/shard_map/ppermute | solution.py:181
  87.9 4.4 %collective-permute-start.7 = (bf16[1024]{0:T(1024)(128)(2,1)S(1)}, bf16[1024]{0:T(1024)(128)(2,1)S(1)}, u32[]{:S(2)}, u32[]{:S(2)}) collective-permute-start(bf16[1024]{0:T(1024)(128)(2,1)S(1)} %get-tuple-element.29), channel_id=1, source_target_pairs={{0,12},{4,0},{8,4},{12,8},{1,13},{5,1},{9,5},{13,9},{2,14},{6,2},{... | collective-permute-start | bytes 6152 | tf_op jit(solution)/shard_map/ppermute | solution.py:194
  93.7 3.1 %collective-permute-done.8 = bf16[1024]{0:T(1024)(128)(2,1)S(1)} collective-permute-done((bf16[1024]{0:T(1024)(128)(2,1)S(1)}, bf16[1024]{0:T(1024)(128)(2,1)S(1)}, u32[]{:S(2)}, u32[]{:S(2)}) %collective-permute-start.8) | collective-permute-done | bytes 2080 | tf_op jit(solution)/shard_map/ppermute | solution.py:194
  96.9 1.2 %collective-permute-done.9 = bf16[1024]{0:T(1024)(128)(2,1)S(1)} collective-permute-done((bf16[1024]{0:T(1024)(128)(2,1)S(1)}, bf16[1024]{0:T(1024)(128)(2,1)S(1)}, u32[]{:S(2)}, u32[]{:S(2)}) %collective-permute-start.9) | collective-permute-done | bytes 2080 | tf_op jit(solution)/shard_map/ppermute | solution.py:194
  98.7 0.8 copy.219
  (157 shorter events, 20.9 us)
Async XLA Ops:
  0.0 66.1 %copy-start = (bf16[1,32,25,256]{3,1,2,0:T(8,128)(2,1)S(1)}, bf16[1,32,25,256]{3,1,2,0:T(8,128)(2,1)}, u32[]{:S(2)}) copy-start(bf16[1,32,25,256]{3,1,2,0:T(8,128)(2,1)} %param.30) | copy-start | bytes 1228804
  5.1 3.1 %copy-start.16 = (s32[64]{0:T(128)S(1)}, s32[64]{0:T(128)}, u32[]{:S(2)}) copy-start(s32[64]{0:T(128)} %param.20) | copy-start | bytes 772
  12.1 1.8 %copy-start.3 = (bf16[12,200,25]{1,2,0:T(8,128)(2,1)S(1)}, bf16[12,200,25]{1,2,0:T(8,128)(2,1)}, u32[]{:S(2)}) copy-start(bf16[12,200,25]{1,2,0:T(8,128)(2,1)} %squeeze.65) | copy-start | bytes 360004
  13.9 1.1 %copy-start.5 = (bf16[12,200,25]{1,2,0:T(8,128)(2,1)}, bf16[12,200,25]{1,2,0:T(8,128)(2,1)S(1)}, u32[]{:S(2)}) copy-start(bf16[12,200,25]{1,2,0:T(8,128)(2,1)S(1)} %squeeze.64) | copy-start | bytes 360004
  24.0 1.6 %copy-start.13 = (f32[2,25,2,12,2,12]{1,4,5,3,2,0:T(2,128)S(1)}, f32[2,25,2,12,2,12]{1,4,5,3,2,0:T(2,128)}, u32[]{:S(2)}) copy-start(f32[2,25,2,12,2,12]{1,4,5,3,2,0:T(2,128)} %param.25) | copy-start | bytes 345604
  27.9 2.8 %copy-start.1 = (f32[8,2,12,25,25]{4,1,3,2,0:T(2,128)S(1)}, f32[8,2,12,25,25]{4,1,3,2,0:T(2,128)}, u32[]{:S(2)}) copy-start(f32[8,2,12,25,25]{4,1,3,2,0:T(2,128)} %param.24) | copy-start | bytes 1440004
  33.5 1.3 %copy-start.2 = (bf16[1,12,8,25,25]{3,0,4,1,2:T(2,128)(2,1)S(1)}, bf16[1,12,8,25,25]{3,0,4,1,2:T(2,128)(2,1)}, u32[]{:S(2)}) copy-start(bf16[1,12,8,25,25]{3,0,4,1,2:T(2,128)(2,1)} %get-tuple-element.38) | copy-start | bytes 360004
  34.0 1.8 %copy-start.6 = (bf16[12,200,25]{1,2,0:T(8,128)(2,1)}, bf16[12,200,25]{1,2,0:T(8,128)(2,1)S(1)}, u32[]{:S(2)}) copy-start(bf16[12,200,25]{1,2,0:T(8,128)(2,1)S(1)} %squeeze.68) | copy-start | bytes 360004
  35.3 1.1 %copy-start.8 = (bf16[12,200,25]{1,2,0:T(8,128)(2,1)}, bf16[12,200,25]{1,2,0:T(8,128)(2,1)S(1)}, u32[]{:S(2)}) copy-start(bf16[12,200,25]{1,2,0:T(8,128)(2,1)S(1)} %squeeze.69) | copy-start | bytes 360004
  40.8 1.9 %copy-start.17 = (s32[16]{0:T(128)S(1)}, s32[16]{0:T(128)}, u32[]{:S(2)}) copy-start(s32[16]{0:T(128)} %param.21) | copy-start | bytes 196
  40.8 1.9 %copy-start.15 = (f32[16,16]{0,1:T(8,128)S(1)}, f32[16,16]{0,1:T(8,128)}, u32[]{:S(2)}) copy-start(f32[16,16]{0,1:T(8,128)} %fusion.34) | copy-start | bytes 3076
  42.7 2.9 %copy-start.4 = (bf16[12,200,25]{1,2,0:T(8,128)(2,1)S(1)}, bf16[12,200,25]{1,2,0:T(8,128)(2,1)}, u32[]{:S(2)}) copy-start(bf16[12,200,25]{1,2,0:T(8,128)(2,1)} %squeeze.65) | copy-start | bytes 360004
  45.9 0.7 copy-start.18
  45.9 1.5 %copy-start.14 = (f32[2,25,2,12,2,12]{1,4,5,3,2,0:T(2,128)S(1)}, f32[2,25,2,12,2,12]{1,4,5,3,2,0:T(2,128)}, u32[]{:S(2)}) copy-start(f32[2,25,2,12,2,12]{1,4,5,3,2,0:T(2,128)} %param.26) | copy-start | bytes 345604
  48.4 1.7 %copy-start.7 = (bf16[12,200,25]{1,2,0:T(8,128)(2,1)S(1)}, bf16[12,200,25]{1,2,0:T(8,128)(2,1)}, u32[]{:S(2)}) copy-start(bf16[12,200,25]{1,2,0:T(8,128)(2,1)} %copy-done.6) | copy-start | bytes 360004
  49.2 1.1 %copy-start.9 = (bf16[12,200,25]{1,2,0:T(8,128)(2,1)S(1)}, bf16[12,200,25]{1,2,0:T(8,128)(2,1)}, u32[]{:S(2)}) copy-start(bf16[12,200,25]{1,2,0:T(8,128)(2,1)} %copy-done.8) | copy-start | bytes 360004
  51.2 2.7 %copy-start.10 = (f32[1,2,25,2,32,2,12]{4,5,6,3,2,1,0:T(2,128)S(1)}, f32[1,2,25,2,32,2,12]{4,5,6,3,2,1,0:T(2,128)}, u32[]{:S(2)}) copy-start(f32[1,2,25,2,32,2,12]{4,5,6,3,2,1,0:T(2,128)} %param.28) | copy-start | bytes 921604
  52.0 3.9 %collective-permute-start = (f32[12,25,16]{1,2,0:T(8,128)S(1)}, f32[12,25,16]{1,2,0:T(8,128)S(1)}, u32[]{:S(2)}, u32[]{:S(2)}) collective-permute-start(f32[12,25,16]{1,2,0:T(8,128)S(1)} %reduce_sum.49), channel_id=1, source_target_pairs={{0,1},{1,0},{2,3},{3,2},{4,5},{5,4},{6,7},{7,6},{8,9},{9,8},{10,11... | collective-permute-start | bytes 57608 | tf_op jit(solution)/shard_map/ppermute | solution.py:174
  53.9 0.7 copy-start.19
  55.9 6.0 %collective-permute-start.1 = (f32[12,25,16]{1,2,0:T(8,128)S(1)}, f32[12,25,16]{1,2,0:T(8,128)S(1)}, u32[]{:S(2)}, u32[]{:S(2)}) collective-permute-start(f32[12,25,16]{1,2,0:T(8,128)S(1)} %add.191), channel_id=1, source_target_pairs={{0,2},{2,0},{1,3},{3,1},{4,6},{6,4},{5,7},{7,5},{8,10},{10,8},{9,1... | collective-permute-start | bytes 57608 | tf_op jit(solution)/shard_map/ppermute | solution.py:174
  61.9 0.6 copy-start.11
  67.3 7.2 %copy-start.12 = (bf16[64,32,32]{0,2,1:T(8,128)(2,1)S(1)}, bf16[64,32,32]{0,2,1:T(8,128)(2,1)}, u32[]{:S(2)}) copy-start(bf16[64,32,32]{0,2,1:T(8,128)(2,1)} %param.31) | copy-start | bytes 393220
  68.3 8.3 %collective-permute-start.2 = (bf16[64,512]{0,1:T(8,128)(2,1)S(1)}, bf16[64,512]{0,1:T(8,128)(2,1)S(1)}, u32[]{:S(2)}, u32[]{:S(2)}) collective-permute-start(bf16[64,512]{0,1:T(8,128)(2,1)S(1)} %bitcast_convert_fusion.1), channel_id=1, source_target_pairs={{0,4},{4,8},{8,12},{12,0},{1,5},{5,9},{9,13},{13,1},{2,6},{6,10},{... | collective-permute-start | bytes 196616 | tf_op jit(solution)/shard_map/ppermute | solution.py:206
  70.2 11.1 %collective-permute-start.3 = (bf16[64,512]{0,1:T(8,128)(2,1)S(1)}, bf16[64,512]{0,1:T(8,128)(2,1)S(1)}, u32[]{:S(2)}, u32[]{:S(2)}) collective-permute-start(bf16[64,512]{0,1:T(8,128)(2,1)S(1)} %bitcast_convert_fusion), channel_id=1, source_target_pairs={{0,8},{4,12},{8,0},{12,4},{1,9},{5,13},{9,1},{13,5},{2,10},{6,14},... | collective-permute-start | bytes 196616 | tf_op jit(solution)/shard_map/ppermute | solution.py:206
  72.9 8.4 %collective-permute-start.4 = (bf16[64,512]{0,1:T(8,128)(2,1)S(1)}, bf16[64,512]{0,1:T(8,128)(2,1)S(1)}, u32[]{:S(2)}, u32[]{:S(2)}) collective-permute-start(bf16[64,512]{0,1:T(8,128)(2,1)S(1)} %convert_element_type.180), channel_id=1, source_target_pairs={{0,12},{4,0},{8,4},{12,8},{1,13},{5,1},{9,5},{13,9},{2,14},{6,2},{... | collective-permute-start | bytes 196616 | tf_op jit(solution)/shard_map/ppermute | solution.py:206
  82.8 1.2 %collective-permute-start.5 = (bf16[2,4,1024]{2,1,0:T(4,128)(2,1)S(1)}, bf16[2,4,1024]{2,1,0:T(4,128)(2,1)S(1)}, u32[]{:S(2)}, u32[]{:S(2)}) collective-permute-start(bf16[2,4,1024]{2,1,0:T(4,128)(2,1)S(1)} %fusion.29), channel_id=1, source_target_pairs={{0,1},{1,0},{2,3},{3,2},{4,5},{5,4},{6,7},{7,6},{8,9},{9,8},{10,11... | collective-permute-start | bytes 49160 | tf_op jit(solution)/shard_map/ppermute | solution.py:181
  84.1 3.7 %collective-permute-start.6 = (bf16[4,1024]{1,0:T(4,128)(2,1)S(1)}, bf16[4,1024]{1,0:T(4,128)(2,1)S(1)}, u32[]{:S(2)}, u32[]{:S(2)}) collective-permute-start(bf16[4,1024]{1,0:T(4,128)(2,1)S(1)} %fusion.31), channel_id=1, source_target_pairs={{0,2},{2,0},{1,3},{3,1},{4,6},{6,4},{5,7},{7,5},{8,10},{10,8},{9,1... | collective-permute-start | bytes 24584 | tf_op jit(solution)/shard_map/ppermute | solution.py:181
  87.9 5.7 %collective-permute-start.7 = (bf16[1024]{0:T(1024)(128)(2,1)S(1)}, bf16[1024]{0:T(1024)(128)(2,1)S(1)}, u32[]{:S(2)}, u32[]{:S(2)}) collective-permute-start(bf16[1024]{0:T(1024)(128)(2,1)S(1)} %get-tuple-element.29), channel_id=1, source_target_pairs={{0,12},{4,0},{8,4},{12,8},{1,13},{5,1},{9,5},{13,9},{2,14},{6,2},{... | collective-permute-start | bytes 6152 | tf_op jit(solution)/shard_map/ppermute | solution.py:194
  92.3 4.5 %collective-permute-start.8 = (bf16[1024]{0:T(1024)(128)(2,1)S(1)}, bf16[1024]{0:T(1024)(128)(2,1)S(1)}, u32[]{:S(2)}, u32[]{:S(2)}) collective-permute-start(bf16[1024]{0:T(1024)(128)(2,1)S(1)} %get-tuple-element.32), channel_id=1, source_target_pairs={{0,8},{4,12},{8,0},{12,4},{1,9},{5,13},{9,1},{13,5},{2,10},{6,14},... | collective-permute-start | bytes 6152 | tf_op jit(solution)/shard_map/ppermute | solution.py:194
  92.7 5.4 %collective-permute-start.9 = (bf16[1024]{0:T(1024)(128)(2,1)S(1)}, bf16[1024]{0:T(1024)(128)(2,1)S(1)}, u32[]{:S(2)}, u32[]{:S(2)}) collective-permute-start(bf16[1024]{0:T(1024)(128)(2,1)S(1)} %get-tuple-element.31), channel_id=1, source_target_pairs={{0,4},{4,8},{8,12},{12,0},{1,5},{5,9},{9,13},{13,1},{2,6},{6,10},{... | collective-permute-start | bytes 6152 | tf_op jit(solution)/shard_map/ppermute | solution.py:194

commit v2 on v1

--- a/solution.py
+++ b/solution.py
@@ -73,13 +73,9 @@
     member = (
         (cluster[:, None] == jnp.arange(leaf_total, dtype=jnp.int32)[None, :]) & alive[:, None]
     ).astype(jnp.bfloat16)
-    ident = jnp.eye(channel, dtype=jnp.bfloat16)
-    spread = (ident[:, None, :, None] * member[None, :, None, :]).reshape(
-        channel * slots, channel * leaf_total
-    )
     leaves = jnp.dot(
-        sphere_block.reshape(degrees * orders, channel * slots),
-        spread,
+        sphere_block.reshape(degrees * orders * channel, slots),
+        member,
         preferred_element_type=jnp.float32,
     ).reshape(degrees, orders, channel * leaf_total)
     moved = move_expansion(leaves, leaf_octant, rotation, axial_one, LEAF_PREC)

time: 100 us -> 92.5 us (0.925)
  other arithmetic: 14.3 us -> 11.4 us
  matrix products: 10.3 us -> 7.76 us
  local copies, waits for them, and re-layouts: 41.2 us -> 39.2 us
    slice x2, local copies, waits for them, and re-layouts: 1.34 us -> 2.93 us  [turn_select(): second = sign * jnp.einsum('lQp,lpC->lQC', mats[1], vectors, precision=prec)]
    reshape x2 -> x1, local copies, waits for them, and re-layouts: 2.68 us -> 1.18 us  [local_boxes(): leaves = jnp.dot(sphere_block.reshape(degrees * orders * channel, slots),...]
    reduce_sum x4, other arithmetic: 4.77 us -> 3.29 us  [turn_select(): return jnp.sum(joined * column_mask[None, :, None, :], axis=1)]
    slice x4, local copies, waits for them, and re-layouts: 8.61 us -> 9.76 us  [turn_select(): first = jnp.einsum('lQp,lpC->lQC', mats[0], vectors, precision=prec)]
    unnamed x41 -> x37, local copies, waits for them, and re-layouts: 2.29 us -> 2.23 us
where the time goes in v2:
time: 92.5 us; the launch traced here: 92 us
  local copies, waits for them, and re-layouts  39.2 us (42%)
  starting transfers between devices  16 us (17%)
  waiting for transfers between devices  16 us (17%)
  other arithmetic  11.4 us (12%)
  matrix products  7.76 us (8%)
  between operations  1.69 us (2%)
    slice x4, local copies, waits for them, and re-layouts, turn_select(): first = jnp.einsum('lQp,lpC->lQC', mats[0], vectors, precision=prec)  9.76 us
    reshape x4, local copies, waits for them, and re-layouts, turn_select(): complex_join(first, second, width // 2).reshape(degrees, 8, orders, width)  6.21 us
    ppermute x3, starting transfers between devices, shift_reduce_scatter(): piece = lax.ppermute(piece, axis, [(i, (i + step) % n) for i in range(n)])  6.2 us
    ppermute x3, waiting for transfers between devices, shift_reduce_scatter(): piece = lax.ppermute(piece, axis, [(i, (i + step) % n) for i in range(n)])  5.83 us
    ppermute x3, starting transfers between devices, shift_all_to_all(): piece = lax.ppermute(piece, axis, [(i, (i + step) % n) for i in range(n)])  4.99 us
    ppermute x3, waiting for transfers between devices, shift_all_to_all(): piece = lax.ppermute(piece, axis, [(i, (i + step) % n) for i in range(n)])  4.94 us
    concatenate x8, other arithmetic, complex_join(): return jnp.concatenate([real, imag], axis=-1)  3.47 us
    reduce_sum x4, other arithmetic, turn_select(): return jnp.sum(joined * column_mask[None, :, None, :], axis=1)  3.29 us
  transfers between devices with their start and end apart: 10, of which 8 were waited for; matrix products, arithmetic and copies ran while one was open for 6% of the time, Pallas kernels for 0%

profile of v2, /device:TPU:0, one launch (start us, length us, event | category | flops | bytes accessed | tf_op | source)
XLA Modules:
  0.0 92.0 jit_solution(4696669765095728481)
XLA Ops:
  0.0 5.7 %fusion.50 = (bf16[1,12,8,25,25]{4,0,3,1,2:T(2,128)(2,1)S(1)}, bf16[1,12,8,25,25]{4,0,3,1,2:T(2,128)(2,1)}) fusion(f32[2,12,8,25,25]{4,0,3,1,2:T(2,128)} %bitcast.229), kind=kLoop, calls=%fused_computation.156 | loop fusion | bytes 480000 | tf_op jit(solution)/shard_map/slice | solution.py:30
  5.7 2.8 %copy.180 = bf16[1,12,8,25,25]{3,2,4,1,0:T(8,128)(2,1)S(1)} copy(bf16[1,12,8,25,25]{4,0,3,1,2:T(2,128)(2,1)} %get-tuple-element.40) | data formatting | bytes 240000 | tf_op jit(solution)/shard_map/slice | solution.py:31
  9.7 0.5 convolution_bitcast_fusion
  10.2 0.6 copy.178
  10.8 1.2 %reshape.561 = bf16[12,25,256]{2,1,0:T(8,128)(2,1)S(1)} reshape(bf16[4800,16]{1,0:T(8,128)(2,1)S(1)} %copy.178) | data formatting | bytes 307200 | tf_op jit(solution)/shard_map/reshape | solution.py:80
  12.0 1.2 %copy.179 = bf16[1,12,8,25,25]{3,2,4,1,0:T(8,128)(2,1)S(1)} copy(bf16[1,12,8,25,25]{4,0,3,1,2:T(2,128)(2,1)S(1)} %get-tuple-element.39) | data formatting | bytes 240000 | tf_op jit(solution)/shard_map/slice | solution.py:30
  13.7 0.5 convolution_bitcast_fusion.2
  15.0 1.6 %pad_maximum_fusion = f32[12,200,256]{2,1,0:T(8,128)} fusion(f32[12,200,128]{2,1,0:T(8,128)S(1)} %get-tuple-element.36, f32[12,200,128]{2,1,0:T(8,128)S(1)} %get-tuple-element.35), kind=kLoop, calls=%fused_computation.3 | loop fusion | flops 614400 | bytes 4915200 | tf_op jit(solution)/shard_map/concatenate | solution.py:18
  16.6 2.5 %reshape.562 = f32[12,8,25,256]{3,2,1,0:T(8,128)S(1)} reshape(f32[12,200,256]{2,1,0:T(8,128)} %pad_maximum_fusion) | data formatting | bytes 4915200 | tf_op jit(solution)/shard_map/reshape | solution.py:32
  19.2 0.6 tile.8
  19.8 0.9 %tile.9 = f32[8,256]{1,0:T(8,128)S(1)} reshape(f32[8,16,16]{2,1,0:T(8,128)} %tile.8) | data formatting | bytes 16384 | tf_op jit(solution)/shard_map/tile | solution.py:35
  20.7 1.1 %multiply_reduce_fusion.1 = bf16[12,25,256]{2,1,0:T(8,128)(2,1)} fusion(f32[12,8,25,256]{3,2,1,0:T(8,128)S(1)} %reshape.562, f32[8,256]{1,0:T(8,128)S(1)} %tile.9), kind=kLoop, calls=%fused_computation.2 | loop fusion | flops 1152000 | bytes 2619392 | tf_op jit(solution)/shard_map/reduce_sum | solution.py:36
  21.8 1.2 %reshape.563 = bf16[12,25,2,2,64]{4,3,2,1,0:T(2,128)(2,1)S(1)} reshape(bf16[12,25,256]{2,1,0:T(8,128)(2,1)} %multiply_reduce_fusion.1) | data formatting | bytes 307200 | tf_op jit(solution)/shard_map/reshape | solution.py:42
  23.6 0.6 copy.227
  24.4 0.6 copy.226
  26.7 0.6 copy-done.2
  27.3 2.7 %fusion.49 = (bf16[1,12,8,25,25]{3,0,4,1,2:T(2,128)(2,1)S(1)}, bf16[1,12,8,25,25]{3,0,4,1,2:T(2,128)(2,1)}) fusion(f32[2,12,8,25,25]{3,0,4,1,2:T(2,128)S(1)} %bitcast.230), kind=kLoop, calls=%fused_computation.155 | loop fusion | bytes 480000 | tf_op jit(solution)/shard_map/slice | solution.py:30
  30.6 0.7 copy-done.3
  31.9 0.5 convolution_bitcast_fusion.1
  33.2 1.6 %pad_maximum_fusion.1 = f32[12,200,256]{2,1,0:T(8,128)} fusion(f32[12,200,128]{2,1,0:T(8,128)S(1)} %get-tuple-element.34, f32[12,200,128]{2,1,0:T(8,128)S(1)} %get-tuple-element.33), kind=kLoop, calls=%fused_computation.4 | loop fusion | flops 614400 | bytes 4915200 | tf_op jit(solution)/shard_map/concatenate | solution.py:18
  34.9 2.7 %reshape.567 = f32[12,8,25,256]{3,2,1,0:T(8,128)S(1)} reshape(f32[12,200,256]{2,1,0:T(8,128)} %pad_maximum_fusion.1) | data formatting | bytes 4915200 | tf_op jit(solution)/shard_map/reshape | solution.py:32
  37.6 1.1 %multiply_reduce_fusion = f32[12,25,256]{2,1,0:T(8,128)} fusion(f32[12,8,25,256]{3,2,1,0:T(8,128)S(1)} %reshape.567, f32[8,256]{1,0:T(8,128)S(1)} %tile.9), kind=kLoop, calls=%fused_computation.1 | loop fusion | flops 1152000 | bytes 2772992 | tf_op jit(solution)/shard_map/reduce_sum | solution.py:36
  39.0 1.6 %fusion.55 = bf16[12,25,32]{1,2,0:T(8,128)(2,1)S(1)} fusion(f32[12,25,256]{2,1,0:T(8,128)} %multiply_reduce_fusion, f32[256,32,1]{0,1,2:T(8,128)S(1)} %reshape.730), kind=kOutput, calls=%fused_computation.161 | convolution fusion | flops 14745600 | bytes 359168 | tf_op jit(solution)/shard_map/lpC,CD->lpD/dot_general | solution.py:90
  41.7 0.5 multiply_reduce_fusion.3
  42.7 0.6 copy.228
  43.5 0.6 copy.229
  46.8 0.5 collective-permute-start
  47.4 1.4 %fusion.54 = (f32[1,1,12,25,25]{4,1,3,2,0:T(1,128)S(1)}, f32[1,1,12,25,25]{4,1,3,2,0:T(1,128)S(1)}) fusion(f32[1,2,12,25,25]{4,1,3,2,0:T(2,128)} %param.27), kind=kLoop, calls=%fused_computation.160 | loop fusion | bytes 120000 | tf_op jit(solution)/shard_map/slice | solution.py:98
  48.9 0.6 fusion.18
  49.5 0.6 dynamic_slice.3
  50.1 0.7 fusion.45
  50.8 2.6 %collective-permute-start.1 = (f32[12,25,16]{1,2,0:T(8,128)S(1)}, f32[12,25,16]{1,2,0:T(8,128)S(1)}, u32[]{:S(2)}, u32[]{:S(2)}) collective-permute-start(f32[12,25,16]{1,2,0:T(8,128)S(1)} %add.191), channel_id=1, source_target_pairs={{0,2},{2,0},{1,3},{3,1},{4,6},{6,4},{5,7},{7,5},{8,10},{10,8},{9,1... | collective-permute-start | bytes 57608 | tf_op jit(solution)/shard_map/ppermute | solution.py:170
  54.7 2.1 %collective-permute-done.1 = f32[12,25,16]{1,2,0:T(8,128)S(1)} collective-permute-done((f32[12,25,16]{1,2,0:T(8,128)S(1)}, f32[12,25,16]{1,2,0:T(8,128)S(1)}, u32[]{:S(2)}, u32[]{:S(2)}) %collective-permute-start.1) | collective-permute-done | bytes 19232 | tf_op jit(solution)/shard_map/ppermute | solution.py:170
  59.8 1.0 %constant_dynamic-slice_fusion.1 = (f32[1,64,512]{1,0,2:T(1,128)S(1)}, f32[1,64,512]{1,0,2:T(1,128)S(1)}, f32[1,64,512]{1,0,2:T(1,128)S(1)}, f32[1,64,512]{1,0,2:T(1,128)S(1)}) fusion(f32[4,64,512]{1,0,2:T(4,128)S(1)} %reshape_reshape.6, s32[]{:T(128)S(6)} %select_n.229, s32[]{:T(128)S(6)} %select_n.227, s32[]{:T(128)S(6)} %select_n.235, pred[]{:T(512)S(6)} %and.156, ...), kind=kLoop, calls=%fused_computation.136 | loop fusion | flops 32768 | bytes 1048593 | tf_op jit(solution)/shard_map/jit(_take) | solution.py:201
  60.8 1.9 %collective-permute-start.2 = (bf16[64,512]{0,1:T(8,128)(2,1)S(1)}, bf16[64,512]{0,1:T(8,128)(2,1)S(1)}, u32[]{:S(2)}, u32[]{:S(2)}) collective-permute-start(bf16[64,512]{0,1:T(8,128)(2,1)S(1)} %bitcast_convert_fusion.1), channel_id=1, source_target_pairs={{0,4},{4,8},{8,12},{12,0},{1,5},{5,9},{9,13},{13,1},{2,6},{6,10},{... | collective-permute-start | bytes 196616 | tf_op jit(solution)/shard_map/ppermute | solution.py:202
  62.7 2.7 %collective-permute-start.3 = (bf16[64,512]{0,1:T(8,128)(2,1)S(1)}, bf16[64,512]{0,1:T(8,128)(2,1)S(1)}, u32[]{:S(2)}, u32[]{:S(2)}) collective-permute-start(bf16[64,512]{0,1:T(8,128)(2,1)S(1)} %bitcast_convert_fusion), channel_id=1, source_target_pairs={{0,8},{4,12},{8,0},{12,4},{1,9},{5,13},{9,1},{13,5},{2,10},{6,14},... | collective-permute-start | bytes 196616 | tf_op jit(solution)/shard_map/ppermute | solution.py:202
  65.4 1.7 %collective-permute-start.4 = (bf16[64,512]{0,1:T(8,128)(2,1)S(1)}, bf16[64,512]{0,1:T(8,128)(2,1)S(1)}, u32[]{:S(2)}, u32[]{:S(2)}) collective-permute-start(bf16[64,512]{0,1:T(8,128)(2,1)S(1)} %convert_element_type.165), channel_id=1, source_target_pairs={{0,12},{4,0},{8,4},{12,8},{1,13},{5,1},{9,5},{13,9},{2,14},{6,2},{... | collective-permute-start | bytes 196616 | tf_op jit(solution)/shard_map/ppermute | solution.py:202
  67.2 0.8 copy.215
  68.0 1.1 %collective-permute-done.2 = bf16[64,512]{0,1:T(8,128)(2,1)S(1)} collective-permute-done((bf16[64,512]{0,1:T(8,128)(2,1)S(1)}, bf16[64,512]{0,1:T(8,128)(2,1)S(1)}, u32[]{:S(2)}, u32[]{:S(2)}) %collective-permute-start.2) | collective-permute-done | bytes 65568 | tf_op jit(solution)/shard_map/ppermute | solution.py:202
  69.1 4.7 %collective-permute-done.3 = bf16[64,512]{0,1:T(8,128)(2,1)S(1)} collective-permute-done((bf16[64,512]{0,1:T(8,128)(2,1)S(1)}, bf16[64,512]{0,1:T(8,128)(2,1)S(1)}, u32[]{:S(2)}, u32[]{:S(2)}) %collective-permute-start.3) | collective-permute-done | bytes 65568 | tf_op jit(solution)/shard_map/ppermute | solution.py:202
  75.5 1.1 %collective-permute-done.5 = bf16[2,4,1024]{2,1,0:T(4,128)(2,1)S(1)} collective-permute-done((bf16[2,4,1024]{2,1,0:T(4,128)(2,1)S(1)}, bf16[2,4,1024]{2,1,0:T(4,128)(2,1)S(1)}, u32[]{:S(2)}, u32[]{:S(2)}) %collective-permute-start.5) | collective-permute-done | bytes 16416 | tf_op jit(solution)/shard_map/ppermute | solution.py:177
  76.6 1.7 %collective-permute-start.6 = (bf16[4,1024]{1,0:T(4,128)(2,1)S(1)}, bf16[4,1024]{1,0:T(4,128)(2,1)S(1)}, u32[]{:S(2)}, u32[]{:S(2)}) collective-permute-start(bf16[4,1024]{1,0:T(4,128)(2,1)S(1)} %fusion.36), channel_id=1, source_target_pairs={{0,2},{2,0},{1,3},{3,1},{4,6},{6,4},{5,7},{7,5},{8,10},{10,8},{9,1... | collective-permute-start | bytes 24584 | tf_op jit(solution)/shard_map/ppermute | solution.py:177
  78.3 2.1 %collective-permute-done.6 = bf16[4,1024]{1,0:T(4,128)(2,1)S(1)} collective-permute-done((bf16[4,1024]{1,0:T(4,128)(2,1)S(1)}, bf16[4,1024]{1,0:T(4,128)(2,1)S(1)}, u32[]{:S(2)}, u32[]{:S(2)}) %collective-permute-start.6) | collective-permute-done | bytes 8224 | tf_op jit(solution)/shard_map/ppermute | solution.py:177
  80.4 4.3 %collective-permute-start.7 = (bf16[1024]{0:T(1024)(128)(2,1)S(1)}, bf16[1024]{0:T(1024)(128)(2,1)S(1)}, u32[]{:S(2)}, u32[]{:S(2)}) collective-permute-start(bf16[1024]{0:T(1024)(128)(2,1)S(1)} %get-tuple-element.29), channel_id=1, source_target_pairs={{0,12},{4,0},{8,4},{12,8},{1,13},{5,1},{9,5},{13,9},{2,14},{6,2},{... | collective-permute-start | bytes 6152 | tf_op jit(solution)/shard_map/ppermute | solution.py:190
  85.5 0.6 collective-permute-done.7
  86.2 3.1 %collective-permute-done.8 = bf16[1024]{0:T(1024)(128)(2,1)S(1)} collective-permute-done((bf16[1024]{0:T(1024)(128)(2,1)S(1)}, bf16[1024]{0:T(1024)(128)(2,1)S(1)}, u32[]{:S(2)}, u32[]{:S(2)}) %collective-permute-start.8) | collective-permute-done | bytes 2080 | tf_op jit(solution)/shard_map/ppermute | solution.py:190
  89.3 1.3 %collective-permute-done.9 = bf16[1024]{0:T(1024)(128)(2,1)S(1)} collective-permute-done((bf16[1024]{0:T(1024)(128)(2,1)S(1)}, bf16[1024]{0:T(1024)(128)(2,1)S(1)}, u32[]{:S(2)}, u32[]{:S(2)}) %collective-permute-start.9) | collective-permute-done | bytes 2080 | tf_op jit(solution)/shard_map/ppermute | solution.py:190
  91.2 0.8 copy.222
  (149 shorter events, 18.2 us)
Async XLA Ops:
  0.0 9.7 %copy-start = (bf16[12,25,2,2,4,64]{5,4,3,2,1,0:T(4,128)(2,1)S(1)}, bf16[12,25,2,2,4,64]{5,4,3,2,1,0:T(4,128)(2,1)}, u32[]{:S(2)}) copy-start(bf16[12,25,2,2,4,64]{5,4,3,2,1,0:T(4,128)(2,1)} %param.18) | copy-start | bytes 1843204
  5.7 4.0 %copy-start.13 = (s32[64]{0:T(128)S(1)}, s32[64]{0:T(128)}, u32[]{:S(2)}) copy-start(s32[64]{0:T(128)} %param.20) | copy-start | bytes 772
  16.6 2.5 %copy-start.14 = (s32[16]{0:T(128)S(1)}, s32[16]{0:T(128)}, u32[]{:S(2)}) copy-start(s32[16]{0:T(128)} %param.22) | copy-start | bytes 196
  21.8 1.6 %copy-start.11 = (f32[2,25,2,12,2,12]{1,4,5,3,2,0:T(2,128)S(1)}, f32[2,25,2,12,2,12]{1,4,5,3,2,0:T(2,128)}, u32[]{:S(2)}) copy-start(f32[2,25,2,12,2,12]{1,4,5,3,2,0:T(2,128)} %param.25) | copy-start | bytes 345604
  25.6 1.7 %copy-start.2 = (f32[8,2,12,25,25]{4,1,3,2,0:T(2,128)S(1)}, f32[8,2,12,25,25]{4,1,3,2,0:T(2,128)}, u32[]{:S(2)}) copy-start(f32[8,2,12,25,25]{4,1,3,2,0:T(2,128)} %param.24) | copy-start | bytes 1440004
  30.0 1.3 %copy-start.3 = (bf16[1,12,8,25,25]{3,0,4,1,2:T(2,128)(2,1)S(1)}, bf16[1,12,8,25,25]{3,0,4,1,2:T(2,128)(2,1)}, u32[]{:S(2)}) copy-start(bf16[1,12,8,25,25]{3,0,4,1,2:T(2,128)(2,1)} %get-tuple-element.38) | copy-start | bytes 360004
  30.6 1.8 %copy-start.4 = (bf16[12,200,25]{1,2,0:T(8,128)(2,1)}, bf16[12,200,25]{1,2,0:T(8,128)(2,1)S(1)}, u32[]{:S(2)}) copy-start(bf16[12,200,25]{1,2,0:T(8,128)(2,1)S(1)} %squeeze.68) | copy-start | bytes 360004
  31.9 1.1 %copy-start.6 = (bf16[12,200,25]{1,2,0:T(8,128)(2,1)}, bf16[12,200,25]{1,2,0:T(8,128)(2,1)S(1)}, u32[]{:S(2)}) copy-start(bf16[12,200,25]{1,2,0:T(8,128)(2,1)S(1)} %squeeze.69) | copy-start | bytes 360004
  37.6 1.2 %copy-start.15 = (s32[16]{0:T(128)S(1)}, s32[16]{0:T(128)}, u32[]{:S(2)}) copy-start(s32[16]{0:T(128)} %param.21) | copy-start | bytes 196
  41.0 0.7 copy-start.16
  41.0 1.5 %copy-start.12 = (f32[2,25,2,12,2,12]{1,4,5,3,2,0:T(2,128)S(1)}, f32[2,25,2,12,2,12]{1,4,5,3,2,0:T(2,128)}, u32[]{:S(2)}) copy-start(f32[2,25,2,12,2,12]{1,4,5,3,2,0:T(2,128)} %param.26) | copy-start | bytes 345604
  43.5 1.5 %copy-start.5 = (bf16[12,200,25]{1,2,0:T(8,128)(2,1)S(1)}, bf16[12,200,25]{1,2,0:T(8,128)(2,1)}, u32[]{:S(2)}) copy-start(bf16[12,200,25]{1,2,0:T(8,128)(2,1)} %copy-done.4) | copy-start | bytes 360004
  44.1 1.1 %copy-start.7 = (bf16[12,200,25]{1,2,0:T(8,128)(2,1)S(1)}, bf16[12,200,25]{1,2,0:T(8,128)(2,1)}, u32[]{:S(2)}) copy-start(bf16[12,200,25]{1,2,0:T(8,128)(2,1)} %copy-done.6) | copy-start | bytes 360004
  46.0 2.7 %copy-start.8 = (f32[1,2,25,2,32,2,12]{4,5,6,3,2,1,0:T(2,128)S(1)}, f32[1,2,25,2,32,2,12]{4,5,6,3,2,1,0:T(2,128)}, u32[]{:S(2)}) copy-start(f32[1,2,25,2,32,2,12]{4,5,6,3,2,1,0:T(2,128)} %param.28) | copy-start | bytes 921604
  46.8 3.9 %collective-permute-start = (f32[12,25,16]{1,2,0:T(8,128)S(1)}, f32[12,25,16]{1,2,0:T(8,128)S(1)}, u32[]{:S(2)}, u32[]{:S(2)}) collective-permute-start(f32[12,25,16]{1,2,0:T(8,128)S(1)} %reduce_sum.49), channel_id=1, source_target_pairs={{0,1},{1,0},{2,3},{3,2},{4,5},{5,4},{6,7},{7,6},{8,9},{9,8},{10,11... | collective-permute-start | bytes 57608 | tf_op jit(solution)/shard_map/ppermute | solution.py:170
  48.8 0.7 copy-start.17
  50.8 6.0 %collective-permute-start.1 = (f32[12,25,16]{1,2,0:T(8,128)S(1)}, f32[12,25,16]{1,2,0:T(8,128)S(1)}, u32[]{:S(2)}, u32[]{:S(2)}) collective-permute-start(f32[12,25,16]{1,2,0:T(8,128)S(1)} %add.191), channel_id=1, source_target_pairs={{0,2},{2,0},{1,3},{3,1},{4,6},{6,4},{5,7},{7,5},{8,10},{10,8},{9,1... | collective-permute-start | bytes 57608 | tf_op jit(solution)/shard_map/ppermute | solution.py:170
  57.1 1.4 %copy-start.9 = (bf16[1,32,25,256]{3,1,2,0:T(8,128)(2,1)S(1)}, bf16[1,32,25,256]{3,1,2,0:T(8,128)(2,1)}, u32[]{:S(2)}) copy-start(bf16[1,32,25,256]{3,1,2,0:T(8,128)(2,1)} %param.30) | copy-start | bytes 1228804
  59.7 7.5 %copy-start.10 = (bf16[64,32,32]{0,2,1:T(8,128)(2,1)S(1)}, bf16[64,32,32]{0,2,1:T(8,128)(2,1)}, u32[]{:S(2)}) copy-start(bf16[64,32,32]{0,2,1:T(8,128)(2,1)} %param.31) | copy-start | bytes 393220
  60.8 8.4 %collective-permute-start.2 = (bf16[64,512]{0,1:T(8,128)(2,1)S(1)}, bf16[64,512]{0,1:T(8,128)(2,1)S(1)}, u32[]{:S(2)}, u32[]{:S(2)}) collective-permute-start(bf16[64,512]{0,1:T(8,128)(2,1)S(1)} %bitcast_convert_fusion.1), channel_id=1, source_target_pairs={{0,4},{4,8},{8,12},{12,0},{1,5},{5,9},{9,13},{13,1},{2,6},{6,10},{... | collective-permute-start | bytes 196616 | tf_op jit(solution)/shard_map/ppermute | solution.py:202
  62.7 11.1 %collective-permute-start.3 = (bf16[64,512]{0,1:T(8,128)(2,1)S(1)}, bf16[64,512]{0,1:T(8,128)(2,1)S(1)}, u32[]{:S(2)}, u32[]{:S(2)}) collective-permute-start(bf16[64,512]{0,1:T(8,128)(2,1)S(1)} %bitcast_convert_fusion), channel_id=1, source_target_pairs={{0,8},{4,12},{8,0},{12,4},{1,9},{5,13},{9,1},{13,5},{2,10},{6,14},... | collective-permute-start | bytes 196616 | tf_op jit(solution)/shard_map/ppermute | solution.py:202
  65.4 8.4 %collective-permute-start.4 = (bf16[64,512]{0,1:T(8,128)(2,1)S(1)}, bf16[64,512]{0,1:T(8,128)(2,1)S(1)}, u32[]{:S(2)}, u32[]{:S(2)}) collective-permute-start(bf16[64,512]{0,1:T(8,128)(2,1)S(1)} %convert_element_type.165), channel_id=1, source_target_pairs={{0,12},{4,0},{8,4},{12,8},{1,13},{5,1},{9,5},{13,9},{2,14},{6,2},{... | collective-permute-start | bytes 196616 | tf_op jit(solution)/shard_map/ppermute | solution.py:202
  75.3 1.2 %collective-permute-start.5 = (bf16[2,4,1024]{2,1,0:T(4,128)(2,1)S(1)}, bf16[2,4,1024]{2,1,0:T(4,128)(2,1)S(1)}, u32[]{:S(2)}, u32[]{:S(2)}) collective-permute-start(bf16[2,4,1024]{2,1,0:T(4,128)(2,1)S(1)} %fusion.32), channel_id=1, source_target_pairs={{0,1},{1,0},{2,3},{3,2},{4,5},{5,4},{6,7},{7,6},{8,9},{9,8},{10,11... | collective-permute-start | bytes 49160 | tf_op jit(solution)/shard_map/ppermute | solution.py:177
  75.4 16.6 %copy-start.1 = (bf16[12,25,2,2,4,64]{5,4,3,2,1,0:T(4,128)(2,1)S(1)}, bf16[12,25,2,2,4,64]{5,4,3,2,1,0:T(4,128)(2,1)}, u32[]{:S(2)}) copy-start(bf16[12,25,2,2,4,64]{5,4,3,2,1,0:T(4,128)(2,1)} %param.18) | copy-start | bytes 1843204
  76.6 3.7 %collective-permute-start.6 = (bf16[4,1024]{1,0:T(4,128)(2,1)S(1)}, bf16[4,1024]{1,0:T(4,128)(2,1)S(1)}, u32[]{:S(2)}, u32[]{:S(2)}) collective-permute-start(bf16[4,1024]{1,0:T(4,128)(2,1)S(1)} %fusion.36), channel_id=1, source_target_pairs={{0,2},{2,0},{1,3},{3,1},{4,6},{6,4},{5,7},{7,5},{8,10},{10,8},{9,1... | collective-permute-start | bytes 24584 | tf_op jit(solution)/shard_map/ppermute | solution.py:177
  80.4 5.7 %collective-permute-start.7 = (bf16[1024]{0:T(1024)(128)(2,1)S(1)}, bf16[1024]{0:T(1024)(128)(2,1)S(1)}, u32[]{:S(2)}, u32[]{:S(2)}) collective-permute-start(bf16[1024]{0:T(1024)(128)(2,1)S(1)} %get-tuple-element.29), channel_id=1, source_target_pairs={{0,12},{4,0},{8,4},{12,8},{1,13},{5,1},{9,5},{13,9},{2,14},{6,2},{... | collective-permute-start | bytes 6152 | tf_op jit(solution)/shard_map/ppermute | solution.py:190
  84.8 4.5 %collective-permute-start.8 = (bf16[1024]{0:T(1024)(128)(2,1)S(1)}, bf16[1024]{0:T(1024)(128)(2,1)S(1)}, u32[]{:S(2)}, u32[]{:S(2)}) collective-permute-start(bf16[1024]{0:T(1024)(128)(2,1)S(1)} %get-tuple-element.32), channel_id=1, source_target_pairs={{0,8},{4,12},{8,0},{12,4},{1,9},{5,13},{9,1},{13,5},{2,10},{6,14},... | collective-permute-start | bytes 6152 | tf_op jit(solution)/shard_map/ppermute | solution.py:190
  85.2 5.4 %collective-permute-start.9 = (bf16[1024]{0:T(1024)(128)(2,1)S(1)}, bf16[1024]{0:T(1024)(128)(2,1)S(1)}, u32[]{:S(2)}, u32[]{:S(2)}) collective-permute-start(bf16[1024]{0:T(1024)(128)(2,1)S(1)} %get-tuple-element.31), channel_id=1, source_target_pairs={{0,4},{4,8},{8,12},{12,0},{1,5},{5,9},{9,13},{13,1},{2,6},{6,10},{... | collective-permute-start | bytes 6152 | tf_op jit(solution)/shard_map/ppermute | solution.py:190

commit v3 on v2

--- a/solution.py
+++ b/solution.py
@@ -83,11 +83,9 @@
     parents = (leaf_parent[:, None] == jnp.arange(box_total, dtype=jnp.int32)[None, :]).astype(
         jnp.float32
     )
-    wide_ident = jnp.eye(channel, dtype=jnp.float32)
-    wide_parents = (wide_ident[:, None, :, None] * parents[None, :, None, :]).reshape(
-        channel * leaf_total, channel * box_total
-    )
-    boxes = jnp.einsum("lpC,CD->lpD", moved, wide_parents, precision=HI)
+    boxes = jnp.dot(moved.reshape(-1, leaf_total), parents, precision=HI).reshape(
+        degrees, orders, channel * box_total
+    )
     outer = move_expansion(boxes, box_octant, rotation, axial_two, LEAF_PREC)
     return outer.reshape(degrees, orders, channel, box_total).sum(-1)
 

time: 92.5 us -> 97.1 us (1.050)
  local copies, waits for them, and re-layouts: 39.2 us -> 43.4 us
    reshape x0 -> x2, local copies, waits for them, and re-layouts: none -> 4.39 us  [the longest x1 2.57 us: local_boxes(): jnp.dot(moved.reshape(-1, leaf_total), parents, precision=HI)]
where the time goes in v3:
time: 97.1 us; the launch traced here: 96.6 us
  local copies, waits for them, and re-layouts  43.4 us (45%)
  waiting for transfers between devices  16.2 us (17%)
  starting transfers between devices  15.7 us (16%)
  other arithmetic  11.3 us (12%)
  matrix products  8.22 us (8%)
  between operations  1.69 us (2%)
    slice x4, local copies, waits for them, and re-layouts, turn_select(): first = jnp.einsum('lQp,lpC->lQC', mats[0], vectors, precision=prec)  9.76 us
    reshape x4, local copies, waits for them, and re-layouts, turn_select(): complex_join(first, second, width // 2).reshape(degrees, 8, orders, width)  6.21 us
    ppermute x3, waiting for transfers between devices, shift_reduce_scatter(): piece = lax.ppermute(piece, axis, [(i, (i + step) % n) for i in range(n)])  6.04 us
    ppermute x3, starting transfers between devices, shift_reduce_scatter(): piece = lax.ppermute(piece, axis, [(i, (i + step) % n) for i in range(n)])  5.94 us
    ppermute x3, starting transfers between devices, shift_all_to_all(): piece = lax.ppermute(piece, axis, [(i, (i + step) % n) for i in range(n)])  5.03 us
    ppermute x3, waiting for transfers between devices, shift_all_to_all(): piece = lax.ppermute(piece, axis, [(i, (i + step) % n) for i in range(n)])  4.9 us
    concatenate x8, other arithmetic, complex_join(): return jnp.concatenate([real, imag], axis=-1)  3.47 us
    reduce_sum x4, other arithmetic, turn_select(): return jnp.sum(joined * column_mask[None, :, None, :], axis=1)  3.29 us
  transfers between devices with their start and end apart: 10, of which 8 were waited for; matrix products, arithmetic and copies ran while one was open for 6% of the time, Pallas kernels for 0%

profile of v3, /device:TPU:0, one launch (start us, length us, event | category | flops | bytes accessed | tf_op | source)
XLA Modules:
  0.0 96.6 jit_solution(1853813927455294408)
XLA Ops:
  0.0 5.7 %fusion.51 = (bf16[1,12,8,25,25]{4,0,3,1,2:T(2,128)(2,1)S(1)}, bf16[1,12,8,25,25]{4,0,3,1,2:T(2,128)(2,1)}) fusion(f32[2,12,8,25,25]{4,0,3,1,2:T(2,128)} %bitcast.224), kind=kLoop, calls=%fused_computation.155 | loop fusion | bytes 480000 | tf_op jit(solution)/shard_map/slice | solution.py:30
  5.7 2.8 %copy.181 = bf16[1,12,8,25,25]{3,2,4,1,0:T(8,128)(2,1)S(1)} copy(bf16[1,12,8,25,25]{4,0,3,1,2:T(2,128)(2,1)} %get-tuple-element.40) | data formatting | bytes 240000 | tf_op jit(solution)/shard_map/slice | solution.py:31
  10.2 0.6 copy.179
  10.8 1.2 %reshape.537 = bf16[12,25,256]{2,1,0:T(8,128)(2,1)S(1)} reshape(bf16[4800,16]{1,0:T(8,128)(2,1)S(1)} %copy.179) | data formatting | bytes 307200 | tf_op jit(solution)/shard_map/reshape | solution.py:80
  12.0 1.2 %copy.180 = bf16[1,12,8,25,25]{3,2,4,1,0:T(8,128)(2,1)S(1)} copy(bf16[1,12,8,25,25]{4,0,3,1,2:T(2,128)(2,1)S(1)} %get-tuple-element.39) | data formatting | bytes 240000 | tf_op jit(solution)/shard_map/slice | solution.py:30
  14.2 0.5 convolution_bitcast_fusion.3
  15.0 1.6 %pad_maximum_fusion = f32[12,200,256]{2,1,0:T(8,128)} fusion(f32[12,200,128]{2,1,0:T(8,128)S(1)} %get-tuple-element.36, f32[12,200,128]{2,1,0:T(8,128)S(1)} %get-tuple-element.35), kind=kLoop, calls=%fused_computation.3 | loop fusion | flops 614400 | bytes 4915200 | tf_op jit(solution)/shard_map/concatenate | solution.py:18
  16.6 2.5 %reshape.538 = f32[12,8,25,256]{3,2,1,0:T(8,128)S(1)} reshape(f32[12,200,256]{2,1,0:T(8,128)} %pad_maximum_fusion) | data formatting | bytes 4915200 | tf_op jit(solution)/shard_map/reshape | solution.py:32
  19.2 0.6 tile.8
  19.8 0.9 tile.9
  20.7 1.1 %multiply_reduce_fusion.1 = bf16[12,25,256]{2,1,0:T(8,128)(2,1)} fusion(f32[12,8,25,256]{3,2,1,0:T(8,128)S(1)} %reshape.538, f32[8,256]{1,0:T(8,128)S(1)} %tile.9), kind=kLoop, calls=%fused_computation.2 | loop fusion | flops 1152000 | bytes 2619392 | tf_op jit(solution)/shard_map/reduce_sum | solution.py:36
  21.8 1.2 %reshape.539 = bf16[12,25,2,2,64]{4,3,2,1,0:T(2,128)(2,1)S(1)} reshape(bf16[12,25,256]{2,1,0:T(8,128)(2,1)} %multiply_reduce_fusion.1) | data formatting | bytes 307200 | tf_op jit(solution)/shard_map/reshape | solution.py:42
  23.6 0.6 copy.231
  24.4 0.6 copy.230
  26.7 0.6 copy-done.2
  27.3 2.7 %fusion.50 = (bf16[1,12,8,25,25]{3,0,4,1,2:T(2,128)(2,1)S(1)}, bf16[1,12,8,25,25]{3,0,4,1,2:T(2,128)(2,1)}) fusion(f32[2,12,8,25,25]{3,0,4,1,2:T(2,128)S(1)} %bitcast.225), kind=kLoop, calls=%fused_computation.154 | loop fusion | bytes 480000 | tf_op jit(solution)/shard_map/slice | solution.py:30
  30.6 0.7 copy-done.3
  32.4 0.5 multiply_bitcast_fusion
  33.2 1.6 %pad_maximum_fusion.1 = f32[12,200,256]{2,1,0:T(8,128)} fusion(f32[12,200,128]{2,1,0:T(8,128)S(1)} %get-tuple-element.34, f32[12,200,128]{2,1,0:T(8,128)S(1)} %get-tuple-element.33), kind=kLoop, calls=%fused_computation.4 | loop fusion | flops 614400 | bytes 4915200 | tf_op jit(solution)/shard_map/concatenate | solution.py:18
  34.8 2.7 %reshape.543 = f32[12,8,25,256]{3,2,1,0:T(8,128)S(1)} reshape(f32[12,200,256]{2,1,0:T(8,128)} %pad_maximum_fusion.1) | data formatting | bytes 4915200 | tf_op jit(solution)/shard_map/reshape | solution.py:32
  37.5 1.1 %multiply_reduce_fusion = f32[12,25,256]{2,1,0:T(8,128)} fusion(f32[12,8,25,256]{3,2,1,0:T(8,128)S(1)} %reshape.543, f32[8,256]{1,0:T(8,128)S(1)} %tile.9), kind=kLoop, calls=%fused_computation.1 | loop fusion | flops 1152000 | bytes 2772992 | tf_op jit(solution)/shard_map/reduce_sum | solution.py:36
  38.7 1.8 %reshape.544 = f32[4800,16]{1,0:T(8,128)S(1)} reshape(f32[12,25,256]{2,1,0:T(8,128)} %multiply_reduce_fusion) | data formatting | bytes 614400 | tf_op jit(solution)/shard_map/reshape | solution.py:86
  40.5 1.9 %fusion.39 = bf16[4800,2]{1,0:T(8,128)(2,1)} fusion(f32[4800,16]{1,0:T(8,128)S(1)} %reshape.544, s32[16]{0:T(128)S(1)} %copy-done.15), kind=kOutput, calls=%fused_computation.123 | convolution fusion | flops 921632 | bytes 326464 | tf_op jit(solution)/shard_map/dot_general | solution.py:86
  42.4 2.6 %reshape.545 = bf16[12,25,32]{2,1,0:T(8,128)(2,1)S(1)} reshape(bf16[4800,2]{1,0:T(8,128)(2,1)} %fusion.39) | data formatting | bytes 38400 | tf_op jit(solution)/shard_map/reshape | solution.py:86
  47.3 0.6 copy.232
  48.1 0.6 copy.233
  51.4 0.5 collective-permute-start
  52.0 1.4 %fusion.55 = (f32[1,1,12,25,25]{4,1,3,2,0:T(1,128)S(1)}, f32[1,1,12,25,25]{4,1,3,2,0:T(1,128)S(1)}) fusion(f32[1,2,12,25,25]{4,1,3,2,0:T(2,128)} %param.27), kind=kLoop, calls=%fused_computation.159 | loop fusion | bytes 120000 | tf_op jit(solution)/shard_map/slice | solution.py:96
  53.5 0.6 fusion.18
  54.1 0.6 dynamic_slice.3
  54.7 0.7 fusion.46
  55.4 2.6 %collective-permute-start.1 = (f32[12,25,16]{1,2,0:T(8,128)S(1)}, f32[12,25,16]{1,2,0:T(8,128)S(1)}, u32[]{:S(2)}, u32[]{:S(2)}) collective-permute-start(f32[12,25,16]{1,2,0:T(8,128)S(1)} %add.191), channel_id=1, source_target_pairs={{0,2},{2,0},{1,3},{3,1},{4,6},{6,4},{5,7},{7,5},{8,10},{10,8},{9,1... | collective-permute-start | bytes 57608 | tf_op jit(solution)/shard_map/ppermute | solution.py:168
  59.3 2.1 %collective-permute-done.1 = f32[12,25,16]{1,2,0:T(8,128)S(1)} collective-permute-done((f32[12,25,16]{1,2,0:T(8,128)S(1)}, f32[12,25,16]{1,2,0:T(8,128)S(1)}, u32[]{:S(2)}, u32[]{:S(2)}) %collective-permute-start.1) | collective-permute-done | bytes 19232 | tf_op jit(solution)/shard_map/ppermute | solution.py:168
  64.4 1.0 %constant_dynamic-slice_fusion.1 = (f32[1,64,512]{1,0,2:T(1,128)S(1)}, f32[1,64,512]{1,0,2:T(1,128)S(1)}, f32[1,64,512]{1,0,2:T(1,128)S(1)}, f32[1,64,512]{1,0,2:T(1,128)S(1)}) fusion(f32[4,64,512]{1,0,2:T(4,128)S(1)} %reshape_reshape.6, s32[]{:T(128)S(6)} %select_n.229, s32[]{:T(128)S(6)} %select_n.227, s32[]{:T(128)S(6)} %select_n.235, pred[]{:T(512)S(6)} %and.156, ...), kind=kLoop, calls=%fused_computation.136 | loop fusion | flops 32768 | bytes 1048593 | tf_op jit(solution)/shard_map/jit(_take) | solution.py:199
  65.4 1.9 %collective-permute-start.2 = (bf16[64,512]{0,1:T(8,128)(2,1)S(1)}, bf16[64,512]{0,1:T(8,128)(2,1)S(1)}, u32[]{:S(2)}, u32[]{:S(2)}) collective-permute-start(bf16[64,512]{0,1:T(8,128)(2,1)S(1)} %bitcast_convert_fusion.1), channel_id=1, source_target_pairs={{0,4},{4,8},{8,12},{12,0},{1,5},{5,9},{9,13},{13,1},{2,6},{6,10},{... | collective-permute-start | bytes 196616 | tf_op jit(solution)/shard_map/ppermute | solution.py:200
  67.3 2.7 %collective-permute-start.3 = (bf16[64,512]{0,1:T(8,128)(2,1)S(1)}, bf16[64,512]{0,1:T(8,128)(2,1)S(1)}, u32[]{:S(2)}, u32[]{:S(2)}) collective-permute-start(bf16[64,512]{0,1:T(8,128)(2,1)S(1)} %bitcast_convert_fusion), channel_id=1, source_target_pairs={{0,8},{4,12},{8,0},{12,4},{1,9},{5,13},{9,1},{13,5},{2,10},{6,14},... | collective-permute-start | bytes 196616 | tf_op jit(solution)/shard_map/ppermute | solution.py:200
  70.0 1.4 %collective-permute-start.4 = (bf16[64,512]{0,1:T(8,128)(2,1)S(1)}, bf16[64,512]{0,1:T(8,128)(2,1)S(1)}, u32[]{:S(2)}, u32[]{:S(2)}) collective-permute-start(bf16[64,512]{0,1:T(8,128)(2,1)S(1)} %convert_element_type.150), channel_id=1, source_target_pairs={{0,12},{4,0},{8,4},{12,8},{1,13},{5,1},{9,5},{13,9},{2,14},{6,2},{... | collective-permute-start | bytes 196616 | tf_op jit(solution)/shard_map/ppermute | solution.py:200
  71.6 0.8 copy.217
  72.4 1.4 %collective-permute-done.2 = bf16[64,512]{0,1:T(8,128)(2,1)S(1)} collective-permute-done((bf16[64,512]{0,1:T(8,128)(2,1)S(1)}, bf16[64,512]{0,1:T(8,128)(2,1)S(1)}, u32[]{:S(2)}, u32[]{:S(2)}) %collective-permute-start.2) | collective-permute-done | bytes 65568 | tf_op jit(solution)/shard_map/ppermute | solution.py:200
  73.8 4.6 %collective-permute-done.3 = bf16[64,512]{0,1:T(8,128)(2,1)S(1)} collective-permute-done((bf16[64,512]{0,1:T(8,128)(2,1)S(1)}, bf16[64,512]{0,1:T(8,128)(2,1)S(1)}, u32[]{:S(2)}, u32[]{:S(2)}) %collective-permute-start.3) | collective-permute-done | bytes 65568 | tf_op jit(solution)/shard_map/ppermute | solution.py:200
  80.1 1.1 %collective-permute-done.5 = bf16[2,4,1024]{2,1,0:T(4,128)(2,1)S(1)} collective-permute-done((bf16[2,4,1024]{2,1,0:T(4,128)(2,1)S(1)}, bf16[2,4,1024]{2,1,0:T(4,128)(2,1)S(1)}, u32[]{:S(2)}, u32[]{:S(2)}) %collective-permute-start.5) | collective-permute-done | bytes 16416 | tf_op jit(solution)/shard_map/ppermute | solution.py:175
  81.2 1.6 %collective-permute-start.6 = (bf16[4,1024]{1,0:T(4,128)(2,1)S(1)}, bf16[4,1024]{1,0:T(4,128)(2,1)S(1)}, u32[]{:S(2)}, u32[]{:S(2)}) collective-permute-start(bf16[4,1024]{1,0:T(4,128)(2,1)S(1)} %fusion.36), channel_id=1, source_target_pairs={{0,2},{2,0},{1,3},{3,1},{4,6},{6,4},{5,7},{7,5},{8,10},{10,8},{9,1... | collective-permute-start | bytes 24584 | tf_op jit(solution)/shard_map/ppermute | solution.py:175
  82.8 2.1 %collective-permute-done.6 = bf16[4,1024]{1,0:T(4,128)(2,1)S(1)} collective-permute-done((bf16[4,1024]{1,0:T(4,128)(2,1)S(1)}, bf16[4,1024]{1,0:T(4,128)(2,1)S(1)}, u32[]{:S(2)}, u32[]{:S(2)}) %collective-permute-start.6) | collective-permute-done | bytes 8224 | tf_op jit(solution)/shard_map/ppermute | solution.py:175
  85.0 4.4 %collective-permute-start.7 = (bf16[1024]{0:T(1024)(128)(2,1)S(1)}, bf16[1024]{0:T(1024)(128)(2,1)S(1)}, u32[]{:S(2)}, u32[]{:S(2)}) collective-permute-start(bf16[1024]{0:T(1024)(128)(2,1)S(1)} %get-tuple-element.29), channel_id=1, source_target_pairs={{0,12},{4,0},{8,4},{12,8},{1,13},{5,1},{9,5},{13,9},{2,14},{6,2},{... | collective-permute-start | bytes 6152 | tf_op jit(solution)/shard_map/ppermute | solution.py:188
  90.1 0.6 collective-permute-done.7
  90.8 3.1 %collective-permute-done.8 = bf16[1024]{0:T(1024)(128)(2,1)S(1)} collective-permute-done((bf16[1024]{0:T(1024)(128)(2,1)S(1)}, bf16[1024]{0:T(1024)(128)(2,1)S(1)}, u32[]{:S(2)}, u32[]{:S(2)}) %collective-permute-start.8) | collective-permute-done | bytes 2080 | tf_op jit(solution)/shard_map/ppermute | solution.py:188
  93.9 1.2 %collective-permute-done.9 = bf16[1024]{0:T(1024)(128)(2,1)S(1)} collective-permute-done((bf16[1024]{0:T(1024)(128)(2,1)S(1)}, bf16[1024]{0:T(1024)(128)(2,1)S(1)}, u32[]{:S(2)}, u32[]{:S(2)}) %collective-permute-start.9) | collective-permute-done | bytes 2080 | tf_op jit(solution)/shard_map/ppermute | solution.py:188
  95.8 0.8 copy.224
  (147 shorter events, 19.2 us)
Async XLA Ops:
  0.0 9.7 %copy-start = (bf16[12,25,2,2,4,64]{5,4,3,2,1,0:T(4,128)(2,1)S(1)}, bf16[12,25,2,2,4,64]{5,4,3,2,1,0:T(4,128)(2,1)}, u32[]{:S(2)}) copy-start(bf16[12,25,2,2,4,64]{5,4,3,2,1,0:T(4,128)(2,1)} %param.18) | copy-start | bytes 1843204
  5.7 4.0 %copy-start.13 = (s32[64]{0:T(128)S(1)}, s32[64]{0:T(128)}, u32[]{:S(2)}) copy-start(s32[64]{0:T(128)} %param.20) | copy-start | bytes 772
  16.6 2.5 %copy-start.14 = (s32[16]{0:T(128)S(1)}, s32[16]{0:T(128)}, u32[]{:S(2)}) copy-start(s32[16]{0:T(128)} %param.22) | copy-start | bytes 196
  21.8 1.6 %copy-start.11 = (f32[2,25,2,12,2,12]{1,4,5,3,2,0:T(2,128)S(1)}, f32[2,25,2,12,2,12]{1,4,5,3,2,0:T(2,128)}, u32[]{:S(2)}) copy-start(f32[2,25,2,12,2,12]{1,4,5,3,2,0:T(2,128)} %param.25) | copy-start | bytes 345604
  25.6 1.7 %copy-start.2 = (f32[8,2,12,25,25]{4,1,3,2,0:T(2,128)S(1)}, f32[8,2,12,25,25]{4,1,3,2,0:T(2,128)}, u32[]{:S(2)}) copy-start(f32[8,2,12,25,25]{4,1,3,2,0:T(2,128)} %param.24) | copy-start | bytes 1440004
  30.0 1.3 %copy-start.3 = (bf16[1,12,8,25,25]{3,0,4,1,2:T(2,128)(2,1)S(1)}, bf16[1,12,8,25,25]{3,0,4,1,2:T(2,128)(2,1)}, u32[]{:S(2)}) copy-start(bf16[1,12,8,25,25]{3,0,4,1,2:T(2,128)(2,1)} %get-tuple-element.38) | copy-start | bytes 360004
  30.6 1.8 %copy-start.4 = (bf16[12,200,25]{1,2,0:T(8,128)(2,1)}, bf16[12,200,25]{1,2,0:T(8,128)(2,1)S(1)}, u32[]{:S(2)}) copy-start(bf16[12,200,25]{1,2,0:T(8,128)(2,1)S(1)} %squeeze.68) | copy-start | bytes 360004
  31.9 1.1 %copy-start.6 = (bf16[12,200,25]{1,2,0:T(8,128)(2,1)}, bf16[12,200,25]{1,2,0:T(8,128)(2,1)S(1)}, u32[]{:S(2)}) copy-start(bf16[12,200,25]{1,2,0:T(8,128)(2,1)S(1)} %squeeze.69) | copy-start | bytes 360004
  38.7 1.8 %copy-start.15 = (s32[16]{0:T(128)S(1)}, s32[16]{0:T(128)}, u32[]{:S(2)}) copy-start(s32[16]{0:T(128)} %param.21) | copy-start | bytes 196
  45.6 0.7 copy-start.16
  45.6 1.5 %copy-start.12 = (f32[2,25,2,12,2,12]{1,4,5,3,2,0:T(2,128)S(1)}, f32[2,25,2,12,2,12]{1,4,5,3,2,0:T(2,128)}, u32[]{:S(2)}) copy-start(f32[2,25,2,12,2,12]{1,4,5,3,2,0:T(2,128)} %param.26) | copy-start | bytes 345604
  48.1 1.5 %copy-start.5 = (bf16[12,200,25]{1,2,0:T(8,128)(2,1)S(1)}, bf16[12,200,25]{1,2,0:T(8,128)(2,1)}, u32[]{:S(2)}) copy-start(bf16[12,200,25]{1,2,0:T(8,128)(2,1)} %copy-done.4) | copy-start | bytes 360004
  48.7 1.1 %copy-start.7 = (bf16[12,200,25]{1,2,0:T(8,128)(2,1)S(1)}, bf16[12,200,25]{1,2,0:T(8,128)(2,1)}, u32[]{:S(2)}) copy-start(bf16[12,200,25]{1,2,0:T(8,128)(2,1)} %copy-done.6) | copy-start | bytes 360004
  50.6 2.7 %copy-start.8 = (f32[1,2,25,2,32,2,12]{4,5,6,3,2,1,0:T(2,128)S(1)}, f32[1,2,25,2,32,2,12]{4,5,6,3,2,1,0:T(2,128)}, u32[]{:S(2)}) copy-start(f32[1,2,25,2,32,2,12]{4,5,6,3,2,1,0:T(2,128)} %param.28) | copy-start | bytes 921604
  51.4 3.9 %collective-permute-start = (f32[12,25,16]{1,2,0:T(8,128)S(1)}, f32[12,25,16]{1,2,0:T(8,128)S(1)}, u32[]{:S(2)}, u32[]{:S(2)}) collective-permute-start(f32[12,25,16]{1,2,0:T(8,128)S(1)} %reduce_sum.49), channel_id=1, source_target_pairs={{0,1},{1,0},{2,3},{3,2},{4,5},{5,4},{6,7},{7,6},{8,9},{9,8},{10,11... | collective-permute-start | bytes 57608 | tf_op jit(solution)/shard_map/ppermute | solution.py:168
  53.4 0.7 copy-start.17
  55.4 6.0 %collective-permute-start.1 = (f32[12,25,16]{1,2,0:T(8,128)S(1)}, f32[12,25,16]{1,2,0:T(8,128)S(1)}, u32[]{:S(2)}, u32[]{:S(2)}) collective-permute-start(f32[12,25,16]{1,2,0:T(8,128)S(1)} %add.191), channel_id=1, source_target_pairs={{0,2},{2,0},{1,3},{3,1},{4,6},{6,4},{5,7},{7,5},{8,10},{10,8},{9,1... | collective-permute-start | bytes 57608 | tf_op jit(solution)/shard_map/ppermute | solution.py:168
  61.7 1.4 %copy-start.9 = (bf16[1,32,25,256]{3,1,2,0:T(8,128)(2,1)S(1)}, bf16[1,32,25,256]{3,1,2,0:T(8,128)(2,1)}, u32[]{:S(2)}) copy-start(bf16[1,32,25,256]{3,1,2,0:T(8,128)(2,1)} %param.30) | copy-start | bytes 1228804
  64.4 7.2 %copy-start.10 = (bf16[64,32,32]{0,2,1:T(8,128)(2,1)S(1)}, bf16[64,32,32]{0,2,1:T(8,128)(2,1)}, u32[]{:S(2)}) copy-start(bf16[64,32,32]{0,2,1:T(8,128)(2,1)} %param.31) | copy-start | bytes 393220
  65.4 8.4 %collective-permute-start.2 = (bf16[64,512]{0,1:T(8,128)(2,1)S(1)}, bf16[64,512]{0,1:T(8,128)(2,1)S(1)}, u32[]{:S(2)}, u32[]{:S(2)}) collective-permute-start(bf16[64,512]{0,1:T(8,128)(2,1)S(1)} %bitcast_convert_fusion.1), channel_id=1, source_target_pairs={{0,4},{4,8},{8,12},{12,0},{1,5},{5,9},{9,13},{13,1},{2,6},{6,10},{... | collective-permute-start | bytes 196616 | tf_op jit(solution)/shard_map/ppermute | solution.py:200
  67.3 11.1 %collective-permute-start.3 = (bf16[64,512]{0,1:T(8,128)(2,1)S(1)}, bf16[64,512]{0,1:T(8,128)(2,1)S(1)}, u32[]{:S(2)}, u32[]{:S(2)}) collective-permute-start(bf16[64,512]{0,1:T(8,128)(2,1)S(1)} %bitcast_convert_fusion), channel_id=1, source_target_pairs={{0,8},{4,12},{8,0},{12,4},{1,9},{5,13},{9,1},{13,5},{2,10},{6,14},... | collective-permute-start | bytes 196616 | tf_op jit(solution)/shard_map/ppermute | solution.py:200
  70.0 8.4 %collective-permute-start.4 = (bf16[64,512]{0,1:T(8,128)(2,1)S(1)}, bf16[64,512]{0,1:T(8,128)(2,1)S(1)}, u32[]{:S(2)}, u32[]{:S(2)}) collective-permute-start(bf16[64,512]{0,1:T(8,128)(2,1)S(1)} %convert_element_type.150), channel_id=1, source_target_pairs={{0,12},{4,0},{8,4},{12,8},{1,13},{5,1},{9,5},{13,9},{2,14},{6,2},{... | collective-permute-start | bytes 196616 | tf_op jit(solution)/shard_map/ppermute | solution.py:200
  79.9 1.2 %collective-permute-start.5 = (bf16[2,4,1024]{2,1,0:T(4,128)(2,1)S(1)}, bf16[2,4,1024]{2,1,0:T(4,128)(2,1)S(1)}, u32[]{:S(2)}, u32[]{:S(2)}) collective-permute-start(bf16[2,4,1024]{2,1,0:T(4,128)(2,1)S(1)} %fusion.32), channel_id=1, source_target_pairs={{0,1},{1,0},{2,3},{3,2},{4,5},{5,4},{6,7},{7,6},{8,9},{9,8},{10,11... | collective-permute-start | bytes 49160 | tf_op jit(solution)/shard_map/ppermute | solution.py:175
  80.0 16.6 %copy-start.1 = (bf16[12,25,2,2,4,64]{5,4,3,2,1,0:T(4,128)(2,1)S(1)}, bf16[12,25,2,2,4,64]{5,4,3,2,1,0:T(4,128)(2,1)}, u32[]{:S(2)}) copy-start(bf16[12,25,2,2,4,64]{5,4,3,2,1,0:T(4,128)(2,1)} %param.18) | copy-start | bytes 1843204
  81.2 3.7 %collective-permute-start.6 = (bf16[4,1024]{1,0:T(4,128)(2,1)S(1)}, bf16[4,1024]{1,0:T(4,128)(2,1)S(1)}, u32[]{:S(2)}, u32[]{:S(2)}) collective-permute-start(bf16[4,1024]{1,0:T(4,128)(2,1)S(1)} %fusion.36), channel_id=1, source_target_pairs={{0,2},{2,0},{1,3},{3,1},{4,6},{6,4},{5,7},{7,5},{8,10},{10,8},{9,1... | collective-permute-start | bytes 24584 | tf_op jit(solution)/shard_map/ppermute | solution.py:175
  85.0 5.7 %collective-permute-start.7 = (bf16[1024]{0:T(1024)(128)(2,1)S(1)}, bf16[1024]{0:T(1024)(128)(2,1)S(1)}, u32[]{:S(2)}, u32[]{:S(2)}) collective-permute-start(bf16[1024]{0:T(1024)(128)(2,1)S(1)} %get-tuple-element.29), channel_id=1, source_target_pairs={{0,12},{4,0},{8,4},{12,8},{1,13},{5,1},{9,5},{13,9},{2,14},{6,2},{... | collective-permute-start | bytes 6152 | tf_op jit(solution)/shard_map/ppermute | solution.py:188
  89.4 4.5 %collective-permute-start.8 = (bf16[1024]{0:T(1024)(128)(2,1)S(1)}, bf16[1024]{0:T(1024)(128)(2,1)S(1)}, u32[]{:S(2)}, u32[]{:S(2)}) collective-permute-start(bf16[1024]{0:T(1024)(128)(2,1)S(1)} %get-tuple-element.32), channel_id=1, source_target_pairs={{0,8},{4,12},{8,0},{12,4},{1,9},{5,13},{9,1},{13,5},{2,10},{6,14},... | collective-permute-start | bytes 6152 | tf_op jit(solution)/shard_map/ppermute | solution.py:188
  89.8 5.4 %collective-permute-start.9 = (bf16[1024]{0:T(1024)(128)(2,1)S(1)}, bf16[1024]{0:T(1024)(128)(2,1)S(1)}, u32[]{:S(2)}, u32[]{:S(2)}) collective-permute-start(bf16[1024]{0:T(1024)(128)(2,1)S(1)} %get-tuple-element.31), channel_id=1, source_target_pairs={{0,4},{4,8},{8,12},{12,0},{1,5},{5,9},{9,13},{13,1},{2,6},{6,10},{... | collective-permute-start | bytes 6152 | tf_op jit(solution)/shard_map/ppermute | solution.py:188

commit v4 on v2

--- a/solution.py
+++ b/solution.py
@@ -88,7 +88,7 @@
         channel * leaf_total, channel * box_total
     )
     boxes = jnp.einsum("lpC,CD->lpD", moved, wide_parents, precision=HI)
-    outer = move_expansion(boxes, box_octant, rotation, axial_two, LEAF_PREC)
+    outer = move_expansion(boxes, box_octant, rotation, axial_two, HI)
     return outer.reshape(degrees, orders, channel, box_total).sum(-1)
 
 

time: 92.5 us -> 98.6 us (1.066)
  local copies, waits for them, and re-layouts: 39.2 us -> 43.3 us
  matrix products: 7.76 us -> 9.6 us
    dot_general x4, matrix products: 1.43 us -> 2.7 us  [turn_select(): first = jnp.einsum('lQp,lpC->lQC', mats[0], vectors, precision=prec)]
    squeeze x2, local copies, waits for them, and re-layouts: 0.91 us -> 2.06 us  [turn_select(): second = sign * jnp.einsum('lQp,lpC->lQC', mats[1], vectors, precision=prec)]
    slice x2, local copies, waits for them, and re-layouts: 2.93 us -> 3.96 us  [turn_select(): second = sign * jnp.einsum('lQp,lpC->lQC', mats[1], vectors, precision=prec)]
    unnamed x37 -> x39, local copies, waits for them, and re-layouts: 2.23 us -> 2.4 us
where the time goes in v4:
time: 98.6 us; the launch traced here: 97.9 us
  local copies, waits for them, and re-layouts  43.3 us (44%)
  waiting for transfers between devices  16.2 us (16%)
  starting transfers between devices  15.7 us (16%)
  other arithmetic  11.4 us (12%)
  matrix products  9.6 us (10%)
  between operations  1.67 us (2%)
    slice x4, local copies, waits for them, and re-layouts, turn_select(): first = jnp.einsum('lQp,lpC->lQC', mats[0], vectors, precision=prec)  9.79 us
    reshape x4, local copies, waits for them, and re-layouts, turn_select(): complex_join(first, second, width // 2).reshape(degrees, 8, orders, width)  6.21 us
    ppermute x3, waiting for transfers between devices, shift_reduce_scatter(): piece = lax.ppermute(piece, axis, [(i, (i + step) % n) for i in range(n)])  6.05 us
    ppermute x3, starting transfers between devices, shift_reduce_scatter(): piece = lax.ppermute(piece, axis, [(i, (i + step) % n) for i in range(n)])  5.96 us
    ppermute x3, starting transfers between devices, shift_all_to_all(): piece = lax.ppermute(piece, axis, [(i, (i + step) % n) for i in range(n)])  5.03 us
    ppermute x3, waiting for transfers between devices, shift_all_to_all(): piece = lax.ppermute(piece, axis, [(i, (i + step) % n) for i in range(n)])  4.9 us
    slice x2, local copies, waits for them, and re-layouts, turn_select(): second = sign * jnp.einsum('lQp,lpC->lQC', mats[1], vectors, precision=prec)  3.96 us
    concatenate x8, other arithmetic, complex_join(): return jnp.concatenate([real, imag], axis=-1)  3.46 us
  transfers between devices with their start and end apart: 10, of which 8 were waited for; matrix products, arithmetic and copies ran while one was open for 6% of the time, Pallas kernels for 0%

profile of v4, /device:TPU:0, one launch (start us, length us, event | category | flops | bytes accessed | tf_op | source)
XLA Modules:
  0.0 97.9 jit_solution(27678616824977301)
XLA Ops:
  0.0 5.7 %fusion.50 = (f32[1,12,8,25,25]{4,0,3,1,2:T(1,128)S(1)}, f32[1,12,8,25,25]{4,0,3,1,2:T(1,128)}) fusion(f32[2,12,8,25,25]{4,0,3,1,2:T(2,128)} %bitcast.229), kind=kLoop, calls=%fused_computation.156 | loop fusion | bytes 960000 | tf_op jit(solution)/shard_map/slice | solution.py:30
  5.7 3.9 %copy.180 = f32[1,12,8,25,25]{3,2,4,1,0:T(8,128)} copy(f32[1,12,8,25,25]{4,0,3,1,2:T(1,128)} %get-tuple-element.40) | data formatting | bytes 480000 | tf_op jit(solution)/shard_map/slice | solution.py:31
  9.6 1.7 %squeeze.65 = f32[12,200,25]{1,2,0:T(8,128)S(1)} reshape(f32[1,12,8,25,25]{3,2,4,1,0:T(8,128)} %copy.180) | data formatting | bytes 480000 | tf_op jit(solution)/shard_map/squeeze | solution.py:31
  12.5 0.6 copy.178
  13.1 1.2 %reshape.561 = bf16[12,25,256]{2,1,0:T(8,128)(2,1)S(1)} reshape(bf16[4800,16]{1,0:T(8,128)(2,1)S(1)} %copy.178) | data formatting | bytes 307200 | tf_op jit(solution)/shard_map/reshape | solution.py:80
  14.2 1.1 %copy.179 = f32[1,12,8,25,25]{3,2,4,1,0:T(8,128)S(1)} copy(f32[1,12,8,25,25]{4,0,3,1,2:T(1,128)S(1)} %get-tuple-element.39) | data formatting | bytes 480000 | tf_op jit(solution)/shard_map/slice | solution.py:30
  15.8 0.5 convolution_bitcast_fusion.2
  16.3 0.5 convolution_bitcast_fusion.3
  17.1 1.6 %pad_maximum_fusion = f32[12,200,256]{2,1,0:T(8,128)} fusion(f32[12,200,128]{2,1,0:T(8,128)S(1)} %get-tuple-element.36, f32[12,200,128]{2,1,0:T(8,128)S(1)} %get-tuple-element.35), kind=kLoop, calls=%fused_computation.3 | loop fusion | flops 614400 | bytes 4915200 | tf_op jit(solution)/shard_map/concatenate | solution.py:18
  18.7 2.5 %reshape.562 = f32[12,8,25,256]{3,2,1,0:T(8,128)S(1)} reshape(f32[12,200,256]{2,1,0:T(8,128)} %pad_maximum_fusion) | data formatting | bytes 4915200 | tf_op jit(solution)/shard_map/reshape | solution.py:32
  21.2 0.6 tile.8
  21.9 0.9 tile.9
  22.8 1.1 %multiply_reduce_fusion.1 = bf16[12,25,256]{2,1,0:T(8,128)(2,1)} fusion(f32[12,8,25,256]{3,2,1,0:T(8,128)S(1)} %reshape.562, f32[8,256]{1,0:T(8,128)S(1)} %tile.9), kind=kLoop, calls=%fused_computation.2 | loop fusion | flops 1152000 | bytes 2619392 | tf_op jit(solution)/shard_map/reduce_sum | solution.py:36
  23.9 1.2 %reshape.563 = bf16[12,25,2,2,64]{4,3,2,1,0:T(2,128)(2,1)S(1)} reshape(bf16[12,25,256]{2,1,0:T(8,128)(2,1)} %multiply_reduce_fusion.1) | data formatting | bytes 307200 | tf_op jit(solution)/shard_map/reshape | solution.py:42
  25.7 0.6 copy.227
  26.4 0.6 copy.226
  28.2 1.0 %copy.186 = bf16[12,25,2,2,64]{4,3,2,1,0:T(2,128)(2,1)} copy(bf16[12,25,2,2,64]{4,2,0,3,1:T(2,128)(2,1)S(1)} %bitcast.234) | data formatting | bytes 307200 | tf_op jit(solution)/shard_map/transpose | solution.py:48
  29.2 1.2 %reshape.566 = bf16[12,25,256]{2,1,0:T(8,128)(2,1)S(1)} reshape(bf16[12,25,2,2,64]{4,3,2,1,0:T(2,128)(2,1)} %copy.186) | data formatting | bytes 307200 | tf_op jit(solution)/shard_map/reshape | solution.py:48
  30.5 2.9 %fusion.49 = (f32[1,12,8,25,25]{3,0,4,1,2:T(1,128)S(1)}, f32[1,12,8,25,25]{3,0,4,1,2:T(1,128)}) fusion(f32[2,12,8,25,25]{3,0,4,1,2:T(2,128)S(1)} %bitcast.230), kind=kLoop, calls=%fused_computation.155 | loop fusion | bytes 960000 | tf_op jit(solution)/shard_map/slice | solution.py:30
  33.9 0.8 copy-done.3
  36.5 1.6 %pad_maximum_fusion.1 = f32[12,200,256]{2,1,0:T(8,128)} fusion(f32[12,200,128]{2,1,0:T(8,128)S(1)} %get-tuple-element.34, f32[12,200,128]{2,1,0:T(8,128)S(1)} %get-tuple-element.33), kind=kLoop, calls=%fused_computation.4 | loop fusion | flops 614400 | bytes 4915200 | tf_op jit(solution)/shard_map/concatenate | solution.py:18
  38.1 2.7 %reshape.567 = f32[12,8,25,256]{3,2,1,0:T(8,128)S(1)} reshape(f32[12,200,256]{2,1,0:T(8,128)} %pad_maximum_fusion.1) | data formatting | bytes 4915200 | tf_op jit(solution)/shard_map/reshape | solution.py:32
  40.8 1.1 %multiply_reduce_fusion = f32[12,25,256]{2,1,0:T(8,128)} fusion(f32[12,8,25,256]{3,2,1,0:T(8,128)S(1)} %reshape.567, f32[8,256]{1,0:T(8,128)S(1)} %tile.9), kind=kLoop, calls=%fused_computation.1 | loop fusion | flops 1152000 | bytes 2772992 | tf_op jit(solution)/shard_map/reduce_sum | solution.py:36
  42.2 1.6 %fusion.55 = f32[12,25,32]{1,2,0:T(8,128)S(1)} fusion(f32[12,25,256]{2,1,0:T(8,128)} %multiply_reduce_fusion, f32[256,32,1]{0,1,2:T(8,128)S(1)} %reshape.730), kind=kOutput, calls=%fused_computation.161 | convolution fusion | flops 14745600 | bytes 378368 | tf_op jit(solution)/shard_map/lpC,CD->lpD/dot_general | solution.py:90
  43.8 1.3 %convolution_bitcast_fusion.6 = f32[12,200,32]{1,2,0:T(8,128)S(1)} fusion(f32[12,25,32]{1,2,0:T(8,128)S(1)} %fusion.55, f32[12,200,25]{1,2,0:T(8,128)} %copy-done.4), kind=kOutput, calls=%fused_computation.17 | convolution fusion | flops 11520000 | bytes 585600 | tf_op jit(solution)/shard_map/lQp,lpC->lQC/dot_general | solution.py:30
  47.3 0.7 copy.228
  48.3 0.7 copy.229
  53.3 1.4 %fusion.54 = (f32[1,1,12,25,25]{4,1,3,2,0:T(1,128)S(1)}, f32[1,1,12,25,25]{4,1,3,2,0:T(1,128)S(1)}) fusion(f32[1,2,12,25,25]{4,1,3,2,0:T(2,128)} %param.27), kind=kLoop, calls=%fused_computation.160 | loop fusion | bytes 120000 | tf_op jit(solution)/shard_map/slice | solution.py:98
  54.8 0.6 fusion.18
  55.4 0.6 dynamic_slice.3
  56.0 0.7 fusion.45
  56.7 2.6 %collective-permute-start.1 = (f32[12,25,16]{1,2,0:T(8,128)S(1)}, f32[12,25,16]{1,2,0:T(8,128)S(1)}, u32[]{:S(2)}, u32[]{:S(2)}) collective-permute-start(f32[12,25,16]{1,2,0:T(8,128)S(1)} %add.191), channel_id=1, source_target_pairs={{0,2},{2,0},{1,3},{3,1},{4,6},{6,4},{5,7},{7,5},{8,10},{10,8},{9,1... | collective-permute-start | bytes 57608 | tf_op jit(solution)/shard_map/ppermute | solution.py:170
  60.7 2.1 %collective-permute-done.1 = f32[12,25,16]{1,2,0:T(8,128)S(1)} collective-permute-done((f32[12,25,16]{1,2,0:T(8,128)S(1)}, f32[12,25,16]{1,2,0:T(8,128)S(1)}, u32[]{:S(2)}, u32[]{:S(2)}) %collective-permute-start.1) | collective-permute-done | bytes 19232 | tf_op jit(solution)/shard_map/ppermute | solution.py:170
  65.7 1.0 %constant_dynamic-slice_fusion.1 = (f32[1,64,512]{1,0,2:T(1,128)S(1)}, f32[1,64,512]{1,0,2:T(1,128)S(1)}, f32[1,64,512]{1,0,2:T(1,128)S(1)}, f32[1,64,512]{1,0,2:T(1,128)S(1)}) fusion(f32[4,64,512]{1,0,2:T(4,128)S(1)} %reshape_reshape.6, s32[]{:T(128)S(6)} %select_n.229, s32[]{:T(128)S(6)} %select_n.227, s32[]{:T(128)S(6)} %select_n.235, pred[]{:T(512)S(6)} %and.156, ...), kind=kLoop, calls=%fused_computation.136 | loop fusion | flops 32768 | bytes 1048593 | tf_op jit(solution)/shard_map/jit(_take) | solution.py:201
  66.7 1.9 %collective-permute-start.2 = (bf16[64,512]{0,1:T(8,128)(2,1)S(1)}, bf16[64,512]{0,1:T(8,128)(2,1)S(1)}, u32[]{:S(2)}, u32[]{:S(2)}) collective-permute-start(bf16[64,512]{0,1:T(8,128)(2,1)S(1)} %bitcast_convert_fusion.1), channel_id=1, source_target_pairs={{0,4},{4,8},{8,12},{12,0},{1,5},{5,9},{9,13},{13,1},{2,6},{6,10},{... | collective-permute-start | bytes 196616 | tf_op jit(solution)/shard_map/ppermute | solution.py:202
  68.7 2.7 %collective-permute-start.3 = (bf16[64,512]{0,1:T(8,128)(2,1)S(1)}, bf16[64,512]{0,1:T(8,128)(2,1)S(1)}, u32[]{:S(2)}, u32[]{:S(2)}) collective-permute-start(bf16[64,512]{0,1:T(8,128)(2,1)S(1)} %bitcast_convert_fusion), channel_id=1, source_target_pairs={{0,8},{4,12},{8,0},{12,4},{1,9},{5,13},{9,1},{13,5},{2,10},{6,14},... | collective-permute-start | bytes 196616 | tf_op jit(solution)/shard_map/ppermute | solution.py:202
  71.4 1.4 %collective-permute-start.4 = (bf16[64,512]{0,1:T(8,128)(2,1)S(1)}, bf16[64,512]{0,1:T(8,128)(2,1)S(1)}, u32[]{:S(2)}, u32[]{:S(2)}) collective-permute-start(bf16[64,512]{0,1:T(8,128)(2,1)S(1)} %convert_element_type.165), channel_id=1, source_target_pairs={{0,12},{4,0},{8,4},{12,8},{1,13},{5,1},{9,5},{13,9},{2,14},{6,2},{... | collective-permute-start | bytes 196616 | tf_op jit(solution)/shard_map/ppermute | solution.py:202
  72.9 0.8 copy.215
  73.7 1.4 %collective-permute-done.2 = bf16[64,512]{0,1:T(8,128)(2,1)S(1)} collective-permute-done((bf16[64,512]{0,1:T(8,128)(2,1)S(1)}, bf16[64,512]{0,1:T(8,128)(2,1)S(1)}, u32[]{:S(2)}, u32[]{:S(2)}) %collective-permute-start.2) | collective-permute-done | bytes 65568 | tf_op jit(solution)/shard_map/ppermute | solution.py:202
  75.1 4.6 %collective-permute-done.3 = bf16[64,512]{0,1:T(8,128)(2,1)S(1)} collective-permute-done((bf16[64,512]{0,1:T(8,128)(2,1)S(1)}, bf16[64,512]{0,1:T(8,128)(2,1)S(1)}, u32[]{:S(2)}, u32[]{:S(2)}) %collective-permute-start.3) | collective-permute-done | bytes 65568 | tf_op jit(solution)/shard_map/ppermute | solution.py:202
  81.4 1.1 %collective-permute-done.5 = bf16[2,4,1024]{2,1,0:T(4,128)(2,1)S(1)} collective-permute-done((bf16[2,4,1024]{2,1,0:T(4,128)(2,1)S(1)}, bf16[2,4,1024]{2,1,0:T(4,128)(2,1)S(1)}, u32[]{:S(2)}, u32[]{:S(2)}) %collective-permute-start.5) | collective-permute-done | bytes 16416 | tf_op jit(solution)/shard_map/ppermute | solution.py:177
  82.5 1.6 %collective-permute-start.6 = (bf16[4,1024]{1,0:T(4,128)(2,1)S(1)}, bf16[4,1024]{1,0:T(4,128)(2,1)S(1)}, u32[]{:S(2)}, u32[]{:S(2)}) collective-permute-start(bf16[4,1024]{1,0:T(4,128)(2,1)S(1)} %fusion.36), channel_id=1, source_target_pairs={{0,2},{2,0},{1,3},{3,1},{4,6},{6,4},{5,7},{7,5},{8,10},{10,8},{9,1... | collective-permute-start | bytes 24584 | tf_op jit(solution)/shard_map/ppermute | solution.py:177
  84.1 2.1 %collective-permute-done.6 = bf16[4,1024]{1,0:T(4,128)(2,1)S(1)} collective-permute-done((bf16[4,1024]{1,0:T(4,128)(2,1)S(1)}, bf16[4,1024]{1,0:T(4,128)(2,1)S(1)}, u32[]{:S(2)}, u32[]{:S(2)}) %collective-permute-start.6) | collective-permute-done | bytes 8224 | tf_op jit(solution)/shard_map/ppermute | solution.py:177
  86.3 4.4 %collective-permute-start.7 = (bf16[1024]{0:T(1024)(128)(2,1)S(1)}, bf16[1024]{0:T(1024)(128)(2,1)S(1)}, u32[]{:S(2)}, u32[]{:S(2)}) collective-permute-start(bf16[1024]{0:T(1024)(128)(2,1)S(1)} %get-tuple-element.29), channel_id=1, source_target_pairs={{0,12},{4,0},{8,4},{12,8},{1,13},{5,1},{9,5},{13,9},{2,14},{6,2},{... | collective-permute-start | bytes 6152 | tf_op jit(solution)/shard_map/ppermute | solution.py:190
  91.5 0.6 collective-permute-done.7
  92.1 3.1 %collective-permute-done.8 = bf16[1024]{0:T(1024)(128)(2,1)S(1)} collective-permute-done((bf16[1024]{0:T(1024)(128)(2,1)S(1)}, bf16[1024]{0:T(1024)(128)(2,1)S(1)}, u32[]{:S(2)}, u32[]{:S(2)}) %collective-permute-start.8) | collective-permute-done | bytes 2080 | tf_op jit(solution)/shard_map/ppermute | solution.py:190
  95.3 1.2 %collective-permute-done.9 = bf16[1024]{0:T(1024)(128)(2,1)S(1)} collective-permute-done((bf16[1024]{0:T(1024)(128)(2,1)S(1)}, bf16[1024]{0:T(1024)(128)(2,1)S(1)}, u32[]{:S(2)}, u32[]{:S(2)}) %collective-permute-start.9) | collective-permute-done | bytes 2080 | tf_op jit(solution)/shard_map/ppermute | solution.py:190
  97.2 0.8 copy.222
  (151 shorter events, 19.8 us)
Async XLA Ops:
  0.0 11.9 %copy-start = (bf16[12,25,2,2,4,64]{5,4,3,2,1,0:T(4,128)(2,1)S(1)}, bf16[12,25,2,2,4,64]{5,4,3,2,1,0:T(4,128)(2,1)}, u32[]{:S(2)}) copy-start(bf16[12,25,2,2,4,64]{5,4,3,2,1,0:T(4,128)(2,1)} %param.18) | copy-start | bytes 1843204
  5.7 6.2 %copy-start.14 = (s32[64]{0:T(128)S(1)}, s32[64]{0:T(128)}, u32[]{:S(2)}) copy-start(s32[64]{0:T(128)} %param.20) | copy-start | bytes 772
  15.8 1.1 %copy-start.4 = (f32[12,200,25]{1,2,0:T(8,128)}, f32[12,200,25]{1,2,0:T(8,128)S(1)}, u32[]{:S(2)}) copy-start(f32[12,200,25]{1,2,0:T(8,128)S(1)} %squeeze.64) | copy-start | bytes 720004
  18.7 2.5 %copy-start.15 = (s32[16]{0:T(128)S(1)}, s32[16]{0:T(128)}, u32[]{:S(2)}) copy-start(s32[16]{0:T(128)} %param.22) | copy-start | bytes 196
  23.9 1.6 %copy-start.13 = (f32[2,25,2,12,2,12]{1,4,5,3,2,0:T(2,128)S(1)}, f32[2,25,2,12,2,12]{1,4,5,3,2,0:T(2,128)}, u32[]{:S(2)}) copy-start(f32[2,25,2,12,2,12]{1,4,5,3,2,0:T(2,128)} %param.25) | copy-start | bytes 345604
  27.7 2.8 %copy-start.2 = (f32[8,2,12,25,25]{4,1,3,2,0:T(2,128)S(1)}, f32[8,2,12,25,25]{4,1,3,2,0:T(2,128)}, u32[]{:S(2)}) copy-start(f32[8,2,12,25,25]{4,1,3,2,0:T(2,128)} %param.24) | copy-start | bytes 1440004
  33.4 1.3 %copy-start.3 = (f32[1,12,8,25,25]{3,0,4,1,2:T(1,128)S(1)}, f32[1,12,8,25,25]{3,0,4,1,2:T(1,128)}, u32[]{:S(2)}) copy-start(f32[1,12,8,25,25]{3,0,4,1,2:T(1,128)} %get-tuple-element.38) | copy-start | bytes 720004
  33.9 1.3 %copy-start.5 = (f32[12,200,25]{1,2,0:T(8,128)}, f32[12,200,25]{1,2,0:T(8,128)S(1)}, u32[]{:S(2)}) copy-start(f32[12,200,25]{1,2,0:T(8,128)S(1)} %squeeze.68) | copy-start | bytes 720004
  35.2 1.1 %copy-start.7 = (f32[12,200,25]{1,2,0:T(8,128)}, f32[12,200,25]{1,2,0:T(8,128)S(1)}, u32[]{:S(2)}) copy-start(f32[12,200,25]{1,2,0:T(8,128)S(1)} %squeeze.69) | copy-start | bytes 720004
  40.8 1.2 %copy-start.16 = (s32[16]{0:T(128)S(1)}, s32[16]{0:T(128)}, u32[]{:S(2)}) copy-start(s32[16]{0:T(128)} %param.21) | copy-start | bytes 196
  45.5 0.7 copy-start.17
  46.2 1.1 %copy-start.11 = (f32[2,25,2,12,2,12]{1,4,5,3,2,0:T(2,128)S(1)}, f32[2,25,2,12,2,12]{1,4,5,3,2,0:T(2,128)}, u32[]{:S(2)}) copy-start(f32[2,25,2,12,2,12]{1,4,5,3,2,0:T(2,128)} %param.26) | copy-start | bytes 345604
  49.3 1.0 %copy-start.6 = (f32[12,200,25]{1,2,0:T(8,128)S(1)}, f32[12,200,25]{1,2,0:T(8,128)}, u32[]{:S(2)}) copy-start(f32[12,200,25]{1,2,0:T(8,128)} %copy-done.5) | copy-start | bytes 720004
  50.0 1.0 %copy-start.8 = (f32[12,200,25]{1,2,0:T(8,128)S(1)}, f32[12,200,25]{1,2,0:T(8,128)}, u32[]{:S(2)}) copy-start(f32[12,200,25]{1,2,0:T(8,128)} %copy-done.7) | copy-start | bytes 720004
  52.0 2.7 %copy-start.9 = (f32[1,2,25,2,32,2,12]{4,5,6,3,2,1,0:T(2,128)S(1)}, f32[1,2,25,2,32,2,12]{4,5,6,3,2,1,0:T(2,128)}, u32[]{:S(2)}) copy-start(f32[1,2,25,2,32,2,12]{4,5,6,3,2,1,0:T(2,128)} %param.28) | copy-start | bytes 921604
  52.8 3.9 %collective-permute-start = (f32[12,25,16]{1,2,0:T(8,128)S(1)}, f32[12,25,16]{1,2,0:T(8,128)S(1)}, u32[]{:S(2)}, u32[]{:S(2)}) collective-permute-start(f32[12,25,16]{1,2,0:T(8,128)S(1)} %reduce_sum.49), channel_id=1, source_target_pairs={{0,1},{1,0},{2,3},{3,2},{4,5},{5,4},{6,7},{7,6},{8,9},{9,8},{10,11... | collective-permute-start | bytes 57608 | tf_op jit(solution)/shard_map/ppermute | solution.py:170
  54.7 0.7 copy-start.18
  56.7 6.0 %collective-permute-start.1 = (f32[12,25,16]{1,2,0:T(8,128)S(1)}, f32[12,25,16]{1,2,0:T(8,128)S(1)}, u32[]{:S(2)}, u32[]{:S(2)}) collective-permute-start(f32[12,25,16]{1,2,0:T(8,128)S(1)} %add.191), channel_id=1, source_target_pairs={{0,2},{2,0},{1,3},{3,1},{4,6},{6,4},{5,7},{7,5},{8,10},{10,8},{9,1... | collective-permute-start | bytes 57608 | tf_op jit(solution)/shard_map/ppermute | solution.py:170
  63.0 1.4 %copy-start.10 = (bf16[1,32,25,256]{3,1,2,0:T(8,128)(2,1)S(1)}, bf16[1,32,25,256]{3,1,2,0:T(8,128)(2,1)}, u32[]{:S(2)}) copy-start(bf16[1,32,25,256]{3,1,2,0:T(8,128)(2,1)} %param.30) | copy-start | bytes 1228804
  65.7 7.2 %copy-start.12 = (bf16[64,32,32]{0,2,1:T(8,128)(2,1)S(1)}, bf16[64,32,32]{0,2,1:T(8,128)(2,1)}, u32[]{:S(2)}) copy-start(bf16[64,32,32]{0,2,1:T(8,128)(2,1)} %param.31) | copy-start | bytes 393220
  66.7 8.4 %collective-permute-start.2 = (bf16[64,512]{0,1:T(8,128)(2,1)S(1)}, bf16[64,512]{0,1:T(8,128)(2,1)S(1)}, u32[]{:S(2)}, u32[]{:S(2)}) collective-permute-start(bf16[64,512]{0,1:T(8,128)(2,1)S(1)} %bitcast_convert_fusion.1), channel_id=1, source_target_pairs={{0,4},{4,8},{8,12},{12,0},{1,5},{5,9},{9,13},{13,1},{2,6},{6,10},{... | collective-permute-start | bytes 196616 | tf_op jit(solution)/shard_map/ppermute | solution.py:202
  68.7 11.1 %collective-permute-start.3 = (bf16[64,512]{0,1:T(8,128)(2,1)S(1)}, bf16[64,512]{0,1:T(8,128)(2,1)S(1)}, u32[]{:S(2)}, u32[]{:S(2)}) collective-permute-start(bf16[64,512]{0,1:T(8,128)(2,1)S(1)} %bitcast_convert_fusion), channel_id=1, source_target_pairs={{0,8},{4,12},{8,0},{12,4},{1,9},{5,13},{9,1},{13,5},{2,10},{6,14},... | collective-permute-start | bytes 196616 | tf_op jit(solution)/shard_map/ppermute | solution.py:202
  71.4 8.4 %collective-permute-start.4 = (bf16[64,512]{0,1:T(8,128)(2,1)S(1)}, bf16[64,512]{0,1:T(8,128)(2,1)S(1)}, u32[]{:S(2)}, u32[]{:S(2)}) collective-permute-start(bf16[64,512]{0,1:T(8,128)(2,1)S(1)} %convert_element_type.165), channel_id=1, source_target_pairs={{0,12},{4,0},{8,4},{12,8},{1,13},{5,1},{9,5},{13,9},{2,14},{6,2},{... | collective-permute-start | bytes 196616 | tf_op jit(solution)/shard_map/ppermute | solution.py:202
  81.3 1.2 %collective-permute-start.5 = (bf16[2,4,1024]{2,1,0:T(4,128)(2,1)S(1)}, bf16[2,4,1024]{2,1,0:T(4,128)(2,1)S(1)}, u32[]{:S(2)}, u32[]{:S(2)}) collective-permute-start(bf16[2,4,1024]{2,1,0:T(4,128)(2,1)S(1)} %fusion.32), channel_id=1, source_target_pairs={{0,1},{1,0},{2,3},{3,2},{4,5},{5,4},{6,7},{7,6},{8,9},{9,8},{10,11... | collective-permute-start | bytes 49160 | tf_op jit(solution)/shard_map/ppermute | solution.py:177
  81.3 16.6 %copy-start.1 = (bf16[12,25,2,2,4,64]{5,4,3,2,1,0:T(4,128)(2,1)S(1)}, bf16[12,25,2,2,4,64]{5,4,3,2,1,0:T(4,128)(2,1)}, u32[]{:S(2)}) copy-start(bf16[12,25,2,2,4,64]{5,4,3,2,1,0:T(4,128)(2,1)} %param.18) | copy-start | bytes 1843204
  82.5 3.7 %collective-permute-start.6 = (bf16[4,1024]{1,0:T(4,128)(2,1)S(1)}, bf16[4,1024]{1,0:T(4,128)(2,1)S(1)}, u32[]{:S(2)}, u32[]{:S(2)}) collective-permute-start(bf16[4,1024]{1,0:T(4,128)(2,1)S(1)} %fusion.36), channel_id=1, source_target_pairs={{0,2},{2,0},{1,3},{3,1},{4,6},{6,4},{5,7},{7,5},{8,10},{10,8},{9,1... | collective-permute-start | bytes 24584 | tf_op jit(solution)/shard_map/ppermute | solution.py:177
  86.3 5.7 %collective-permute-start.7 = (bf16[1024]{0:T(1024)(128)(2,1)S(1)}, bf16[1024]{0:T(1024)(128)(2,1)S(1)}, u32[]{:S(2)}, u32[]{:S(2)}) collective-permute-start(bf16[1024]{0:T(1024)(128)(2,1)S(1)} %get-tuple-element.29), channel_id=1, source_target_pairs={{0,12},{4,0},{8,4},{12,8},{1,13},{5,1},{9,5},{13,9},{2,14},{6,2},{... | collective-permute-start | bytes 6152 | tf_op jit(solution)/shard_map/ppermute | solution.py:190
  90.7 4.5 %collective-permute-start.8 = (bf16[1024]{0:T(1024)(128)(2,1)S(1)}, bf16[1024]{0:T(1024)(128)(2,1)S(1)}, u32[]{:S(2)}, u32[]{:S(2)}) collective-permute-start(bf16[1024]{0:T(1024)(128)(2,1)S(1)} %get-tuple-element.32), channel_id=1, source_target_pairs={{0,8},{4,12},{8,0},{12,4},{1,9},{5,13},{9,1},{13,5},{2,10},{6,14},... | collective-permute-start | bytes 6152 | tf_op jit(solution)/shard_map/ppermute | solution.py:190
  91.1 5.4 %collective-permute-start.9 = (bf16[1024]{0:T(1024)(128)(2,1)S(1)}, bf16[1024]{0:T(1024)(128)(2,1)S(1)}, u32[]{:S(2)}, u32[]{:S(2)}) collective-permute-start(bf16[1024]{0:T(1024)(128)(2,1)S(1)} %get-tuple-element.31), channel_id=1, source_target_pairs={{0,4},{4,8},{8,12},{12,0},{1,5},{5,9},{9,13},{13,1},{2,6},{6,10},{... | collective-permute-start | bytes 6152 | tf_op jit(solution)/shard_map/ppermute | solution.py:190

commit v5 on v2

--- a/solution.py
+++ b/solution.py
@@ -21,14 +21,15 @@
 def turn_select(vectors, rotation, octants, backward, prec):
     degrees, orders, width = vectors.shape
     if backward:
-        mats = jnp.transpose(rotation, (1, 2, 0, 4, 3))
+        mats = jnp.transpose(rotation, (2, 1, 0, 4, 3))
         sign = -1.0
     else:
-        mats = jnp.transpose(rotation, (1, 2, 0, 3, 4))
+        mats = jnp.transpose(rotation, (2, 1, 0, 3, 4))
         sign = 1.0
-    mats = mats.reshape(2, degrees, 8 * orders, orders)
-    first = jnp.einsum("lQp,lpC->lQC", mats[0], vectors, precision=prec)
-    second = sign * jnp.einsum("lQp,lpC->lQC", mats[1], vectors, precision=prec)
+    mats = mats.reshape(degrees, 2 * 8 * orders, orders)
+    both = jnp.einsum("lQp,lpC->lQC", mats, vectors, precision=prec)
+    first = both[:, : 8 * orders]
+    second = sign * both[:, 8 * orders :]
     joined = complex_join(first, second, width // 2).reshape(degrees, 8, orders, width)
     count = octants.shape[0]
     chosen = (octants[None, :] == jnp.arange(8, dtype=jnp.int32)[:, None]).astype(jnp.float32)
@@ -41,9 +42,10 @@
     rest = width // 4
     moved = vectors.reshape(degrees, orders, 2, 2, rest)
     moved = jnp.transpose(moved, (1, 3, 0, 2, 4)).reshape(orders, 2 * degrees, 2 * rest)
-    mats = axial.reshape(2, orders, 2 * degrees, 2 * degrees)
-    first = jnp.einsum("qab,qbC->qaC", mats[0], moved, precision=prec)
-    second = jnp.einsum("qab,qbC->qaC", mats[1], moved, precision=prec)
+    mats = jnp.swapaxes(axial.reshape(2, orders, 2 * degrees, 2 * degrees), 0, 1).reshape(orders, 4 * degrees, 2 * degrees)
+    both = jnp.einsum("qab,qbC->qaC", mats, moved, precision=prec)
+    first = both[:, : 2 * degrees]
+    second = both[:, 2 * degrees :]
     joined = complex_join(first, second, rest).reshape(orders, 2, degrees, 2, rest)
     return jnp.transpose(joined, (2, 0, 3, 1, 4)).reshape(degrees, orders, width)
 

time: 92.5 us -> 84.7 us (0.916)
  local copies, waits for them, and re-layouts: 39.2 us -> 31.9 us
  matrix products: 7.76 us -> 6.73 us
    slice x8 -> x0, local copies, waits for them, and re-layouts: 13.1 us -> none  [the longest x4 9.76 us: turn_select(): first = jnp.einsum('lQp,lpC->lQC', mats[0], vectors, precision=prec)]
    transpose x0 -> x4, local copies, waits for them, and re-layouts: none -> 6.32 us  [the longest x1 3.63 us: turn_select(): mats = jnp.transpose(rotation, (2, 1, 0, 3, 4))]
    squeeze x12 -> x0, local copies, waits for them, and re-layouts: 4.87 us -> none  [the longest x4 1.52 us: axial_apply(): second = jnp.einsum('qab,qbC->qaC', mats[1], moved, precision=prec)]
    reshape x0 -> x4, local copies, waits for them, and re-layouts: none -> 4.27 us  [the longest x2 3.95 us: turn_select(): mats = mats.reshape(degrees, 2 * 8 * orders, orders)]
    dot_general x12 -> x6, matrix products: 3.69 us -> 2.66 us  [the longest x4 2.16 us: turn_select(): both = jnp.einsum('lQp,lpC->lQC', mats, vectors, precision=prec)]
    unnamed x37 -> x33, local copies, waits for them, and re-layouts: 2.23 us -> 2.43 us
  transfers between devices with their start and end apart: 10 -> 10, of which waited for: 8 -> 8; matrix products, arithmetic and copies ran while one was open for 6% -> 7% of each run, Pallas kernels for 0% -> 0%
where the time goes in v5:
time: 84.7 us; the launch traced here: 84.2 us
  local copies, waits for them, and re-layouts  31.9 us (38%)
  starting transfers between devices  16 us (19%)
  waiting for transfers between devices  16 us (19%)
  other arithmetic  12 us (14%)
  matrix products  6.73 us (8%)
  between operations  1.58 us (2%)
    reshape x4, local copies, waits for them, and re-layouts, turn_select(): complex_join(first, second, width // 2).reshape(degrees, 8, orders, width)  6.17 us
    ppermute x3, starting transfers between devices, shift_reduce_scatter(): piece = lax.ppermute(piece, axis, [(i, (i + step) % n) for i in range(n)])  6.16 us
    ppermute x3, waiting for transfers between devices, shift_reduce_scatter(): piece = lax.ppermute(piece, axis, [(i, (i + step) % n) for i in range(n)])  5.85 us
    ppermute x3, starting transfers between devices, shift_all_to_all(): piece = lax.ppermute(piece, axis, [(i, (i + step) % n) for i in range(n)])  5.01 us
    ppermute x3, waiting for transfers between devices, shift_all_to_all(): piece = lax.ppermute(piece, axis, [(i, (i + step) % n) for i in range(n)])  4.92 us
    reshape x2, local copies, waits for them, and re-layouts, turn_select(): mats = mats.reshape(degrees, 2 * 8 * orders, orders)  3.95 us
    transpose x1, local copies, waits for them, and re-layouts, turn_select(): mats = jnp.transpose(rotation, (2, 1, 0, 3, 4))  3.63 us
    concatenate x8, other arithmetic, complex_join(): return jnp.concatenate([real, imag], axis=-1)  3.51 us
  transfers between devices with their start and end apart: 10, of which 8 were waited for; matrix products, arithmetic and copies ran while one was open for 7% of the time, Pallas kernels for 0%

profile of v5, /device:TPU:0, one launch (start us, length us, event | category | flops | bytes accessed | tf_op | source)
XLA Modules:
  0.0 84.2 jit_solution(14599336844059850115)
XLA Ops:
  0.0 3.6 %copy.144 = bf16[12,2,8,25,25]{3,2,1,4,0:T(8,128)(2,1)S(1)} copy(f32[12,2,8,25,25]{4,1,3,0,2:T(2,128)} %bitcast.207) | data formatting | bytes 720000 | tf_op jit(solution)/shard_map/transpose | solution.py:27
  3.7 1.4 %reshape.560 = bf16[12,400,25]{1,2,0:T(8,128)(2,1)S(1)} reshape(bf16[12,2,8,25,25]{3,2,1,4,0:T(8,128)(2,1)S(1)} %copy.144) | data formatting | bytes 480000 | tf_op jit(solution)/shard_map/reshape | solution.py:29
  5.8 0.5 convolution_bitcast_fusion
  6.3 0.6 copy.143
  6.9 1.2 %reshape.559 = bf16[12,25,256]{2,1,0:T(8,128)(2,1)S(1)} reshape(bf16[4800,16]{1,0:T(8,128)(2,1)S(1)} %copy.143) | data formatting | bytes 307200 | tf_op jit(solution)/shard_map/reshape | solution.py:82
  8.1 0.8 %convolution_bitcast_fusion.2 = f32[12,400,256]{2,1,0:T(8,128)S(1)} fusion(bf16[12,25,256]{2,1,0:T(8,128)(2,1)S(1)} %reshape.559, bf16[12,400,25]{1,2,0:T(8,128)(2,1)S(1)} %reshape.560), kind=kOutput, calls=%fused_computation.7 | convolution fusion | flops 61440000 | bytes 5308800 | tf_op jit(solution)/shard_map/lQp,lpC->lQC/dot_general | solution.py:30
  9.2 1.6 %pad_maximum_fusion = f32[12,200,256]{2,1,0:T(8,128)} fusion(f32[12,200,128]{2,1,0:T(8,128)S(1)} %get-tuple-element.36, f32[12,200,128]{2,1,0:T(8,128)S(1)} %get-tuple-element.35), kind=kLoop, calls=%fused_computation.4 | loop fusion | flops 614400 | bytes 4915200 | tf_op jit(solution)/shard_map/concatenate | solution.py:18
  10.8 2.5 %reshape.561 = f32[12,8,25,256]{3,2,1,0:T(8,128)S(1)} reshape(f32[12,200,256]{2,1,0:T(8,128)} %pad_maximum_fusion) | data formatting | bytes 4915200 | tf_op jit(solution)/shard_map/reshape | solution.py:33
  13.3 0.6 tile.8
  14.0 0.9 %tile.9 = f32[8,256]{1,0:T(8,128)S(1)} reshape(f32[8,16,16]{2,1,0:T(8,128)} %tile.8) | data formatting | bytes 16384 | tf_op jit(solution)/shard_map/tile | solution.py:36
  14.9 1.0 %multiply_reduce_fusion.1 = bf16[12,25,256]{2,1,0:T(8,128)(2,1)} fusion(f32[12,8,25,256]{3,2,1,0:T(8,128)S(1)} %reshape.561, f32[8,256]{1,0:T(8,128)S(1)} %tile.9), kind=kLoop, calls=%fused_computation.2 | loop fusion | flops 1152000 | bytes 2619392 | tf_op jit(solution)/shard_map/reduce_sum | solution.py:37
  16.0 1.2 %reshape.562 = bf16[12,25,2,2,64]{4,3,2,1,0:T(2,128)(2,1)S(1)} reshape(bf16[12,25,256]{2,1,0:T(8,128)(2,1)} %multiply_reduce_fusion.1) | data formatting | bytes 307200 | tf_op jit(solution)/shard_map/reshape | solution.py:43
  18.0 0.6 copy.147
  20.2 0.6 copy-done.2
  20.7 1.5 %copy.149 = bf16[12,2,8,25,25]{3,2,1,4,0:T(8,128)(2,1)} copy(f32[12,2,8,25,25]{3,1,4,0,2:T(2,128)S(1)} %bitcast.208) | data formatting | bytes 720000 | tf_op jit(solution)/shard_map/transpose | solution.py:24
  22.3 2.5 %reshape.568 = bf16[12,400,25]{1,2,0:T(8,128)(2,1)S(1)} reshape(bf16[12,2,8,25,25]{3,2,1,4,0:T(8,128)(2,1)} %copy.149) | data formatting | bytes 480000 | tf_op jit(solution)/shard_map/reshape | solution.py:29
  24.8 0.8 %convolution_bitcast_fusion.1 = f32[12,400,256]{2,1,0:T(8,128)S(1)} fusion(bf16[12,25,256]{2,1,0:T(8,128)(2,1)S(1)} %reshape.567, bf16[12,400,25]{1,2,0:T(8,128)(2,1)S(1)} %reshape.568), kind=kOutput, calls=%fused_computation.6 | convolution fusion | flops 61440000 | bytes 5308800 | tf_op jit(solution)/shard_map/lQp,lpC->lQC/dot_general | solution.py:30
  26.1 1.6 %pad_maximum_fusion.1 = f32[12,200,256]{2,1,0:T(8,128)} fusion(f32[12,200,128]{2,1,0:T(8,128)S(1)} %get-tuple-element.34, f32[12,200,128]{2,1,0:T(8,128)S(1)} %get-tuple-element.33), kind=kLoop, calls=%fused_computation.5 | loop fusion | flops 614400 | bytes 4915200 | tf_op jit(solution)/shard_map/concatenate | solution.py:18
  27.8 2.7 %reshape.569 = f32[12,8,25,256]{3,2,1,0:T(8,128)S(1)} reshape(f32[12,200,256]{2,1,0:T(8,128)} %pad_maximum_fusion.1) | data formatting | bytes 4915200 | tf_op jit(solution)/shard_map/reshape | solution.py:33
  30.4 1.1 %multiply_reduce_fusion = f32[12,25,256]{2,1,0:T(8,128)} fusion(f32[12,8,25,256]{3,2,1,0:T(8,128)S(1)} %reshape.569, f32[8,256]{1,0:T(8,128)S(1)} %tile.9), kind=kLoop, calls=%fused_computation.1 | loop fusion | flops 1152000 | bytes 2772992 | tf_op jit(solution)/shard_map/reduce_sum | solution.py:37
  31.8 1.6 %fusion.50 = bf16[12,25,32]{1,2,0:T(8,128)(2,1)S(1)} fusion(f32[12,25,256]{2,1,0:T(8,128)} %multiply_reduce_fusion, f32[256,32,1]{0,1,2:T(8,128)S(1)} %reshape.734), kind=kOutput, calls=%fused_computation.152 | convolution fusion | flops 14745600 | bytes 359168 | tf_op jit(solution)/shard_map/lpC,CD->lpD/dot_general | solution.py:92
  33.9 0.5 reshape.570
  34.6 0.5 multiply_reduce_fusion.3
  35.8 0.6 copy.153
  37.7 0.5 reshape.577
  38.3 0.5 multiply_reduce_fusion.2
  39.1 0.5 collective-permute-start
  39.6 1.4 %fusion.49 = (f32[1,1,12,25,25]{4,1,3,2,0:T(1,128)S(1)}, f32[1,1,12,25,25]{4,1,3,2,0:T(1,128)S(1)}) fusion(f32[1,2,12,25,25]{4,1,3,2,0:T(2,128)} %param.27), kind=kLoop, calls=%fused_computation.151 | loop fusion | bytes 120000 | tf_op jit(solution)/shard_map/slice | solution.py:100
  41.1 0.6 fusion.17
  41.7 0.6 dynamic_slice.3
  42.3 0.7 fusion.44
  43.0 2.6 %collective-permute-start.1 = (f32[12,25,16]{1,2,0:T(8,128)S(1)}, f32[12,25,16]{1,2,0:T(8,128)S(1)}, u32[]{:S(2)}, u32[]{:S(2)}) collective-permute-start(f32[12,25,16]{1,2,0:T(8,128)S(1)} %add.191), channel_id=1, source_target_pairs={{0,2},{2,0},{1,3},{3,1},{4,6},{6,4},{5,7},{7,5},{8,10},{10,8},{9,1... | collective-permute-start | bytes 57608 | tf_op jit(solution)/shard_map/ppermute | solution.py:172
  47.0 2.1 %collective-permute-done.1 = f32[12,25,16]{1,2,0:T(8,128)S(1)} collective-permute-done((f32[12,25,16]{1,2,0:T(8,128)S(1)}, f32[12,25,16]{1,2,0:T(8,128)S(1)}, u32[]{:S(2)}, u32[]{:S(2)}) %collective-permute-start.1) | collective-permute-done | bytes 19232 | tf_op jit(solution)/shard_map/ppermute | solution.py:172
  52.0 1.0 %constant_dynamic-slice_fusion.1 = (f32[1,64,512]{1,0,2:T(1,128)S(1)}, f32[1,64,512]{1,0,2:T(1,128)S(1)}, f32[1,64,512]{1,0,2:T(1,128)S(1)}, f32[1,64,512]{1,0,2:T(1,128)S(1)}) fusion(f32[4,64,512]{1,0,2:T(4,128)S(1)} %reshape_reshape.6, s32[]{:T(128)S(6)} %select_n.229, s32[]{:T(128)S(6)} %select_n.227, s32[]{:T(128)S(6)} %select_n.235, pred[]{:T(512)S(6)} %and.156, ...), kind=kLoop, calls=%fused_computation.131 | loop fusion | flops 32768 | bytes 1048593 | tf_op jit(solution)/shard_map/jit(_take) | solution.py:203
  53.0 1.9 %collective-permute-start.2 = (bf16[64,512]{0,1:T(8,128)(2,1)S(1)}, bf16[64,512]{0,1:T(8,128)(2,1)S(1)}, u32[]{:S(2)}, u32[]{:S(2)}) collective-permute-start(bf16[64,512]{0,1:T(8,128)(2,1)S(1)} %bitcast_convert_fusion.1), channel_id=1, source_target_pairs={{0,4},{4,8},{8,12},{12,0},{1,5},{5,9},{9,13},{13,1},{2,6},{6,10},{... | collective-permute-start | bytes 196616 | tf_op jit(solution)/shard_map/ppermute | solution.py:204
  54.9 2.6 %collective-permute-start.3 = (bf16[64,512]{0,1:T(8,128)(2,1)S(1)}, bf16[64,512]{0,1:T(8,128)(2,1)S(1)}, u32[]{:S(2)}, u32[]{:S(2)}) collective-permute-start(bf16[64,512]{0,1:T(8,128)(2,1)S(1)} %bitcast_convert_fusion), channel_id=1, source_target_pairs={{0,8},{4,12},{8,0},{12,4},{1,9},{5,13},{9,1},{13,5},{2,10},{6,14},... | collective-permute-start | bytes 196616 | tf_op jit(solution)/shard_map/ppermute | solution.py:204
  57.6 1.6 %collective-permute-start.4 = (bf16[64,512]{0,1:T(8,128)(2,1)S(1)}, bf16[64,512]{0,1:T(8,128)(2,1)S(1)}, u32[]{:S(2)}, u32[]{:S(2)}) collective-permute-start(bf16[64,512]{0,1:T(8,128)(2,1)S(1)} %convert_element_type.165), channel_id=1, source_target_pairs={{0,12},{4,0},{8,4},{12,8},{1,13},{5,1},{9,5},{13,9},{2,14},{6,2},{... | collective-permute-start | bytes 196616 | tf_op jit(solution)/shard_map/ppermute | solution.py:204
  59.4 0.8 copy.172
  60.2 1.2 %collective-permute-done.2 = bf16[64,512]{0,1:T(8,128)(2,1)S(1)} collective-permute-done((bf16[64,512]{0,1:T(8,128)(2,1)S(1)}, bf16[64,512]{0,1:T(8,128)(2,1)S(1)}, u32[]{:S(2)}, u32[]{:S(2)}) %collective-permute-start.2) | collective-permute-done | bytes 65568 | tf_op jit(solution)/shard_map/ppermute | solution.py:204
  61.4 4.7 %collective-permute-done.3 = bf16[64,512]{0,1:T(8,128)(2,1)S(1)} collective-permute-done((bf16[64,512]{0,1:T(8,128)(2,1)S(1)}, bf16[64,512]{0,1:T(8,128)(2,1)S(1)}, u32[]{:S(2)}, u32[]{:S(2)}) %collective-permute-start.3) | collective-permute-done | bytes 65568 | tf_op jit(solution)/shard_map/ppermute | solution.py:204
  67.7 1.1 %collective-permute-done.5 = bf16[2,4,1024]{2,1,0:T(4,128)(2,1)S(1)} collective-permute-done((bf16[2,4,1024]{2,1,0:T(4,128)(2,1)S(1)}, bf16[2,4,1024]{2,1,0:T(4,128)(2,1)S(1)}, u32[]{:S(2)}, u32[]{:S(2)}) %collective-permute-start.5) | collective-permute-done | bytes 16416 | tf_op jit(solution)/shard_map/ppermute | solution.py:179
  68.8 1.7 %collective-permute-start.6 = (bf16[4,1024]{1,0:T(4,128)(2,1)S(1)}, bf16[4,1024]{1,0:T(4,128)(2,1)S(1)}, u32[]{:S(2)}, u32[]{:S(2)}) collective-permute-start(bf16[4,1024]{1,0:T(4,128)(2,1)S(1)} %fusion.35), channel_id=1, source_target_pairs={{0,2},{2,0},{1,3},{3,1},{4,6},{6,4},{5,7},{7,5},{8,10},{10,8},{9,1... | collective-permute-start | bytes 24584 | tf_op jit(solution)/shard_map/ppermute | solution.py:179
  70.5 2.1 %collective-permute-done.6 = bf16[4,1024]{1,0:T(4,128)(2,1)S(1)} collective-permute-done((bf16[4,1024]{1,0:T(4,128)(2,1)S(1)}, bf16[4,1024]{1,0:T(4,128)(2,1)S(1)}, u32[]{:S(2)}, u32[]{:S(2)}) %collective-permute-start.6) | collective-permute-done | bytes 8224 | tf_op jit(solution)/shard_map/ppermute | solution.py:179
  72.6 4.4 %collective-permute-start.7 = (bf16[1024]{0:T(1024)(128)(2,1)S(1)}, bf16[1024]{0:T(1024)(128)(2,1)S(1)}, u32[]{:S(2)}, u32[]{:S(2)}) collective-permute-start(bf16[1024]{0:T(1024)(128)(2,1)S(1)} %get-tuple-element.29), channel_id=1, source_target_pairs={{0,12},{4,0},{8,4},{12,8},{1,13},{5,1},{9,5},{13,9},{2,14},{6,2},{... | collective-permute-start | bytes 6152 | tf_op jit(solution)/shard_map/ppermute | solution.py:192
  77.7 0.6 collective-permute-done.7
  78.4 3.1 %collective-permute-done.8 = bf16[1024]{0:T(1024)(128)(2,1)S(1)} collective-permute-done((bf16[1024]{0:T(1024)(128)(2,1)S(1)}, bf16[1024]{0:T(1024)(128)(2,1)S(1)}, u32[]{:S(2)}, u32[]{:S(2)}) %collective-permute-start.8) | collective-permute-done | bytes 2080 | tf_op jit(solution)/shard_map/ppermute | solution.py:192
  81.6 1.2 %collective-permute-done.9 = bf16[1024]{0:T(1024)(128)(2,1)S(1)} collective-permute-done((bf16[1024]{0:T(1024)(128)(2,1)S(1)}, bf16[1024]{0:T(1024)(128)(2,1)S(1)}, u32[]{:S(2)}, u32[]{:S(2)}) %collective-permute-start.9) | collective-permute-done | bytes 2080 | tf_op jit(solution)/shard_map/ppermute | solution.py:192
  83.5 0.8 copy.179
  (129 shorter events, 13.8 us)
Async XLA Ops:
  0.0 5.8 %copy-start = (bf16[12,25,2,2,4,64]{5,4,3,2,1,0:T(4,128)(2,1)S(1)}, bf16[12,25,2,2,4,64]{5,4,3,2,1,0:T(4,128)(2,1)}, u32[]{:S(2)}) copy-start(bf16[12,25,2,2,4,64]{5,4,3,2,1,0:T(4,128)(2,1)} %param.18) | copy-start | bytes 1843204
  3.7 2.1 %copy-start.10 = (s32[64]{0:T(128)S(1)}, s32[64]{0:T(128)}, u32[]{:S(2)}) copy-start(s32[64]{0:T(128)} %param.20) | copy-start | bytes 772
  10.8 2.5 %copy-start.11 = (s32[16]{0:T(128)S(1)}, s32[16]{0:T(128)}, u32[]{:S(2)}) copy-start(s32[16]{0:T(128)} %param.22) | copy-start | bytes 196
  16.0 1.6 %copy-start.7 = (f32[2,25,2,12,2,12]{1,4,5,3,2,0:T(2,128)S(1)}, f32[2,25,2,12,2,12]{1,4,5,3,2,0:T(2,128)}, u32[]{:S(2)}) copy-start(f32[2,25,2,12,2,12]{1,4,5,3,2,0:T(2,128)} %param.25) | copy-start | bytes 345604
  19.0 1.7 %copy-start.2 = (f32[8,2,12,25,25]{4,1,3,2,0:T(2,128)S(1)}, f32[8,2,12,25,25]{4,1,3,2,0:T(2,128)}, u32[]{:S(2)}) copy-start(f32[8,2,12,25,25]{4,1,3,2,0:T(2,128)} %param.24) | copy-start | bytes 1440004
  24.8 0.9 %copy-start.3 = (bf16[12,400,25]{1,2,0:T(8,128)(2,1)}, bf16[12,400,25]{1,2,0:T(8,128)(2,1)S(1)}, u32[]{:S(2)}) copy-start(bf16[12,400,25]{1,2,0:T(8,128)(2,1)S(1)} %reshape.568) | copy-start | bytes 720004
  30.4 1.2 %copy-start.12 = (s32[16]{0:T(128)S(1)}, s32[16]{0:T(128)}, u32[]{:S(2)}) copy-start(s32[16]{0:T(128)} %param.21) | copy-start | bytes 196
  33.8 0.7 copy-start.13
  33.9 1.5 %copy-start.8 = (f32[2,25,2,12,2,12]{1,4,5,3,2,0:T(2,128)S(1)}, f32[2,25,2,12,2,12]{1,4,5,3,2,0:T(2,128)}, u32[]{:S(2)}) copy-start(f32[2,25,2,12,2,12]{1,4,5,3,2,0:T(2,128)} %param.26) | copy-start | bytes 345604
  35.4 1.8 %copy-start.4 = (bf16[12,400,25]{1,2,0:T(8,128)(2,1)S(1)}, bf16[12,400,25]{1,2,0:T(8,128)(2,1)}, u32[]{:S(2)}) copy-start(bf16[12,400,25]{1,2,0:T(8,128)(2,1)} %copy-done.3) | copy-start | bytes 720004
  38.3 2.7 %copy-start.5 = (f32[1,2,25,2,32,2,12]{4,5,6,3,2,1,0:T(2,128)S(1)}, f32[1,2,25,2,32,2,12]{4,5,6,3,2,1,0:T(2,128)}, u32[]{:S(2)}) copy-start(f32[1,2,25,2,32,2,12]{4,5,6,3,2,1,0:T(2,128)} %param.28) | copy-start | bytes 921604
  39.1 3.9 %collective-permute-start = (f32[12,25,16]{1,2,0:T(8,128)S(1)}, f32[12,25,16]{1,2,0:T(8,128)S(1)}, u32[]{:S(2)}, u32[]{:S(2)}) collective-permute-start(f32[12,25,16]{1,2,0:T(8,128)S(1)} %reduce_sum.49), channel_id=1, source_target_pairs={{0,1},{1,0},{2,3},{3,2},{4,5},{5,4},{6,7},{7,6},{8,9},{9,8},{10,11... | collective-permute-start | bytes 57608 | tf_op jit(solution)/shard_map/ppermute | solution.py:172
  41.0 0.7 copy-start.14
  43.0 6.0 %collective-permute-start.1 = (f32[12,25,16]{1,2,0:T(8,128)S(1)}, f32[12,25,16]{1,2,0:T(8,128)S(1)}, u32[]{:S(2)}, u32[]{:S(2)}) collective-permute-start(f32[12,25,16]{1,2,0:T(8,128)S(1)} %add.191), channel_id=1, source_target_pairs={{0,2},{2,0},{1,3},{3,1},{4,6},{6,4},{5,7},{7,5},{8,10},{10,8},{9,1... | collective-permute-start | bytes 57608 | tf_op jit(solution)/shard_map/ppermute | solution.py:172
  49.3 1.4 %copy-start.6 = (bf16[1,32,25,256]{3,1,2,0:T(8,128)(2,1)S(1)}, bf16[1,32,25,256]{3,1,2,0:T(8,128)(2,1)}, u32[]{:S(2)}) copy-start(bf16[1,32,25,256]{3,1,2,0:T(8,128)(2,1)} %param.30) | copy-start | bytes 1228804
  52.0 7.4 %copy-start.9 = (bf16[64,32,32]{0,2,1:T(8,128)(2,1)S(1)}, bf16[64,32,32]{0,2,1:T(8,128)(2,1)}, u32[]{:S(2)}) copy-start(bf16[64,32,32]{0,2,1:T(8,128)(2,1)} %param.31) | copy-start | bytes 393220
  53.0 8.3 %collective-permute-start.2 = (bf16[64,512]{0,1:T(8,128)(2,1)S(1)}, bf16[64,512]{0,1:T(8,128)(2,1)S(1)}, u32[]{:S(2)}, u32[]{:S(2)}) collective-permute-start(bf16[64,512]{0,1:T(8,128)(2,1)S(1)} %bitcast_convert_fusion.1), channel_id=1, source_target_pairs={{0,4},{4,8},{8,12},{12,0},{1,5},{5,9},{9,13},{13,1},{2,6},{6,10},{... | collective-permute-start | bytes 196616 | tf_op jit(solution)/shard_map/ppermute | solution.py:204
  54.9 11.1 %collective-permute-start.3 = (bf16[64,512]{0,1:T(8,128)(2,1)S(1)}, bf16[64,512]{0,1:T(8,128)(2,1)S(1)}, u32[]{:S(2)}, u32[]{:S(2)}) collective-permute-start(bf16[64,512]{0,1:T(8,128)(2,1)S(1)} %bitcast_convert_fusion), channel_id=1, source_target_pairs={{0,8},{4,12},{8,0},{12,4},{1,9},{5,13},{9,1},{13,5},{2,10},{6,14},... | collective-permute-start | bytes 196616 | tf_op jit(solution)/shard_map/ppermute | solution.py:204
  57.6 8.4 %collective-permute-start.4 = (bf16[64,512]{0,1:T(8,128)(2,1)S(1)}, bf16[64,512]{0,1:T(8,128)(2,1)S(1)}, u32[]{:S(2)}, u32[]{:S(2)}) collective-permute-start(bf16[64,512]{0,1:T(8,128)(2,1)S(1)} %convert_element_type.165), channel_id=1, source_target_pairs={{0,12},{4,0},{8,4},{12,8},{1,13},{5,1},{9,5},{13,9},{2,14},{6,2},{... | collective-permute-start | bytes 196616 | tf_op jit(solution)/shard_map/ppermute | solution.py:204
  67.5 1.2 %collective-permute-start.5 = (bf16[2,4,1024]{2,1,0:T(4,128)(2,1)S(1)}, bf16[2,4,1024]{2,1,0:T(4,128)(2,1)S(1)}, u32[]{:S(2)}, u32[]{:S(2)}) collective-permute-start(bf16[2,4,1024]{2,1,0:T(4,128)(2,1)S(1)} %fusion.31), channel_id=1, source_target_pairs={{0,1},{1,0},{2,3},{3,2},{4,5},{5,4},{6,7},{7,6},{8,9},{9,8},{10,11... | collective-permute-start | bytes 49160 | tf_op jit(solution)/shard_map/ppermute | solution.py:179
  67.6 16.6 %copy-start.1 = (bf16[12,25,2,2,4,64]{5,4,3,2,1,0:T(4,128)(2,1)S(1)}, bf16[12,25,2,2,4,64]{5,4,3,2,1,0:T(4,128)(2,1)}, u32[]{:S(2)}) copy-start(bf16[12,25,2,2,4,64]{5,4,3,2,1,0:T(4,128)(2,1)} %param.18) | copy-start | bytes 1843204
  68.8 3.7 %collective-permute-start.6 = (bf16[4,1024]{1,0:T(4,128)(2,1)S(1)}, bf16[4,1024]{1,0:T(4,128)(2,1)S(1)}, u32[]{:S(2)}, u32[]{:S(2)}) collective-permute-start(bf16[4,1024]{1,0:T(4,128)(2,1)S(1)} %fusion.35), channel_id=1, source_target_pairs={{0,2},{2,0},{1,3},{3,1},{4,6},{6,4},{5,7},{7,5},{8,10},{10,8},{9,1... | collective-permute-start | bytes 24584 | tf_op jit(solution)/shard_map/ppermute | solution.py:179
  72.6 5.7 %collective-permute-start.7 = (bf16[1024]{0:T(1024)(128)(2,1)S(1)}, bf16[1024]{0:T(1024)(128)(2,1)S(1)}, u32[]{:S(2)}, u32[]{:S(2)}) collective-permute-start(bf16[1024]{0:T(1024)(128)(2,1)S(1)} %get-tuple-element.29), channel_id=1, source_target_pairs={{0,12},{4,0},{8,4},{12,8},{1,13},{5,1},{9,5},{13,9},{2,14},{6,2},{... | collective-permute-start | bytes 6152 | tf_op jit(solution)/shard_map/ppermute | solution.py:192
  77.0 4.5 %collective-permute-start.8 = (bf16[1024]{0:T(1024)(128)(2,1)S(1)}, bf16[1024]{0:T(1024)(128)(2,1)S(1)}, u32[]{:S(2)}, u32[]{:S(2)}) collective-permute-start(bf16[1024]{0:T(1024)(128)(2,1)S(1)} %get-tuple-element.32), channel_id=1, source_target_pairs={{0,8},{4,12},{8,0},{12,4},{1,9},{5,13},{9,1},{13,5},{2,10},{6,14},... | collective-permute-start | bytes 6152 | tf_op jit(solution)/shard_map/ppermute | solution.py:192
  77.4 5.4 %collective-permute-start.9 = (bf16[1024]{0:T(1024)(128)(2,1)S(1)}, bf16[1024]{0:T(1024)(128)(2,1)S(1)}, u32[]{:S(2)}, u32[]{:S(2)}) collective-permute-start(bf16[1024]{0:T(1024)(128)(2,1)S(1)} %get-tuple-element.31), channel_id=1, source_target_pairs={{0,4},{4,8},{8,12},{12,0},{1,5},{5,9},{9,13},{13,1},{2,6},{6,10},{... | collective-permute-start | bytes 6152 | tf_op jit(solution)/shard_map/ppermute | solution.py:192

commit v6 on v5

--- a/solution.py
+++ b/solution.py
@@ -97,15 +97,19 @@
 def owner_frame(owner_sum, owner_turn, owner_shift):
     degrees, orders, width = owner_sum.shape
     states = width // 4
-    first = jnp.einsum("lqp,lpC->lqC", owner_turn[0], owner_sum, precision=HI)
-    second = jnp.einsum("lqp,lpC->lqC", owner_turn[1], owner_sum, precision=HI)
+    turns = jnp.swapaxes(owner_turn, 0, 1).reshape(degrees, 2 * orders, orders)
+    both = jnp.einsum("lqp,lpC->lqC", turns, owner_sum, precision=HI)
+    first = both[:, :orders]
+    second = both[:, orders:]
     turned = complex_join(first, second, width // 2)
     moved = turned.reshape(degrees, orders, 2, 2, states)
     moved = jnp.transpose(moved, (1, 3, 0, 2, 4)).reshape(orders, 2 * degrees, 2 * states)
     root_degrees = owner_shift.shape[3]
     mats = owner_shift.reshape(2, orders, 2 * root_degrees, 2 * degrees)
-    first = jnp.einsum("qab,qbC->qaC", mats[0], moved, precision=HI)
-    second = jnp.einsum("qab,qbC->qaC", mats[1], moved, precision=HI)
+    mats = jnp.swapaxes(mats, 0, 1).reshape(orders, 4 * root_degrees, 2 * degrees)
+    both = jnp.einsum("qab,qbC->qaC", mats, moved, precision=HI)
+    first = both[:, : 2 * root_degrees]
+    second = both[:, 2 * root_degrees :]
     joined = complex_join(first, second, states).reshape(orders, 2, root_degrees, 2, states)
     framed = jnp.transpose(joined, (2, 1, 3, 4, 0)).reshape(root_degrees, 4 * states, orders)
     return framed.astype(jnp.bfloat16)

time: 84.7 us -> 83.9 us (level)
  waiting for transfers between devices: 16 us -> 14.3 us
    slice x4 -> x0, local copies, waits for them, and re-layouts: 2.09 us -> none  [the longest x1 1.37 us: owner_frame(): first = jnp.einsum('lqp,lpC->lqC', owner_turn[0], owner_sum, precision=HI)]
    ppermute x2, waiting for transfers between devices: 2.08 us -> 0.08 us  [pair_sum(): return x + lax.ppermute(x, axis, [(0, 1), (1, 0)])]
    transpose x0 -> x2, local copies, waits for them, and re-layouts: none -> 1.54 us  [the longest x1 1.22 us: owner_frame(): turns = jnp.swapaxes(owner_turn, 0, 1).reshape(degrees, 2 * orders, orders)]
    unnamed x33 -> x34, local copies, waits for them, and re-layouts: 2.43 us -> 3.06 us
  transfers between devices with their start and end apart: 10 -> 10, of which waited for: 8 -> 8; matrix products, arithmetic and copies ran while one was open for 7% -> 8% of each run, Pallas kernels for 0% -> 0%
where the time goes in v6:
time: 83.9 us; the launch traced here: 83.4 us
  local copies, waits for them, and re-layouts  32.6 us (39%)
  starting transfers between devices  15.8 us (19%)
  waiting for transfers between devices  14.3 us (17%)
  other arithmetic  12.2 us (15%)
  matrix products  7.02 us (8%)
  between operations  1.55 us (2%)
    reshape x4, local copies, waits for them, and re-layouts, turn_select(): complex_join(first, second, width // 2).reshape(degrees, 8, orders, width)  6.17 us
    ppermute x3, starting transfers between devices, shift_reduce_scatter(): piece = lax.ppermute(piece, axis, [(i, (i + step) % n) for i in range(n)])  6.16 us
    ppermute x3, waiting for transfers between devices, shift_reduce_scatter(): piece = lax.ppermute(piece, axis, [(i, (i + step) % n) for i in range(n)])  6.02 us
    ppermute x3, starting transfers between devices, shift_all_to_all(): piece = lax.ppermute(piece, axis, [(i, (i + step) % n) for i in range(n)])  5.03 us
    ppermute x3, waiting for transfers between devices, shift_all_to_all(): piece = lax.ppermute(piece, axis, [(i, (i + step) % n) for i in range(n)])  4.9 us
    reshape x2, local copies, waits for them, and re-layouts, turn_select(): mats = mats.reshape(degrees, 2 * 8 * orders, orders)  3.95 us
    transpose x1, local copies, waits for them, and re-layouts, turn_select(): mats = jnp.transpose(rotation, (2, 1, 0, 3, 4))  3.63 us
    concatenate x8, other arithmetic, complex_join(): return jnp.concatenate([real, imag], axis=-1)  3.49 us
  transfers between devices with their start and end apart: 10, of which 8 were waited for; matrix products, arithmetic and copies ran while one was open for 8% of the time, Pallas kernels for 0%

profile of v6, /device:TPU:0, one launch (start us, length us, event | category | flops | bytes accessed | tf_op | source)
XLA Modules:
  0.0 83.4 jit_solution(12235847941923141602)
XLA Ops:
  0.0 3.6 %copy.133 = bf16[12,2,8,25,25]{3,2,1,4,0:T(8,128)(2,1)S(1)} copy(f32[12,2,8,25,25]{4,1,3,0,2:T(2,128)} %bitcast.202) | data formatting | bytes 720000 | tf_op jit(solution)/shard_map/transpose | solution.py:27
  3.7 1.4 %reshape.558 = bf16[12,400,25]{1,2,0:T(8,128)(2,1)S(1)} reshape(bf16[12,2,8,25,25]{3,2,1,4,0:T(8,128)(2,1)S(1)} %copy.133) | data formatting | bytes 480000 | tf_op jit(solution)/shard_map/reshape | solution.py:29
  5.8 0.5 convolution_bitcast_fusion
  6.3 0.6 copy.132
  6.9 1.2 %reshape.557 = bf16[12,25,256]{2,1,0:T(8,128)(2,1)S(1)} reshape(bf16[4800,16]{1,0:T(8,128)(2,1)S(1)} %copy.132) | data formatting | bytes 307200 | tf_op jit(solution)/shard_map/reshape | solution.py:82
  8.1 0.8 %convolution_bitcast_fusion.2 = f32[12,400,256]{2,1,0:T(8,128)S(1)} fusion(bf16[12,25,256]{2,1,0:T(8,128)(2,1)S(1)} %reshape.557, bf16[12,400,25]{1,2,0:T(8,128)(2,1)S(1)} %reshape.558), kind=kOutput, calls=%fused_computation.7 | convolution fusion | flops 61440000 | bytes 5308800 | tf_op jit(solution)/shard_map/lQp,lpC->lQC/dot_general | solution.py:30
  9.2 1.6 %pad_maximum_fusion = f32[12,200,256]{2,1,0:T(8,128)} fusion(f32[12,200,128]{2,1,0:T(8,128)S(1)} %get-tuple-element.36, f32[12,200,128]{2,1,0:T(8,128)S(1)} %get-tuple-element.35), kind=kLoop, calls=%fused_computation.4 | loop fusion | flops 614400 | bytes 4915200 | tf_op jit(solution)/shard_map/concatenate | solution.py:18
  10.8 2.5 %reshape.559 = f32[12,8,25,256]{3,2,1,0:T(8,128)S(1)} reshape(f32[12,200,256]{2,1,0:T(8,128)} %pad_maximum_fusion) | data formatting | bytes 4915200 | tf_op jit(solution)/shard_map/reshape | solution.py:33
  13.3 0.6 tile.8
  14.0 0.9 %tile.9 = f32[8,256]{1,0:T(8,128)S(1)} reshape(f32[8,16,16]{2,1,0:T(8,128)} %tile.8) | data formatting | bytes 16384 | tf_op jit(solution)/shard_map/tile | solution.py:36
  14.9 1.1 %multiply_reduce_fusion.1 = bf16[12,25,256]{2,1,0:T(8,128)(2,1)} fusion(f32[12,8,25,256]{3,2,1,0:T(8,128)S(1)} %reshape.559, f32[8,256]{1,0:T(8,128)S(1)} %tile.9), kind=kLoop, calls=%fused_computation.2 | loop fusion | flops 1152000 | bytes 2619392 | tf_op jit(solution)/shard_map/reduce_sum | solution.py:37
  16.0 1.2 %reshape.560 = bf16[12,25,2,2,64]{4,3,2,1,0:T(2,128)(2,1)S(1)} reshape(bf16[12,25,256]{2,1,0:T(8,128)(2,1)} %multiply_reduce_fusion.1) | data formatting | bytes 307200 | tf_op jit(solution)/shard_map/reshape | solution.py:43
  18.0 0.6 copy.136
  20.2 0.6 copy-done.2
  20.8 1.5 %copy.138 = bf16[12,2,8,25,25]{3,2,1,4,0:T(8,128)(2,1)} copy(f32[12,2,8,25,25]{3,1,4,0,2:T(2,128)S(1)} %bitcast.203) | data formatting | bytes 720000 | tf_op jit(solution)/shard_map/transpose | solution.py:24
  22.3 2.5 %reshape.566 = bf16[12,400,25]{1,2,0:T(8,128)(2,1)S(1)} reshape(bf16[12,2,8,25,25]{3,2,1,4,0:T(8,128)(2,1)} %copy.138) | data formatting | bytes 480000 | tf_op jit(solution)/shard_map/reshape | solution.py:29
  24.8 0.8 %convolution_bitcast_fusion.1 = f32[12,400,256]{2,1,0:T(8,128)S(1)} fusion(bf16[12,25,256]{2,1,0:T(8,128)(2,1)S(1)} %reshape.565, bf16[12,400,25]{1,2,0:T(8,128)(2,1)S(1)} %reshape.566), kind=kOutput, calls=%fused_computation.6 | convolution fusion | flops 61440000 | bytes 5308800 | tf_op jit(solution)/shard_map/lQp,lpC->lQC/dot_general | solution.py:30
  26.2 1.6 %pad_maximum_fusion.1 = f32[12,200,256]{2,1,0:T(8,128)} fusion(f32[12,200,128]{2,1,0:T(8,128)S(1)} %get-tuple-element.34, f32[12,200,128]{2,1,0:T(8,128)S(1)} %get-tuple-element.33), kind=kLoop, calls=%fused_computation.5 | loop fusion | flops 614400 | bytes 4915200 | tf_op jit(solution)/shard_map/concatenate | solution.py:18
  27.8 2.7 %reshape.567 = f32[12,8,25,256]{3,2,1,0:T(8,128)S(1)} reshape(f32[12,200,256]{2,1,0:T(8,128)} %pad_maximum_fusion.1) | data formatting | bytes 4915200 | tf_op jit(solution)/shard_map/reshape | solution.py:33
  30.4 1.1 %multiply_reduce_fusion = f32[12,25,256]{2,1,0:T(8,128)} fusion(f32[12,8,25,256]{3,2,1,0:T(8,128)S(1)} %reshape.567, f32[8,256]{1,0:T(8,128)S(1)} %tile.9), kind=kLoop, calls=%fused_computation.1 | loop fusion | flops 1152000 | bytes 2772992 | tf_op jit(solution)/shard_map/reduce_sum | solution.py:37
  31.8 1.6 %fusion.47 = bf16[12,25,32]{1,2,0:T(8,128)(2,1)S(1)} fusion(f32[12,25,256]{2,1,0:T(8,128)} %multiply_reduce_fusion, f32[256,32,1]{0,1,2:T(8,128)S(1)} %reshape.734), kind=kOutput, calls=%fused_computation.145 | convolution fusion | flops 14745600 | bytes 359168 | tf_op jit(solution)/shard_map/lpC,CD->lpD/dot_general | solution.py:92
  33.9 0.5 reshape.568
  34.6 0.5 multiply_reduce_fusion.3
  35.8 0.6 copy.142
  38.3 0.5 multiply_reduce_fusion.2
  39.6 0.6 fusion.18
  40.2 0.6 dynamic_slice.3
  40.8 0.7 fusion.43
  41.5 2.6 %collective-permute-start.1 = (f32[12,25,16]{1,2,0:T(8,128)S(1)}, f32[12,25,16]{1,2,0:T(8,128)}, u32[]{:S(2)}, u32[]{:S(2)}) collective-permute-start(f32[12,25,16]{1,2,0:T(8,128)S(1)} %add.191), channel_id=1, source_target_pairs={{0,2},{2,0},{1,3},{3,1},{4,6},{6,4},{5,7},{7,5},{8,10},{10,8},{9,1... | collective-permute-start | bytes 57608 | tf_op jit(solution)/shard_map/ppermute | solution.py:176
  44.1 1.2 %copy.146 = f32[12,2,25,25]{2,1,3,0:T(2,128)S(1)} copy(f32[12,2,25,25]{3,1,2,0:T(2,128)} %bitcast.226) | data formatting | bytes 120000 | tf_op jit(solution)/shard_map/transpose | solution.py:100
  45.5 0.6 copy.148
  46.2 0.7 reshape_squeeze.3
  47.6 1.1 %convolution_bitcast_fusion.9 = f32[12,50,16]{1,2,0:T(8,128)S(1)} fusion(f32[12,50,25]{1,2,0:T(8,128)S(1)} %reshape.577, f32[12,25,16]{1,2,0:T(8,128)S(1)} %add.191, f32[12,25,16]{1,2,0:T(8,128)} %collective-permute-done.1), kind=kOutput, calls=%fused_computation.22 | convolution fusion | flops 1444800 | bytes 136800 | tf_op jit(solution)/shard_map/lqp,lpC->lqC/dot_general | solution.py:101
  51.0 1.0 %constant_dynamic-slice_fusion.1 = (f32[1,64,512]{1,0,2:T(1,128)S(1)}, f32[1,64,512]{1,0,2:T(1,128)S(1)}, f32[1,64,512]{1,0,2:T(1,128)S(1)}, f32[1,64,512]{1,0,2:T(1,128)S(1)}) fusion(f32[4,64,512]{1,0,2:T(4,128)S(1)} %reshape_reshape.6, s32[]{:T(128)S(6)} %select_n.229, s32[]{:T(128)S(6)} %select_n.227, s32[]{:T(128)S(6)} %select_n.235, pred[]{:T(512)S(6)} %and.156, ...), kind=kLoop, calls=%fused_computation.126 | loop fusion | flops 32768 | bytes 1048593 | tf_op jit(solution)/shard_map/jit(_take) | solution.py:207
  52.1 1.9 %collective-permute-start.2 = (bf16[64,512]{0,1:T(8,128)(2,1)S(1)}, bf16[64,512]{0,1:T(8,128)(2,1)S(1)}, u32[]{:S(2)}, u32[]{:S(2)}) collective-permute-start(bf16[64,512]{0,1:T(8,128)(2,1)S(1)} %bitcast_convert_fusion.1), channel_id=1, source_target_pairs={{0,4},{4,8},{8,12},{12,0},{1,5},{5,9},{9,13},{13,1},{2,6},{6,10},{... | collective-permute-start | bytes 196616 | tf_op jit(solution)/shard_map/ppermute | solution.py:208
  54.0 2.6 %collective-permute-start.3 = (bf16[64,512]{0,1:T(8,128)(2,1)S(1)}, bf16[64,512]{0,1:T(8,128)(2,1)S(1)}, u32[]{:S(2)}, u32[]{:S(2)}) collective-permute-start(bf16[64,512]{0,1:T(8,128)(2,1)S(1)} %bitcast_convert_fusion), channel_id=1, source_target_pairs={{0,8},{4,12},{8,0},{12,4},{1,9},{5,13},{9,1},{13,5},{2,10},{6,14},... | collective-permute-start | bytes 196616 | tf_op jit(solution)/shard_map/ppermute | solution.py:208
  56.7 1.6 %collective-permute-start.4 = (bf16[64,512]{0,1:T(8,128)(2,1)S(1)}, bf16[64,512]{0,1:T(8,128)(2,1)S(1)}, u32[]{:S(2)}, u32[]{:S(2)}) collective-permute-start(bf16[64,512]{0,1:T(8,128)(2,1)S(1)} %convert_element_type.165), channel_id=1, source_target_pairs={{0,12},{4,0},{8,4},{12,8},{1,13},{5,1},{9,5},{13,9},{2,14},{6,2},{... | collective-permute-start | bytes 196616 | tf_op jit(solution)/shard_map/ppermute | solution.py:208
  58.4 0.8 copy.159
  59.2 1.2 %collective-permute-done.2 = bf16[64,512]{0,1:T(8,128)(2,1)S(1)} collective-permute-done((bf16[64,512]{0,1:T(8,128)(2,1)S(1)}, bf16[64,512]{0,1:T(8,128)(2,1)S(1)}, u32[]{:S(2)}, u32[]{:S(2)}) %collective-permute-start.2) | collective-permute-done | bytes 65568 | tf_op jit(solution)/shard_map/ppermute | solution.py:208
  60.4 4.8 %collective-permute-done.3 = bf16[64,512]{0,1:T(8,128)(2,1)S(1)} collective-permute-done((bf16[64,512]{0,1:T(8,128)(2,1)S(1)}, bf16[64,512]{0,1:T(8,128)(2,1)S(1)}, u32[]{:S(2)}, u32[]{:S(2)}) %collective-permute-start.3) | collective-permute-done | bytes 65568 | tf_op jit(solution)/shard_map/ppermute | solution.py:208
  66.9 1.1 %collective-permute-done.5 = bf16[2,4,1024]{2,1,0:T(4,128)(2,1)S(1)} collective-permute-done((bf16[2,4,1024]{2,1,0:T(4,128)(2,1)S(1)}, bf16[2,4,1024]{2,1,0:T(4,128)(2,1)S(1)}, u32[]{:S(2)}, u32[]{:S(2)}) %collective-permute-start.5) | collective-permute-done | bytes 16416 | tf_op jit(solution)/shard_map/ppermute | solution.py:183
  68.0 1.5 %collective-permute-start.6 = (bf16[4,1024]{1,0:T(4,128)(2,1)S(1)}, bf16[4,1024]{1,0:T(4,128)(2,1)S(1)}, u32[]{:S(2)}, u32[]{:S(2)}) collective-permute-start(bf16[4,1024]{1,0:T(4,128)(2,1)S(1)} %fusion.34), channel_id=1, source_target_pairs={{0,2},{2,0},{1,3},{3,1},{4,6},{6,4},{5,7},{7,5},{8,10},{10,8},{9,1... | collective-permute-start | bytes 24584 | tf_op jit(solution)/shard_map/ppermute | solution.py:183
  69.5 2.2 %collective-permute-done.6 = bf16[4,1024]{1,0:T(4,128)(2,1)S(1)} collective-permute-done((bf16[4,1024]{1,0:T(4,128)(2,1)S(1)}, bf16[4,1024]{1,0:T(4,128)(2,1)S(1)}, u32[]{:S(2)}, u32[]{:S(2)}) %collective-permute-start.6) | collective-permute-done | bytes 8224 | tf_op jit(solution)/shard_map/ppermute | solution.py:183
  71.8 4.4 %collective-permute-start.7 = (bf16[1024]{0:T(1024)(128)(2,1)S(1)}, bf16[1024]{0:T(1024)(128)(2,1)S(1)}, u32[]{:S(2)}, u32[]{:S(2)}) collective-permute-start(bf16[1024]{0:T(1024)(128)(2,1)S(1)} %get-tuple-element.29), channel_id=1, source_target_pairs={{0,12},{4,0},{8,4},{12,8},{1,13},{5,1},{9,5},{13,9},{2,14},{6,2},{... | collective-permute-start | bytes 6152 | tf_op jit(solution)/shard_map/ppermute | solution.py:196
  77.0 0.6 collective-permute-done.7
  77.6 3.1 %collective-permute-done.8 = bf16[1024]{0:T(1024)(128)(2,1)S(1)} collective-permute-done((bf16[1024]{0:T(1024)(128)(2,1)S(1)}, bf16[1024]{0:T(1024)(128)(2,1)S(1)}, u32[]{:S(2)}, u32[]{:S(2)}) %collective-permute-start.8) | collective-permute-done | bytes 2080 | tf_op jit(solution)/shard_map/ppermute | solution.py:196
  80.8 1.2 %collective-permute-done.9 = bf16[1024]{0:T(1024)(128)(2,1)S(1)} collective-permute-done((bf16[1024]{0:T(1024)(128)(2,1)S(1)}, bf16[1024]{0:T(1024)(128)(2,1)S(1)}, u32[]{:S(2)}, u32[]{:S(2)}) %collective-permute-start.9) | collective-permute-done | bytes 2080 | tf_op jit(solution)/shard_map/ppermute | solution.py:196
  82.7 0.8 copy.166
  (127 shorter events, 13.7 us)
Async XLA Ops:
  0.0 5.8 %copy-start = (bf16[12,25,2,2,4,64]{5,4,3,2,1,0:T(4,128)(2,1)S(1)}, bf16[12,25,2,2,4,64]{5,4,3,2,1,0:T(4,128)(2,1)}, u32[]{:S(2)}) copy-start(bf16[12,25,2,2,4,64]{5,4,3,2,1,0:T(4,128)(2,1)} %param.18) | copy-start | bytes 1843204
  3.7 2.1 %copy-start.10 = (s32[64]{0:T(128)S(1)}, s32[64]{0:T(128)}, u32[]{:S(2)}) copy-start(s32[64]{0:T(128)} %param.20) | copy-start | bytes 772
  10.8 2.5 %copy-start.11 = (s32[16]{0:T(128)S(1)}, s32[16]{0:T(128)}, u32[]{:S(2)}) copy-start(s32[16]{0:T(128)} %param.22) | copy-start | bytes 196
  16.0 1.6 %copy-start.7 = (f32[2,25,2,12,2,12]{1,4,5,3,2,0:T(2,128)S(1)}, f32[2,25,2,12,2,12]{1,4,5,3,2,0:T(2,128)}, u32[]{:S(2)}) copy-start(f32[2,25,2,12,2,12]{1,4,5,3,2,0:T(2,128)} %param.25) | copy-start | bytes 345604
  19.1 1.7 %copy-start.2 = (f32[8,2,12,25,25]{4,1,3,2,0:T(2,128)S(1)}, f32[8,2,12,25,25]{4,1,3,2,0:T(2,128)}, u32[]{:S(2)}) copy-start(f32[8,2,12,25,25]{4,1,3,2,0:T(2,128)} %param.24) | copy-start | bytes 1440004
  24.8 0.9 %copy-start.3 = (bf16[12,400,25]{1,2,0:T(8,128)(2,1)}, bf16[12,400,25]{1,2,0:T(8,128)(2,1)S(1)}, u32[]{:S(2)}) copy-start(bf16[12,400,25]{1,2,0:T(8,128)(2,1)S(1)} %reshape.566) | copy-start | bytes 720004
  30.4 1.1 %copy-start.12 = (s32[16]{0:T(128)S(1)}, s32[16]{0:T(128)}, u32[]{:S(2)}) copy-start(s32[16]{0:T(128)} %param.21) | copy-start | bytes 196
  33.8 0.7 copy-start.13
  33.9 1.5 %copy-start.8 = (f32[2,25,2,12,2,12]{1,4,5,3,2,0:T(2,128)S(1)}, f32[2,25,2,12,2,12]{1,4,5,3,2,0:T(2,128)}, u32[]{:S(2)}) copy-start(f32[2,25,2,12,2,12]{1,4,5,3,2,0:T(2,128)} %param.26) | copy-start | bytes 345604
  35.3 1.8 %copy-start.4 = (bf16[12,400,25]{1,2,0:T(8,128)(2,1)S(1)}, bf16[12,400,25]{1,2,0:T(8,128)(2,1)}, u32[]{:S(2)}) copy-start(bf16[12,400,25]{1,2,0:T(8,128)(2,1)} %copy-done.3) | copy-start | bytes 720004
  38.3 1.9 %copy-start.14 = (f32[4]{0:T(128)S(1)}, f32[4]{0:T(128)}, u32[]{:S(2)}) copy-start(f32[4]{0:T(128)} %param.29) | copy-start | bytes 52
  38.3 7.2 %copy-start.5 = (f32[1,2,25,2,32,2,12]{4,5,6,3,2,1,0:T(2,128)S(1)}, f32[1,2,25,2,32,2,12]{4,5,6,3,2,1,0:T(2,128)}, u32[]{:S(2)}) copy-start(f32[1,2,25,2,32,2,12]{4,5,6,3,2,1,0:T(2,128)} %param.28) | copy-start | bytes 921604
  39.1 2.4 %collective-permute-start = (f32[12,25,16]{1,2,0:T(8,128)S(1)}, f32[12,25,16]{1,2,0:T(8,128)S(1)}, u32[]{:S(2)}, u32[]{:S(2)}) collective-permute-start(f32[12,25,16]{1,2,0:T(8,128)S(1)} %reduce_sum.49), channel_id=1, source_target_pairs={{0,1},{1,0},{2,3},{3,2},{4,5},{5,4},{6,7},{7,6},{8,9},{9,8},{10,11... | collective-permute-start | bytes 57608 | tf_op jit(solution)/shard_map/ppermute | solution.py:176
  41.5 6.1 %collective-permute-start.1 = (f32[12,25,16]{1,2,0:T(8,128)S(1)}, f32[12,25,16]{1,2,0:T(8,128)}, u32[]{:S(2)}, u32[]{:S(2)}) collective-permute-start(f32[12,25,16]{1,2,0:T(8,128)S(1)} %add.191), channel_id=1, source_target_pairs={{0,2},{2,0},{1,3},{3,1},{4,6},{6,4},{5,7},{7,5},{8,10},{10,8},{9,1... | collective-permute-start | bytes 57608 | tf_op jit(solution)/shard_map/ppermute | solution.py:176
  47.2 2.6 %copy-start.6 = (bf16[1,32,25,256]{3,1,2,0:T(8,128)(2,1)S(1)}, bf16[1,32,25,256]{3,1,2,0:T(8,128)(2,1)}, u32[]{:S(2)}) copy-start(bf16[1,32,25,256]{3,1,2,0:T(8,128)(2,1)} %param.30) | copy-start | bytes 1228804
  51.0 7.4 %copy-start.9 = (bf16[64,32,32]{0,2,1:T(8,128)(2,1)S(1)}, bf16[64,32,32]{0,2,1:T(8,128)(2,1)}, u32[]{:S(2)}) copy-start(bf16[64,32,32]{0,2,1:T(8,128)(2,1)} %param.31) | copy-start | bytes 393220
  52.1 8.3 %collective-permute-start.2 = (bf16[64,512]{0,1:T(8,128)(2,1)S(1)}, bf16[64,512]{0,1:T(8,128)(2,1)S(1)}, u32[]{:S(2)}, u32[]{:S(2)}) collective-permute-start(bf16[64,512]{0,1:T(8,128)(2,1)S(1)} %bitcast_convert_fusion.1), channel_id=1, source_target_pairs={{0,4},{4,8},{8,12},{12,0},{1,5},{5,9},{9,13},{13,1},{2,6},{6,10},{... | collective-permute-start | bytes 196616 | tf_op jit(solution)/shard_map/ppermute | solution.py:208
  54.0 11.3 %collective-permute-start.3 = (bf16[64,512]{0,1:T(8,128)(2,1)S(1)}, bf16[64,512]{0,1:T(8,128)(2,1)S(1)}, u32[]{:S(2)}, u32[]{:S(2)}) collective-permute-start(bf16[64,512]{0,1:T(8,128)(2,1)S(1)} %bitcast_convert_fusion), channel_id=1, source_target_pairs={{0,8},{4,12},{8,0},{12,4},{1,9},{5,13},{9,1},{13,5},{2,10},{6,14},... | collective-permute-start | bytes 196616 | tf_op jit(solution)/shard_map/ppermute | solution.py:208
  56.7 8.6 %collective-permute-start.4 = (bf16[64,512]{0,1:T(8,128)(2,1)S(1)}, bf16[64,512]{0,1:T(8,128)(2,1)S(1)}, u32[]{:S(2)}, u32[]{:S(2)}) collective-permute-start(bf16[64,512]{0,1:T(8,128)(2,1)S(1)} %convert_element_type.165), channel_id=1, source_target_pairs={{0,12},{4,0},{8,4},{12,8},{1,13},{5,1},{9,5},{13,9},{2,14},{6,2},{... | collective-permute-start | bytes 196616 | tf_op jit(solution)/shard_map/ppermute | solution.py:208
  66.7 1.2 %collective-permute-start.5 = (bf16[2,4,1024]{2,1,0:T(4,128)(2,1)S(1)}, bf16[2,4,1024]{2,1,0:T(4,128)(2,1)S(1)}, u32[]{:S(2)}, u32[]{:S(2)}) collective-permute-start(bf16[2,4,1024]{2,1,0:T(4,128)(2,1)S(1)} %fusion.30), channel_id=1, source_target_pairs={{0,1},{1,0},{2,3},{3,2},{4,5},{5,4},{6,7},{7,6},{8,9},{9,8},{10,11... | collective-permute-start | bytes 49160 | tf_op jit(solution)/shard_map/ppermute | solution.py:183
  66.8 16.6 %copy-start.1 = (bf16[12,25,2,2,4,64]{5,4,3,2,1,0:T(4,128)(2,1)S(1)}, bf16[12,25,2,2,4,64]{5,4,3,2,1,0:T(4,128)(2,1)}, u32[]{:S(2)}) copy-start(bf16[12,25,2,2,4,64]{5,4,3,2,1,0:T(4,128)(2,1)} %param.18) | copy-start | bytes 1843204
  68.0 3.7 %collective-permute-start.6 = (bf16[4,1024]{1,0:T(4,128)(2,1)S(1)}, bf16[4,1024]{1,0:T(4,128)(2,1)S(1)}, u32[]{:S(2)}, u32[]{:S(2)}) collective-permute-start(bf16[4,1024]{1,0:T(4,128)(2,1)S(1)} %fusion.34), channel_id=1, source_target_pairs={{0,2},{2,0},{1,3},{3,1},{4,6},{6,4},{5,7},{7,5},{8,10},{10,8},{9,1... | collective-permute-start | bytes 24584 | tf_op jit(solution)/shard_map/ppermute | solution.py:183
  71.8 5.7 %collective-permute-start.7 = (bf16[1024]{0:T(1024)(128)(2,1)S(1)}, bf16[1024]{0:T(1024)(128)(2,1)S(1)}, u32[]{:S(2)}, u32[]{:S(2)}) collective-permute-start(bf16[1024]{0:T(1024)(128)(2,1)S(1)} %get-tuple-element.29), channel_id=1, source_target_pairs={{0,12},{4,0},{8,4},{12,8},{1,13},{5,1},{9,5},{13,9},{2,14},{6,2},{... | collective-permute-start | bytes 6152 | tf_op jit(solution)/shard_map/ppermute | solution.py:196
  76.2 4.5 %collective-permute-start.8 = (bf16[1024]{0:T(1024)(128)(2,1)S(1)}, bf16[1024]{0:T(1024)(128)(2,1)S(1)}, u32[]{:S(2)}, u32[]{:S(2)}) collective-permute-start(bf16[1024]{0:T(1024)(128)(2,1)S(1)} %get-tuple-element.32), channel_id=1, source_target_pairs={{0,8},{4,12},{8,0},{12,4},{1,9},{5,13},{9,1},{13,5},{2,10},{6,14},... | collective-permute-start | bytes 6152 | tf_op jit(solution)/shard_map/ppermute | solution.py:196
  76.6 5.4 %collective-permute-start.9 = (bf16[1024]{0:T(1024)(128)(2,1)S(1)}, bf16[1024]{0:T(1024)(128)(2,1)S(1)}, u32[]{:S(2)}, u32[]{:S(2)}) collective-permute-start(bf16[1024]{0:T(1024)(128)(2,1)S(1)} %get-tuple-element.31), channel_id=1, source_target_pairs={{0,4},{4,8},{8,12},{12,0},{1,5},{5,9},{9,13},{13,1},{2,6},{6,10},{... | collective-permute-start | bytes 6152 | tf_op jit(solution)/shard_map/ppermute | solution.py:196

commit v7 on v6

--- a/solution.py
+++ b/solution.py
@@ -184,28 +184,29 @@
     return keep + got.astype(keep.dtype)
 
 
+def rolled_blocks(x, start):
+    n = x.shape[0]
+    return lax.dynamic_slice_in_dim(jnp.concatenate([x, x], axis=0), start % n, n, axis=0)
+
+
 def shift_all_to_all(x, axis):
     n = lax.axis_size(axis)
     me = lax.axis_index(axis)
-    rows = jnp.arange(n)
-    result = jnp.zeros_like(x)
-    for step in range(n):
-        target = (me + step) % n
-        piece = jnp.take(x, target, axis=0)
-        if step:
-            piece = lax.ppermute(piece, axis, [(i, (i + step) % n) for i in range(n)])
-        source = (me - step) % n
-        result = jnp.where((rows == source).reshape((n,) + (1,) * (x.ndim - 1)), piece[None], result)
-    return result
+    sends = rolled_blocks(x, me)
+    got = [sends[0]]
+    for step in range(1, n):
+        got.append(lax.ppermute(sends[step], axis, [(i, (i + step) % n) for i in range(n)]))
+    ahead = jnp.stack([got[(n - k) % n] for k in range(n)], axis=0)
+    return rolled_blocks(ahead, n - me)
 
 
 def shift_reduce_scatter(x, axis):
     n = lax.axis_size(axis)
     me = lax.axis_index(axis)
-    total = jnp.take(x, me, axis=0)
+    sends = rolled_blocks(x, me)
+    total = sends[0]
     for step in range(1, n):
-        piece = jnp.take(x, (me + step) % n, axis=0).astype(jnp.bfloat16)
-        piece = lax.ppermute(piece, axis, [(i, (i + step) % n) for i in range(n)])
+        piece = lax.ppermute(sends[step].astype(jnp.bfloat16), axis, [(i, (i + step) % n) for i in range(n)])
         total = total + piece.astype(total.dtype)
     return total
 

time: 83.9 us -> 82.9 us (0.988)
  matrix products: 7.02 us -> 6.13 us
    transpose x1, local copies, waits for them, and re-layouts: 1.22 us -> 0.26 us  [owner_frame(): turns = jnp.swapaxes(owner_turn, 0, 1).reshape(degrees, 2 * orders, orders)]
    slice x0 -> x3, local copies, waits for them, and re-layouts: none -> 0.92 us  [the longest x1 0.69 us: shift_reduce_scatter(): sends[step].astype(jnp.bfloat16)]
    dot_general x1, matrix products: 1.09 us -> 0.2 us  [owner_frame(): both = jnp.einsum('lqp,lpC->lqC', turns, owner_sum, precision=HI)]
    ppermute x2, waiting for transfers between devices: 0.08 us -> 0.93 us  [pair_sum(): return x + lax.ppermute(x, axis, [(0, 1), (1, 0)])]
    unnamed x34 -> x36, local copies, waits for them, and re-layouts: 3.06 us -> 3.07 us
  transfers between devices with their start and end apart: 10 -> 10, of which waited for: 8 -> 8; matrix products, arithmetic and copies ran while one was open for 8% -> 7% of each run, Pallas kernels for 0% -> 0%
where the time goes in v7:
time: 82.9 us; the launch traced here: 82.5 us
  local copies, waits for them, and re-layouts  32.5 us (39%)
  starting transfers between devices  16 us (19%)
  waiting for transfers between devices  14.3 us (17%)
  other arithmetic  12 us (14%)
  matrix products  6.13 us (7%)
  between operations  1.56 us (2%)
    ppermute x3, starting transfers between devices, shift_reduce_scatter(): lax.ppermute(sends[step].astype(jnp.bfloat16), axis, [(i, (i + step) % n)...  6.17 us
    reshape x4, local copies, waits for them, and re-layouts, turn_select(): complex_join(first, second, width // 2).reshape(degrees, 8, orders, width)  6.17 us
    ppermute x3, waiting for transfers between devices, shift_reduce_scatter(): lax.ppermute(sends[step].astype(jnp.bfloat16), axis, [(i, (i + step) % n)...  5.22 us
    ppermute x3, waiting for transfers between devices, shift_all_to_all(): lax.ppermute(sends[step], axis, [(i, (i + step) % n) for i in range(n)])  5.1 us
    ppermute x3, starting transfers between devices, shift_all_to_all(): lax.ppermute(sends[step], axis, [(i, (i + step) % n) for i in range(n)])  5 us
    reshape x2, local copies, waits for them, and re-layouts, turn_select(): mats = mats.reshape(degrees, 2 * 8 * orders, orders)  3.95 us
    transpose x1, local copies, waits for them, and re-layouts, turn_select(): mats = jnp.transpose(rotation, (2, 1, 0, 3, 4))  3.63 us
    concatenate x8, other arithmetic, complex_join(): return jnp.concatenate([real, imag], axis=-1)  3.5 us
  transfers between devices with their start and end apart: 10, of which 8 were waited for; matrix products, arithmetic and copies ran while one was open for 7% of the time, Pallas kernels for 0%

profile of v7, /device:TPU:0, one launch (start us, length us, event | category | flops | bytes accessed | tf_op | source)
XLA Modules:
  0.0 82.5 jit_solution(15976363862607676116)
XLA Ops:
  0.0 3.6 %copy.219 = bf16[12,2,8,25,25]{3,2,1,4,0:T(8,128)(2,1)S(1)} copy(f32[12,2,8,25,25]{4,1,3,0,2:T(2,128)} %bitcast.200) | data formatting | bytes 720000 | tf_op jit(solution)/shard_map/transpose | solution.py:27
  3.7 1.4 %reshape.477 = bf16[12,400,25]{1,2,0:T(8,128)(2,1)S(1)} reshape(bf16[12,2,8,25,25]{3,2,1,4,0:T(8,128)(2,1)S(1)} %copy.219) | data formatting | bytes 480000 | tf_op jit(solution)/shard_map/reshape | solution.py:29
  5.8 0.5 convolution_bitcast_fusion
  6.3 0.6 copy.218
  6.9 1.2 %reshape.476 = bf16[12,25,256]{2,1,0:T(8,128)(2,1)S(1)} reshape(bf16[4800,16]{1,0:T(8,128)(2,1)S(1)} %copy.218) | data formatting | bytes 307200 | tf_op jit(solution)/shard_map/reshape | solution.py:82
  8.1 0.8 %convolution_bitcast_fusion.2 = f32[12,400,256]{2,1,0:T(8,128)S(1)} fusion(bf16[12,25,256]{2,1,0:T(8,128)(2,1)S(1)} %reshape.476, bf16[12,400,25]{1,2,0:T(8,128)(2,1)S(1)} %reshape.477), kind=kOutput, calls=%fused_computation.7 | convolution fusion | flops 61440000 | bytes 5308800 | tf_op jit(solution)/shard_map/lQp,lpC->lQC/dot_general | solution.py:30
  9.2 1.6 %pad_maximum_fusion = f32[12,200,256]{2,1,0:T(8,128)} fusion(f32[12,200,128]{2,1,0:T(8,128)S(1)} %get-tuple-element.13, f32[12,200,128]{2,1,0:T(8,128)S(1)} %get-tuple-element.12), kind=kLoop, calls=%fused_computation.4 | loop fusion | flops 614400 | bytes 4915200 | tf_op jit(solution)/shard_map/concatenate | solution.py:18
  10.8 2.5 %reshape.478 = f32[12,8,25,256]{3,2,1,0:T(8,128)S(1)} reshape(f32[12,200,256]{2,1,0:T(8,128)} %pad_maximum_fusion) | data formatting | bytes 4915200 | tf_op jit(solution)/shard_map/reshape | solution.py:33
  13.3 0.6 tile.8
  14.0 0.9 %tile.9 = f32[8,256]{1,0:T(8,128)S(1)} reshape(f32[8,16,16]{2,1,0:T(8,128)} %tile.8) | data formatting | bytes 16384 | tf_op jit(solution)/shard_map/tile | solution.py:36
  14.9 1.1 %multiply_reduce_fusion.1 = bf16[12,25,256]{2,1,0:T(8,128)(2,1)} fusion(f32[12,8,25,256]{3,2,1,0:T(8,128)S(1)} %reshape.478, f32[8,256]{1,0:T(8,128)S(1)} %tile.9), kind=kLoop, calls=%fused_computation.2 | loop fusion | flops 1152000 | bytes 2619392 | tf_op jit(solution)/shard_map/reduce_sum | solution.py:37
  16.0 1.2 %reshape.479 = bf16[12,25,2,2,64]{4,3,2,1,0:T(2,128)(2,1)S(1)} reshape(bf16[12,25,256]{2,1,0:T(8,128)(2,1)} %multiply_reduce_fusion.1) | data formatting | bytes 307200 | tf_op jit(solution)/shard_map/reshape | solution.py:43
  18.0 0.6 copy.222
  20.2 0.6 copy-done.2
  20.8 1.5 %copy.224 = bf16[12,2,8,25,25]{3,2,1,4,0:T(8,128)(2,1)} copy(f32[12,2,8,25,25]{3,1,4,0,2:T(2,128)S(1)} %bitcast.201) | data formatting | bytes 720000 | tf_op jit(solution)/shard_map/transpose | solution.py:24
  22.3 2.5 %reshape.485 = bf16[12,400,25]{1,2,0:T(8,128)(2,1)S(1)} reshape(bf16[12,2,8,25,25]{3,2,1,4,0:T(8,128)(2,1)} %copy.224) | data formatting | bytes 480000 | tf_op jit(solution)/shard_map/reshape | solution.py:29
  24.8 0.8 %convolution_bitcast_fusion.1 = f32[12,400,256]{2,1,0:T(8,128)S(1)} fusion(bf16[12,25,256]{2,1,0:T(8,128)(2,1)S(1)} %reshape.484, bf16[12,400,25]{1,2,0:T(8,128)(2,1)S(1)} %reshape.485), kind=kOutput, calls=%fused_computation.6 | convolution fusion | flops 61440000 | bytes 5308800 | tf_op jit(solution)/shard_map/lQp,lpC->lQC/dot_general | solution.py:30
  26.2 1.6 %pad_maximum_fusion.1 = f32[12,200,256]{2,1,0:T(8,128)} fusion(f32[12,200,128]{2,1,0:T(8,128)S(1)} %get-tuple-element.11, f32[12,200,128]{2,1,0:T(8,128)S(1)} %get-tuple-element.10), kind=kLoop, calls=%fused_computation.5 | loop fusion | flops 614400 | bytes 4915200 | tf_op jit(solution)/shard_map/concatenate | solution.py:18
  27.8 2.7 %reshape.486 = f32[12,8,25,256]{3,2,1,0:T(8,128)S(1)} reshape(f32[12,200,256]{2,1,0:T(8,128)} %pad_maximum_fusion.1) | data formatting | bytes 4915200 | tf_op jit(solution)/shard_map/reshape | solution.py:33
  30.5 1.1 %multiply_reduce_fusion = f32[12,25,256]{2,1,0:T(8,128)} fusion(f32[12,8,25,256]{3,2,1,0:T(8,128)S(1)} %reshape.486, f32[8,256]{1,0:T(8,128)S(1)} %tile.9), kind=kLoop, calls=%fused_computation.1 | loop fusion | flops 1152000 | bytes 2772992 | tf_op jit(solution)/shard_map/reduce_sum | solution.py:37
  31.9 1.6 %fusion.45 = bf16[12,25,32]{1,2,0:T(8,128)(2,1)S(1)} fusion(f32[12,25,256]{2,1,0:T(8,128)} %multiply_reduce_fusion, f32[256,32,1]{0,1,2:T(8,128)S(1)} %reshape.506), kind=kOutput, calls=%fused_computation.139 | convolution fusion | flops 14745600 | bytes 359168 | tf_op jit(solution)/shard_map/lpC,CD->lpD/dot_general | solution.py:92
  34.6 0.5 multiply_reduce_fusion.3
  35.8 0.6 copy.228
  38.3 0.5 multiply_reduce_fusion.2
  39.1 0.5 collective-permute-start
  39.6 0.6 dynamic_slice.12
  40.2 0.7 fusion.38
  40.9 2.6 %collective-permute-start.1 = (f32[12,25,16]{1,2,0:T(8,128)S(1)}, f32[12,25,16]{1,2,0:T(8,128)S(1)}, u32[]{:S(2)}, u32[]{:S(2)}) collective-permute-start(f32[12,25,16]{1,2,0:T(8,128)S(1)} %add.158), channel_id=1, source_target_pairs={{0,2},{2,0},{1,3},{3,1},{4,6},{6,4},{5,7},{7,5},{8,10},{10,8},{9,1... | collective-permute-start | bytes 57608 | tf_op jit(solution)/shard_map/ppermute | solution.py:176
  44.0 0.6 copy.234
  44.6 0.7 reshape_squeeze.3
  46.0 0.9 %collective-permute-done.1 = f32[12,25,16]{1,2,0:T(8,128)S(1)} collective-permute-done((f32[12,25,16]{1,2,0:T(8,128)S(1)}, f32[12,25,16]{1,2,0:T(8,128)S(1)}, u32[]{:S(2)}, u32[]{:S(2)}) %collective-permute-start.1) | collective-permute-done | bytes 19232 | tf_op jit(solution)/shard_map/ppermute | solution.py:176
  49.4 1.0 %fusion.42 = (bf16[4,64,512]{1,0,2:T(4,128)(2,1)S(1)}, f32[4,64,512]{1,0,2:T(4,128)S(1)}) fusion(s32[]{:T(128)S(6)} %select_n.118, f32[4,64,512]{1,0,2:T(4,128)S(1)} %reshape_reshape.6), kind=kLoop, calls=%fused_computation.137 | loop fusion | flops 262144 | bytes 1310724 | tf_op jit(solution)/shard_map/convert.5
  50.5 0.7 fusion.44
  51.2 1.9 %collective-permute-start.2 = (bf16[64,512]{0,1:T(8,128)(2,1)S(1)}, bf16[64,512]{0,1:T(8,128)(2,1)S(1)}, u32[]{:S(2)}, u32[]{:S(2)}) collective-permute-start(bf16[64,512]{0,1:T(8,128)(2,1)S(1)} %bitcast.228), channel_id=1, source_target_pairs={{0,4},{4,8},{8,12},{12,0},{1,5},{5,9},{9,13},{13,1},{2,6},{6,10},{... | collective-permute-start | bytes 196616 | tf_op jit(solution)/shard_map/ppermute | solution.py:209
  53.1 2.6 %collective-permute-start.3 = (bf16[64,512]{0,1:T(8,128)(2,1)S(1)}, bf16[64,512]{0,1:T(8,128)(2,1)S(1)}, u32[]{:S(2)}, u32[]{:S(2)}) collective-permute-start(bf16[64,512]{0,1:T(8,128)(2,1)S(1)} %bitcast.229), channel_id=1, source_target_pairs={{0,8},{4,12},{8,0},{12,4},{1,9},{5,13},{9,1},{13,5},{2,10},{6,14},... | collective-permute-start | bytes 196616 | tf_op jit(solution)/shard_map/ppermute | solution.py:209
  55.8 1.6 %collective-permute-start.4 = (bf16[64,512]{0,1:T(8,128)(2,1)S(1)}, bf16[64,512]{0,1:T(8,128)(2,1)S(1)}, u32[]{:S(2)}, u32[]{:S(2)}) collective-permute-start(bf16[64,512]{0,1:T(8,128)(2,1)S(1)} %bitcast.230), channel_id=1, source_target_pairs={{0,12},{4,0},{8,4},{12,8},{1,13},{5,1},{9,5},{13,9},{2,14},{6,2},{... | collective-permute-start | bytes 196616 | tf_op jit(solution)/shard_map/ppermute | solution.py:209
  57.4 0.6 fusion.16
  58.0 0.8 copy.248
  59.0 0.6 collective-permute-done.2
  59.6 4.7 %collective-permute-done.3 = bf16[64,512]{0,1:T(8,128)(2,1)S(1)} collective-permute-done((bf16[64,512]{0,1:T(8,128)(2,1)S(1)}, bf16[64,512]{0,1:T(8,128)(2,1)S(1)}, u32[]{:S(2)}, u32[]{:S(2)}) %collective-permute-start.3) | collective-permute-done | bytes 65568 | tf_op jit(solution)/shard_map/ppermute | solution.py:209
  65.8 1.2 %collective-permute-done.5 = bf16[2,4,1024]{2,1,0:T(4,128)(2,1)S(1)} collective-permute-done((bf16[2,4,1024]{2,1,0:T(4,128)(2,1)S(1)}, bf16[2,4,1024]{2,1,0:T(4,128)(2,1)S(1)}, u32[]{:S(2)}, u32[]{:S(2)}) %collective-permute-start.5) | collective-permute-done | bytes 16416 | tf_op jit(solution)/shard_map/ppermute | solution.py:183
  67.0 1.6 %collective-permute-start.6 = (bf16[4,1024]{1,0:T(4,128)(2,1)S(1)}, bf16[4,1024]{1,0:T(4,128)(2,1)S(1)}, u32[]{:S(2)}, u32[]{:S(2)}) collective-permute-start(bf16[4,1024]{1,0:T(4,128)(2,1)S(1)} %fusion.32), channel_id=1, source_target_pairs={{0,2},{2,0},{1,3},{3,1},{4,6},{6,4},{5,7},{7,5},{8,10},{10,8},{9,1... | collective-permute-start | bytes 24584 | tf_op jit(solution)/shard_map/ppermute | solution.py:183
  68.8 1.9 %collective-permute-done.6 = bf16[4,1024]{1,0:T(4,128)(2,1)S(1)} collective-permute-done((bf16[4,1024]{1,0:T(4,128)(2,1)S(1)}, bf16[4,1024]{1,0:T(4,128)(2,1)S(1)}, u32[]{:S(2)}, u32[]{:S(2)}) %collective-permute-start.6) | collective-permute-done | bytes 8224 | tf_op jit(solution)/shard_map/ppermute | solution.py:183
  70.8 4.4 %collective-permute-start.7 = (bf16[1024]{0:T(1024)(128)(2,1)S(1)}, bf16[1024]{0:T(1024)(128)(2,1)S(1)}, u32[]{:S(2)}, u32[]{:S(2)}) collective-permute-start(bf16[1024]{0:T(1024)(128)(2,1)S(1)} %get-tuple-element.7), channel_id=1, source_target_pairs={{0,12},{4,0},{8,4},{12,8},{1,13},{5,1},{9,5},{13,9},{2,14},{6,2},{... | collective-permute-start | bytes 6152 | tf_op jit(solution)/shard_map/ppermute | solution.py:198
  75.9 0.6 collective-permute-done.7
  76.5 3.2 %collective-permute-done.8 = bf16[1024]{0:T(1024)(128)(2,1)S(1)} collective-permute-done((bf16[1024]{0:T(1024)(128)(2,1)S(1)}, bf16[1024]{0:T(1024)(128)(2,1)S(1)}, u32[]{:S(2)}, u32[]{:S(2)}) %collective-permute-start.8) | collective-permute-done | bytes 2080 | tf_op jit(solution)/shard_map/ppermute | solution.py:198
  79.7 1.3 %collective-permute-done.9 = bf16[1024]{0:T(1024)(128)(2,1)S(1)} collective-permute-done((bf16[1024]{0:T(1024)(128)(2,1)S(1)}, bf16[1024]{0:T(1024)(128)(2,1)S(1)}, u32[]{:S(2)}, u32[]{:S(2)}) %collective-permute-start.9) | collective-permute-done | bytes 2080 | tf_op jit(solution)/shard_map/ppermute | solution.py:198
  81.7 0.8 copy.256
  (132 shorter events, 14.0 us)
Async XLA Ops:
  0.0 5.8 %copy-start = (bf16[12,25,2,2,4,64]{5,4,3,2,1,0:T(4,128)(2,1)S(1)}, bf16[12,25,2,2,4,64]{5,4,3,2,1,0:T(4,128)(2,1)}, u32[]{:S(2)}) copy-start(bf16[12,25,2,2,4,64]{5,4,3,2,1,0:T(4,128)(2,1)} %param.14) | copy-start | bytes 1843204
  3.7 2.1 %copy-start.11 = (s32[64]{0:T(128)S(1)}, s32[64]{0:T(128)}, u32[]{:S(2)}) copy-start(s32[64]{0:T(128)} %param.16) | copy-start | bytes 772
  10.8 2.5 %copy-start.12 = (s32[16]{0:T(128)S(1)}, s32[16]{0:T(128)}, u32[]{:S(2)}) copy-start(s32[16]{0:T(128)} %param.18) | copy-start | bytes 196
  16.0 1.6 %copy-start.7 = (f32[2,25,2,12,2,12]{1,4,5,3,2,0:T(2,128)S(1)}, f32[2,25,2,12,2,12]{1,4,5,3,2,0:T(2,128)}, u32[]{:S(2)}) copy-start(f32[2,25,2,12,2,12]{1,4,5,3,2,0:T(2,128)} %param.21) | copy-start | bytes 345604
  19.1 1.7 %copy-start.2 = (f32[8,2,12,25,25]{4,1,3,2,0:T(2,128)S(1)}, f32[8,2,12,25,25]{4,1,3,2,0:T(2,128)}, u32[]{:S(2)}) copy-start(f32[8,2,12,25,25]{4,1,3,2,0:T(2,128)} %param.20) | copy-start | bytes 1440004
  24.8 0.9 %copy-start.3 = (bf16[12,400,25]{1,2,0:T(8,128)(2,1)}, bf16[12,400,25]{1,2,0:T(8,128)(2,1)S(1)}, u32[]{:S(2)}) copy-start(bf16[12,400,25]{1,2,0:T(8,128)(2,1)S(1)} %reshape.485) | copy-start | bytes 720004
  30.4 1.2 %copy-start.13 = (s32[16]{0:T(128)S(1)}, s32[16]{0:T(128)}, u32[]{:S(2)}) copy-start(s32[16]{0:T(128)} %param.17) | copy-start | bytes 196
  33.8 0.7 copy-start.14
  33.9 1.5 %copy-start.8 = (f32[2,25,2,12,2,12]{1,4,5,3,2,0:T(2,128)S(1)}, f32[2,25,2,12,2,12]{1,4,5,3,2,0:T(2,128)}, u32[]{:S(2)}) copy-start(f32[2,25,2,12,2,12]{1,4,5,3,2,0:T(2,128)} %param.22) | copy-start | bytes 345604
  35.4 1.8 %copy-start.4 = (bf16[12,400,25]{1,2,0:T(8,128)(2,1)S(1)}, bf16[12,400,25]{1,2,0:T(8,128)(2,1)}, u32[]{:S(2)}) copy-start(bf16[12,400,25]{1,2,0:T(8,128)(2,1)} %copy-done.3) | copy-start | bytes 720004
  37.8 1.9 %copy-start.15 = (f32[4]{0:T(128)S(1)}, f32[4]{0:T(128)}, u32[]{:S(2)}) copy-start(f32[4]{0:T(128)} %param.25) | copy-start | bytes 52
  38.3 5.2 %copy-start.9 = (f32[1,2,12,25,25]{4,1,3,2,0:T(2,128)S(1)}, f32[1,2,12,25,25]{4,1,3,2,0:T(2,128)}, u32[]{:S(2)}) copy-start(f32[1,2,12,25,25]{4,1,3,2,0:T(2,128)} %param.23) | copy-start | bytes 180004
  38.3 5.7 %copy-start.5 = (f32[1,2,25,2,32,2,12]{4,5,6,3,2,1,0:T(2,128)S(1)}, f32[1,2,25,2,32,2,12]{4,5,6,3,2,1,0:T(2,128)}, u32[]{:S(2)}) copy-start(f32[1,2,25,2,32,2,12]{4,5,6,3,2,1,0:T(2,128)} %param.24) | copy-start | bytes 921604
  39.1 1.8 %collective-permute-start = (f32[12,25,16]{1,2,0:T(8,128)S(1)}, f32[12,25,16]{1,2,0:T(8,128)S(1)}, u32[]{:S(2)}, u32[]{:S(2)}) collective-permute-start(f32[12,25,16]{1,2,0:T(8,128)S(1)} %reduce_sum.49), channel_id=1, source_target_pairs={{0,1},{1,0},{2,3},{3,2},{4,5},{5,4},{6,7},{7,6},{8,9},{9,8},{10,11... | collective-permute-start | bytes 57608 | tf_op jit(solution)/shard_map/ppermute | solution.py:176
  40.9 6.0 %collective-permute-start.1 = (f32[12,25,16]{1,2,0:T(8,128)S(1)}, f32[12,25,16]{1,2,0:T(8,128)S(1)}, u32[]{:S(2)}, u32[]{:S(2)}) collective-permute-start(f32[12,25,16]{1,2,0:T(8,128)S(1)} %add.158), channel_id=1, source_target_pairs={{0,2},{2,0},{1,3},{3,1},{4,6},{6,4},{5,7},{7,5},{8,10},{10,8},{9,1... | collective-permute-start | bytes 57608 | tf_op jit(solution)/shard_map/ppermute | solution.py:176
  45.6 2.6 %copy-start.6 = (bf16[1,32,25,256]{3,1,2,0:T(8,128)(2,1)S(1)}, bf16[1,32,25,256]{3,1,2,0:T(8,128)(2,1)}, u32[]{:S(2)}) copy-start(bf16[1,32,25,256]{3,1,2,0:T(8,128)(2,1)} %param.26) | copy-start | bytes 1228804
  50.5 7.6 %copy-start.10 = (bf16[64,32,32]{0,2,1:T(8,128)(2,1)S(1)}, bf16[64,32,32]{0,2,1:T(8,128)(2,1)}, u32[]{:S(2)}) copy-start(bf16[64,32,32]{0,2,1:T(8,128)(2,1)} %param.27) | copy-start | bytes 393220
  51.2 8.4 %collective-permute-start.2 = (bf16[64,512]{0,1:T(8,128)(2,1)S(1)}, bf16[64,512]{0,1:T(8,128)(2,1)S(1)}, u32[]{:S(2)}, u32[]{:S(2)}) collective-permute-start(bf16[64,512]{0,1:T(8,128)(2,1)S(1)} %bitcast.228), channel_id=1, source_target_pairs={{0,4},{4,8},{8,12},{12,0},{1,5},{5,9},{9,13},{13,1},{2,6},{6,10},{... | collective-permute-start | bytes 196616 | tf_op jit(solution)/shard_map/ppermute | solution.py:209
  53.1 11.1 %collective-permute-start.3 = (bf16[64,512]{0,1:T(8,128)(2,1)S(1)}, bf16[64,512]{0,1:T(8,128)(2,1)S(1)}, u32[]{:S(2)}, u32[]{:S(2)}) collective-permute-start(bf16[64,512]{0,1:T(8,128)(2,1)S(1)} %bitcast.229), channel_id=1, source_target_pairs={{0,8},{4,12},{8,0},{12,4},{1,9},{5,13},{9,1},{13,5},{2,10},{6,14},... | collective-permute-start | bytes 196616 | tf_op jit(solution)/shard_map/ppermute | solution.py:209
  55.8 8.4 %collective-permute-start.4 = (bf16[64,512]{0,1:T(8,128)(2,1)S(1)}, bf16[64,512]{0,1:T(8,128)(2,1)S(1)}, u32[]{:S(2)}, u32[]{:S(2)}) collective-permute-start(bf16[64,512]{0,1:T(8,128)(2,1)S(1)} %bitcast.230), channel_id=1, source_target_pairs={{0,12},{4,0},{8,4},{12,8},{1,13},{5,1},{9,5},{13,9},{2,14},{6,2},{... | collective-permute-start | bytes 196616 | tf_op jit(solution)/shard_map/ppermute | solution.py:209
  65.7 1.2 %collective-permute-start.5 = (bf16[2,4,1024]{2,1,0:T(4,128)(2,1)S(1)}, bf16[2,4,1024]{2,1,0:T(4,128)(2,1)S(1)}, u32[]{:S(2)}, u32[]{:S(2)}) collective-permute-start(bf16[2,4,1024]{2,1,0:T(4,128)(2,1)S(1)} %fusion.28), channel_id=1, source_target_pairs={{0,1},{1,0},{2,3},{3,2},{4,5},{5,4},{6,7},{7,6},{8,9},{9,8},{10,11... | collective-permute-start | bytes 49160 | tf_op jit(solution)/shard_map/ppermute | solution.py:183
  67.0 15.5 %copy-start.1 = (bf16[12,25,2,2,4,64]{5,4,3,2,1,0:T(4,128)(2,1)S(1)}, bf16[12,25,2,2,4,64]{5,4,3,2,1,0:T(4,128)(2,1)}, u32[]{:S(2)}) copy-start(bf16[12,25,2,2,4,64]{5,4,3,2,1,0:T(4,128)(2,1)} %param.14) | copy-start | bytes 1843204
  67.0 3.7 %collective-permute-start.6 = (bf16[4,1024]{1,0:T(4,128)(2,1)S(1)}, bf16[4,1024]{1,0:T(4,128)(2,1)S(1)}, u32[]{:S(2)}, u32[]{:S(2)}) collective-permute-start(bf16[4,1024]{1,0:T(4,128)(2,1)S(1)} %fusion.32), channel_id=1, source_target_pairs={{0,2},{2,0},{1,3},{3,1},{4,6},{6,4},{5,7},{7,5},{8,10},{10,8},{9,1... | collective-permute-start | bytes 24584 | tf_op jit(solution)/shard_map/ppermute | solution.py:183
  70.8 5.7 %collective-permute-start.7 = (bf16[1024]{0:T(1024)(128)(2,1)S(1)}, bf16[1024]{0:T(1024)(128)(2,1)S(1)}, u32[]{:S(2)}, u32[]{:S(2)}) collective-permute-start(bf16[1024]{0:T(1024)(128)(2,1)S(1)} %get-tuple-element.7), channel_id=1, source_target_pairs={{0,12},{4,0},{8,4},{12,8},{1,13},{5,1},{9,5},{13,9},{2,14},{6,2},{... | collective-permute-start | bytes 6152 | tf_op jit(solution)/shard_map/ppermute | solution.py:198
  75.2 4.5 %collective-permute-start.8 = (bf16[1024]{0:T(1024)(128)(2,1)S(1)}, bf16[1024]{0:T(1024)(128)(2,1)S(1)}, u32[]{:S(2)}, u32[]{:S(2)}) collective-permute-start(bf16[1024]{0:T(1024)(128)(2,1)S(1)} %get-tuple-element.6), channel_id=1, source_target_pairs={{0,8},{4,12},{8,0},{12,4},{1,9},{5,13},{9,1},{13,5},{2,10},{6,14},... | collective-permute-start | bytes 6152 | tf_op jit(solution)/shard_map/ppermute | solution.py:198
  75.6 5.4 %collective-permute-start.9 = (bf16[1024]{0:T(1024)(128)(2,1)S(1)}, bf16[1024]{0:T(1024)(128)(2,1)S(1)}, u32[]{:S(2)}, u32[]{:S(2)}) collective-permute-start(bf16[1024]{0:T(1024)(128)(2,1)S(1)} %get-tuple-element.5), channel_id=1, source_target_pairs={{0,4},{4,8},{8,12},{12,0},{1,5},{5,9},{9,13},{13,1},{2,6},{6,10},{... | collective-permute-start | bytes 6152 | tf_op jit(solution)/shard_map/ppermute | solution.py:198
